TPU v7x, 128 devices: a whole 4x4x4 slice. The times are simulated.
128 devices in a mesh: occ: 8 (over z_lo, y), aux: 16 (over z_hi, x, core).
Axes of the slice: x: 4, y: 4, z: 4 (z_hi: 2, z_lo: 2; z = z_hi * 2 + z_lo), core: 2. Of those that a mesh axis runs over, the one named last changes fastest.
Arguments:
- factors: float32 [16384, 8, 768], P('aux', 'occ'), may hold values from -1.25 to 1.25
- eps_occ: float32 [8], replicated, may hold values from -2 to -0.5
- eps_vir: float32 [768], replicated, may hold values from 0.5 to 3
Outputs:
- density: float32 [16384, 8, 768], P('aux', 'occ')
All inputs are finite; a program needn't handle non-finite values.
Results may differ from a plain program's by a relative error of at most 0.0003.
Values sent between devices are 32-bit elements; how exact they have to be, the bound alone decides.
No kernel may reach another device: no remote copies, remote signals or barrier semaphores. Data moves between devices by JAX's collectives and lax.ppermute only.
A program may use at most 128 MiB of HBM per device.

v0:
```python
import jax
import jax.numpy as jnp
import numpy as np
from jax import lax
from jax.sharding import PartitionSpec as P


PREC = lax.Precision.HIGH


def passed_along(value, axis, steps):
    count = lax.axis_size(axis)
    pairs = [(source, (source + steps) % count) for source in range(count)]
    return lax.ppermute(value, axis, pairs)


def pair_values(eps_occ, eps_vir, group, occ_dev):
    occ_part = lax.dynamic_slice_in_dim(eps_occ, group * occ_dev, occ_dev)
    return (occ_part[:, None] - eps_vir[None, :]).reshape(-1)


def aux_stages(count):
    assert count == 16
    stages = []
    core = [(i ^ 1, i & 1) for i in range(count)]
    stages.append(core)

    def x_of(i):
        return (i >> 1) & 3

    def with_x(i, x):
        return (i & ~6) | (x << 1)

    first, second = [], []
    for i in range(count):
        x = x_of(i)
        if i & 1 == 0:
            first.append((with_x(i, x ^ 1), (x & 1) ^ (x >> 1)))
            second.append((with_x(i, 3 - x), x >> 1))
        else:
            first.append((with_x(i, 3 - x), x >> 1))
            second.append((with_x(i, x ^ 1), x & 1))
    stages.append(first)
    stages.append(second)
    stages.append([(i ^ 8, (i >> 3) & 1) for i in range(count)])
    for s, stage in enumerate(stages):
        for i, (j, k) in enumerate(stage):
            assert stage[j][0] == i and stage[j][1] != k
            for t in range(s):
                assert stages[t][i][1] == stages[t][j][1]
    share = [0] * count
    for i in range(count):
        for stage in stages:
            share[i] = share[i] * 2 + stage[i][1]
    assert sorted(share) == list(range(count))
    return stages, share


def keep_bits(stages, share):
    table = np.array([[stage[i][1] for stage in stages] for i in range(len(share))], np.int32)
    idx = lax.axis_index("aux")
    bits = jnp.asarray(table)[idx]
    return [bits[s] for s in range(len(stages))], jnp.asarray(np.array(share, np.int32))[idx]


def reduce_scatter_rows(value, stages, bits):
    for stage, bit in zip(stages, bits):
        half = value.shape[0] // 2
        pairs = [(i, j) for i, (j, _) in enumerate(stage)]
        keep = lax.dynamic_slice_in_dim(value, bit * half, half, 0)
        send = lax.dynamic_slice_in_dim(value, (1 - bit) * half, half, 0)
        value = keep + lax.ppermute(send, "aux", pairs)
    return value


def all_gather_rows(value, stages, bits):
    for stage, bit in reversed(list(zip(stages, bits))):
        rows = value.shape[0]
        pairs = [(i, j) for i, (j, _) in enumerate(stage)]
        got = lax.ppermute(value, "aux", pairs)
        out = jnp.zeros((2 * rows,) + value.shape[1:], value.dtype)
        out = lax.dynamic_update_slice_in_dim(out, value, bit * rows, 0)
        value = lax.dynamic_update_slice_in_dim(out, got, (1 - bit) * rows, 0)
    return value


def body(factors, eps_occ, eps_vir):
    aux_dev, occ_dev, virt = factors.shape
    width = occ_dev * virt
    group = lax.axis_index("occ")
    groups = lax.axis_size("occ")
    aux_count = lax.axis_size("aux")
    stages, share = aux_stages(aux_count)
    bits, my_share = keep_bits(stages, share)
    rows = width // aux_count

    own = factors.reshape(aux_dev, width)
    below = passed_along(factors, "occ", 1).reshape(aux_dev, width)
    above = passed_along(factors, "occ", -1).reshape(aux_dev, width)

    own_vals = pair_values(eps_occ, eps_vir, group, occ_dev)
    up_vals = pair_values(eps_occ, eps_vir, (group + 1) % groups, occ_dev)
    my_vals = lax.dynamic_slice_in_dim(own_vals, my_share * rows, rows)

    contract_p = (((0,), (0,)), ((), ()))
    contract_b = (((1,), (1,)), ((), ()))
    diag = lax.dot_general(own, own, contract_p, precision=PREC,
                           preferred_element_type=jnp.float32)
    diag_share = reduce_scatter_rows(diag, stages, bits)
    diag_amp = diag_share / (my_vals[:, None] + own_vals[None, :])
    diag_full = all_gather_rows(diag_amp, stages, bits)
    t_own = lax.dot_general(own, diag_full, contract_b, precision=PREC,
                            preferred_element_type=jnp.float32)
    above, below, t_own = lax.optimization_barrier((above, below, t_own))

    up = lax.dot_general(own, above, contract_p, precision=PREC,
                         preferred_element_type=jnp.float32)
    up_share = reduce_scatter_rows(up, stages, bits)
    up_amp = up_share / (my_vals[:, None] + up_vals[None, :])
    prev_amp = passed_along(up_amp, "occ", 1)
    up_full = all_gather_rows(up_amp, stages, bits)
    prev_full = all_gather_rows(prev_amp, stages, bits)
    t_up = lax.dot_general(above, up_full, contract_b, precision=PREC,
                           preferred_element_type=jnp.float32)
    t_prev = lax.dot_general(below, prev_full, (((1,), (0,)), ((), ())),
                             precision=PREC, preferred_element_type=jnp.float32)
    total = t_own + t_up + t_prev
    return (1.3 * total).reshape(aux_dev, occ_dev, virt)


def solution(mesh):
    return jax.shard_map(
        body,
        mesh=mesh,
        in_specs=(P("aux", "occ", None), P(), P()),
        out_specs=P("aux", "occ", None),
        check_vma=False,
    )
```

profile of v0, /device:TPU:1, one launch (start us, length us, event | category | flops | bytes accessed | tf_op | source)
XLA Modules:
  0.0 232.5 jit_solution(12057181936281381765)
XLA Ops:
  0.0 0.7 constant_dynamic-slice_fusion.7
  0.7 0.7 fusion.13
  2.0 7.3 %fusion.4 = f32[768,768]{1,0:T(8,128)S(1)} fusion(f32[1024,1,768]{2,1,0:T(1,128)} %param.5), kind=kOutput, calls=%fused_computation.4 | convolution fusion | flops 3623878656 | bytes 5505024 | tf_op jit(solution)/shard_map/dot_general | solution.py:107
  9.4 1.5 collective-permute-start.2
  12.2 1.3 collective-permute-done.2
  13.5 1.4 dynamic-slice_add_fusion
  14.9 1.0 copy-done.1
  15.9 0.9 constant_dynamic-slice_fusion.5
  16.8 2.6 %collective-permute-start.3 = (f32[192,768]{1,0:T(8,128)}, f32[192,768]{1,0:T(8,128)}, u32[]{:S(2)}, u32[]{:S(2)}) collective-permute-start(f32[192,768]{1,0:T(8,128)} %constant_dynamic-slice_fusion.5), channel_id=1, source_target_pairs={{0,2},{1,7},{2,0},{3,5},{4,6},{5,3},{6,4},{7,1},{8,10},{9,15},{10,... | collective-permute-start | bytes 1769480 | tf_op jit(solution)/shard_map/ppermute | solution.py:72
  20.7 6.3 %collective-permute-done.3 = f32[192,768]{1,0:T(8,128)} collective-permute-done((f32[192,768]{1,0:T(8,128)}, f32[192,768]{1,0:T(8,128)}, u32[]{:S(2)}, u32[]{:S(2)}) %collective-permute-start.3) | collective-permute-done | bytes 589856 | tf_op jit(solution)/shard_map/ppermute | solution.py:72
  27.0 1.3 dynamic-slice_add_fusion.2
  29.2 1.4 collective-permute-start.1
  30.6 2.8 %collective-permute-start = (f32[1024,1,768]{2,1,0:T(1,128)S(1)}, f32[1024,1,768]{2,1,0:T(1,128)}, u32[]{:S(2)}, u32[]{:S(2)}) collective-permute-start(f32[1024,1,768]{2,1,0:T(1,128)S(1)} %copy-done), channel_id=1, source_target_pairs={{0,112},{16,0},{32,16},{48,32},{64,48},{80,64},{96,80},{112,96},{1... | collective-permute-start | bytes 9437192 | tf_op jit(solution)/shard_map/ppermute | solution.py:14
  36.8 0.7 fusion.12
  37.5 1.1 dynamic-slice_add_fusion.4
  38.6 0.7 constant_dynamic-slice_fusion.3
  39.3 3.3 %collective-permute-start.5 = (f32[48,768]{1,0:T(8,128)}, f32[48,768]{1,0:T(8,128)}, u32[]{:S(2)}, u32[]{:S(2)}) collective-permute-start(f32[48,768]{1,0:T(8,128)} %constant_dynamic-slice_fusion.3), channel_id=1, source_target_pairs={{0,8},{1,9},{2,10},{3,11},{4,12},{5,13},{6,14},{7,15},{8,0},{9,1},... | collective-permute-start | bytes 442376 | tf_op jit(solution)/shard_map/ppermute | solution.py:72
  42.6 1.3 broadcast_subtract_fusion
  44.0 64.2 %collective-permute-done.5 = f32[48,768]{1,0:T(8,128)} collective-permute-done((f32[48,768]{1,0:T(8,128)}, f32[48,768]{1,0:T(8,128)}, u32[]{:S(2)}, u32[]{:S(2)}) %collective-permute-start.5) | collective-permute-done | bytes 147488 | tf_op jit(solution)/shard_map/ppermute | solution.py:72
  108.2 1.0 constant_dynamic-update-slice_fusion.23
  109.3 6.4 %collective-permute-done.6 = f32[48,768]{1,0:T(8,128)S(1)} collective-permute-done((f32[48,768]{1,0:T(8,128)S(1)}, f32[48,768]{1,0:T(8,128)S(1)}, u32[]{:S(2)}, u32[]{:S(2)}) %collective-permute-start.6) | collective-permute-done | bytes 147488 | tf_op jit(solution)/shard_map/ppermute | solution.py:80
  115.7 0.9 collective-permute-start.7
  116.6 5.0 %collective-permute-done.7 = f32[96,768]{1,0:T(8,128)S(1)} collective-permute-done((f32[96,768]{1,0:T(8,128)S(1)}, f32[96,768]{1,0:T(8,128)S(1)}, u32[]{:S(2)}, u32[]{:S(2)}) %collective-permute-start.7) | collective-permute-done | bytes 294944 | tf_op jit(solution)/shard_map/ppermute | solution.py:80
  121.7 2.6 %collective-permute-start.8 = (f32[192,768]{1,0:T(8,128)S(1)}, f32[192,768]{1,0:T(8,128)S(1)}, u32[]{:S(2)}, u32[]{:S(2)}) collective-permute-start(f32[192,768]{1,0:T(8,128)S(1)} %constant_dynamic-update-slice_fusion.20), channel_id=1, source_target_pairs={{0,2},{1,7},{2,0},{3,5},{4,6},{5,3},{6,4},{7,1},{8,10},{9,15},{10,... | collective-permute-start | bytes 1769480 | tf_op jit(solution)/shard_map/ppermute | solution.py:80
  124.4 7.3 %collective-permute-done.8 = f32[192,768]{1,0:T(8,128)S(1)} collective-permute-done((f32[192,768]{1,0:T(8,128)S(1)}, f32[192,768]{1,0:T(8,128)S(1)}, u32[]{:S(2)}, u32[]{:S(2)}) %collective-permute-start.8) | collective-permute-done | bytes 589856 | tf_op jit(solution)/shard_map/ppermute | solution.py:80
  131.7 3.6 %collective-permute-start.9 = (f32[384,768]{1,0:T(8,128)S(1)}, f32[384,768]{1,0:T(8,128)S(1)}, u32[]{:S(2)}, u32[]{:S(2)}) collective-permute-start(f32[384,768]{1,0:T(8,128)S(1)} %constant_dynamic-update-slice_fusion.18), channel_id=1, source_target_pairs={{0,1},{1,0},{2,3},{3,2},{4,5},{5,4},{6,7},{7,6},{8,9},{9,8},{10,11... | collective-permute-start | bytes 3538952 | tf_op jit(solution)/shard_map/ppermute | solution.py:80
  135.4 2.1 copy.30
  137.5 2.1 copy.31
  139.9 4.0 %fusion.9 = f32[1024,768]{0,1:T(8,128)S(1)} fusion(f32[768,768]{1,0:T(8,128)S(1)} %constant_dynamic-update-slice_fusion.16, f32[1024,1,768]{2,1,0:T(1,128)S(1)} %copy-done), kind=kOutput, calls=%fused_computation.12 | convolution fusion | flops 3623878656 | bytes 8650752 | tf_op jit(solution)/shard_map/dot_general | solution.py:112
  143.9 4.8 %fusion = f32[768,768]{0,1:T(8,128)S(1)} fusion(f32[1024,768]{1,0:T(8,128)S(1)} %bitcast.40, f32[1024,1,768]{2,1,0:T(1,128)S(1)} %copy-done), kind=kOutput, calls=%fused_computation | convolution fusion | flops 3623878656 | bytes 8650752 | tf_op jit(solution)/shard_map/dot_general | solution.py:116
  148.9 2.8 %collective-permute-done.10 = f32[384,768]{1,0:T(8,128)S(1)} collective-permute-done((f32[384,768]{1,0:T(8,128)S(1)}, f32[384,768]{1,0:T(8,128)S(1)}, u32[]{:S(2)}, u32[]{:S(2)}) %collective-permute-start.10) | collective-permute-done | bytes 1179680 | tf_op jit(solution)/shard_map/ppermute | solution.py:72
  151.9 2.6 %collective-permute-start.11 = (f32[192,768]{1,0:T(8,128)S(1)}, f32[192,768]{1,0:T(8,128)S(1)}, u32[]{:S(2)}, u32[]{:S(2)}) collective-permute-start(f32[192,768]{1,0:T(8,128)S(1)} %constant_dynamic-slice_fusion.2), channel_id=1, source_target_pairs={{0,2},{1,7},{2,0},{3,5},{4,6},{5,3},{6,4},{7,1},{8,10},{9,15},{10,... | collective-permute-start | bytes 1769480 | tf_op jit(solution)/shard_map/ppermute | solution.py:72
  154.5 7.4 %collective-permute-done.11 = f32[192,768]{1,0:T(8,128)S(1)} collective-permute-done((f32[192,768]{1,0:T(8,128)S(1)}, f32[192,768]{1,0:T(8,128)S(1)}, u32[]{:S(2)}, u32[]{:S(2)}) %collective-permute-start.11) | collective-permute-done | bytes 589856 | tf_op jit(solution)/shard_map/ppermute | solution.py:72
  162.2 5.9 %collective-permute-done.12 = f32[96,768]{1,0:T(8,128)S(1)} collective-permute-done((f32[96,768]{1,0:T(8,128)S(1)}, f32[96,768]{1,0:T(8,128)S(1)}, u32[]{:S(2)}, u32[]{:S(2)}) %collective-permute-start.12) | collective-permute-done | bytes 294944 | tf_op jit(solution)/shard_map/ppermute | solution.py:72
  168.2 5.5 %collective-permute-done.13 = f32[48,768]{1,0:T(8,128)S(1)} collective-permute-done((f32[48,768]{1,0:T(8,128)S(1)}, f32[48,768]{1,0:T(8,128)S(1)}, u32[]{:S(2)}, u32[]{:S(2)}) %collective-permute-start.13) | collective-permute-done | bytes 147488 | tf_op jit(solution)/shard_map/ppermute | solution.py:72
  174.0 5.4 %collective-permute-done.14 = f32[48,768]{1,0:T(8,128)S(1)} collective-permute-done((f32[48,768]{1,0:T(8,128)S(1)}, f32[48,768]{1,0:T(8,128)S(1)}, u32[]{:S(2)}, u32[]{:S(2)}) %collective-permute-start.14) | collective-permute-done | bytes 147488 | tf_op jit(solution)/shard_map/ppermute | solution.py:80
  179.4 0.7 collective-permute-start.15
  180.2 2.9 %collective-permute-start.19 = (f32[48,768]{1,0:T(8,128)S(1)}, f32[48,768]{1,0:T(8,128)S(1)}, u32[]{:S(2)}, u32[]{:S(2)}) collective-permute-start(f32[48,768]{1,0:T(8,128)S(1)} %collective-permute-done.18), channel_id=1, source_target_pairs={{0,8},{1,9},{2,10},{3,11},{4,12},{5,13},{6,14},{7,15},{8,0},{9,1},... | collective-permute-start | bytes 442376 | tf_op jit(solution)/shard_map/ppermute | solution.py:80
  183.2 1.9 collective-permute-done.15
  185.1 2.8 %collective-permute-start.16 = (f32[192,768]{1,0:T(8,128)S(1)}, f32[192,768]{1,0:T(8,128)S(1)}, u32[]{:S(2)}, u32[]{:S(2)}) collective-permute-start(f32[192,768]{1,0:T(8,128)S(1)} %constant_dynamic-update-slice_fusion.12), channel_id=1, source_target_pairs={{0,2},{1,7},{2,0},{3,5},{4,6},{5,3},{6,4},{7,1},{8,10},{9,15},{10,... | collective-permute-start | bytes 1769480 | tf_op jit(solution)/shard_map/ppermute | solution.py:80
  188.2 5.6 %collective-permute-done.20 = f32[96,768]{1,0:T(8,128)S(1)} collective-permute-done((f32[96,768]{1,0:T(8,128)S(1)}, f32[96,768]{1,0:T(8,128)S(1)}, u32[]{:S(2)}, u32[]{:S(2)}) %collective-permute-start.20) | collective-permute-done | bytes 294944 | tf_op jit(solution)/shard_map/ppermute | solution.py:80
  193.9 2.0 collective-permute-start.21
  196.0 1.7 collective-permute-done.16
  197.8 10.5 %collective-permute-start.17 = (f32[384,768]{1,0:T(8,128)S(1)}, f32[384,768]{1,0:T(8,128)S(1)}, u32[]{:S(2)}, u32[]{:S(2)}) collective-permute-start(f32[384,768]{1,0:T(8,128)S(1)} %constant_dynamic-update-slice_fusion.10), channel_id=1, source_target_pairs={{0,1},{1,0},{2,3},{3,2},{4,5},{5,4},{6,7},{7,6},{8,9},{9,8},{10,11... | collective-permute-start | bytes 3538952 | tf_op jit(solution)/shard_map/ppermute | solution.py:80
  208.5 9.5 %collective-permute-start.22 = (f32[384,768]{1,0:T(8,128)S(1)}, f32[384,768]{1,0:T(8,128)S(1)}, u32[]{:S(2)}, u32[]{:S(2)}) collective-permute-start(f32[384,768]{1,0:T(8,128)S(1)} %constant_dynamic-update-slice_fusion.2), channel_id=1, source_target_pairs={{0,1},{1,0},{2,3},{3,2},{4,5},{5,4},{6,7},{7,6},{8,9},{9,8},{10,11... | collective-permute-start | bytes 3538952 | tf_op jit(solution)/shard_map/ppermute | solution.py:80
  218.7 4.1 %fusion.14 = f32[1024,768]{0,1:T(8,128)S(1)} fusion(f32[1024,768]{1,0:T(8,128)S(1)} %bitcast.41, f32[768,768]{1,0:T(8,128)S(1)} %constant_dynamic-update-slice_fusion.8), kind=kOutput, calls=%fused_computation.58 | convolution fusion | flops 3623878656 | bytes 8650752 | tf_op jit(solution)/shard_map/dot_general | solution.py:123
  222.9 4.3 %multiply_bitcast_fusion = f32[1024,1,768]{0,2,1:T(8,128)S(1)} fusion(f32[1024,768]{0,1:T(8,128)S(1)} %fusion.9, f32[1024,768]{0,1:T(8,128)S(1)} %fusion.14, f32[1024,768]{1,0:T(8,128)S(1)} %bitcast.42, f32[768,768]{1,0:T(8,128)S(1)} %constant_dynamic-update-slice_fusion), kind=kOutput, calls=%fused_computation.8 | convolution fusion | flops 3626237952 | bytes 14942208 | tf_op jit(solution)/shard_map/dot_general | solution.py:125
  227.2 5.3 %copy.8 = f32[1024,1,768]{2,1,0:T(1,128)} copy(f32[1024,1,768]{0,2,1:T(8,128)S(1)} %multiply_bitcast_fusion) | data formatting | bytes 6291456 | tf_op jit(solution)/shard_map/reshape | solution.py:128
  (74 shorter events, 4.9 us)
Async XLA Ops:
  9.4 4.1 %collective-permute-start.2 = (f32[384,768]{1,0:T(8,128)S(1)}, f32[384,768]{1,0:T(8,128)}, u32[]{:S(2)}, u32[]{:S(2)}) collective-permute-start(f32[384,768]{1,0:T(8,128)S(1)} %constant_dynamic-slice_fusion.6), channel_id=1, source_target_pairs={{0,1},{1,0},{2,3},{3,2},{4,5},{5,4},{6,7},{7,6},{8,9},{9,8},{10,11... | collective-permute-start | bytes 3538952 | tf_op jit(solution)/shard_map/ppermute | solution.py:72
  14.9 1.0 copy-start.1
  15.9 13.3 %copy-start = (f32[1024,1,768]{2,1,0:T(1,128)S(1)}, f32[1024,1,768]{2,1,0:T(1,128)}, u32[]{:S(2)}) copy-start(f32[1024,1,768]{2,1,0:T(1,128)} %param.5) | copy-start | bytes 9437188
  15.9 18.2 %copy-start.5 = (s32[16]{0:T(128)S(1)}, s32[16]{0:T(128)}, u32[]{:S(2)}) copy-start(s32[16]{0:T(128)} %constant.68.clone) | copy-start | bytes 196
  15.9 20.9 %copy-start.4 = (f32[8]{0:T(128)S(1)}, f32[8]{0:T(128)}, u32[]{:S(2)}) copy-start(f32[8]{0:T(128)} %param.6) | copy-start | bytes 100
  15.9 26.7 %copy-start.3 = (f32[768]{0:T(1024)S(1)}, f32[768]{0:T(1024)}, u32[]{:S(2)}) copy-start(f32[768]{0:T(1024)} %param.7) | copy-start | bytes 9220
  16.8 10.3 %collective-permute-start.3 = (f32[192,768]{1,0:T(8,128)}, f32[192,768]{1,0:T(8,128)}, u32[]{:S(2)}, u32[]{:S(2)}) collective-permute-start(f32[192,768]{1,0:T(8,128)} %constant_dynamic-slice_fusion.5), channel_id=1, source_target_pairs={{0,2},{1,7},{2,0},{3,5},{4,6},{5,3},{6,4},{7,1},{8,10},{9,15},{10,... | collective-permute-start | bytes 1769480 | tf_op jit(solution)/shard_map/ppermute | solution.py:72
  28.3 0.8 copy-start.2
  28.4 9.1 %collective-permute-start.4 = (f32[96,768]{1,0:T(8,128)S(1)}, f32[96,768]{1,0:T(8,128)}, u32[]{:S(2)}, u32[]{:S(2)}) collective-permute-start(f32[96,768]{1,0:T(8,128)S(1)} %constant_dynamic-slice_fusion.4), channel_id=1, source_target_pairs={{0,6},{1,3},{2,4},{3,1},{4,2},{5,7},{6,0},{7,5},{8,14},{9,11},{10,... | collective-permute-start | bytes 884744 | tf_op jit(solution)/shard_map/ppermute | solution.py:72
  29.2 106.2 %collective-permute-start.1 = (f32[1024,1,768]{2,1,0:T(1,128)S(1)}, f32[1024,1,768]{2,1,0:T(1,128)}, u32[]{:S(2)}, u32[]{:S(2)}) collective-permute-start(f32[1024,1,768]{2,1,0:T(1,128)S(1)} %copy-done), channel_id=1, source_target_pairs={{0,16},{16,32},{32,48},{48,64},{64,80},{80,96},{96,112},{112,0},{1... | collective-permute-start | bytes 9437192 | tf_op jit(solution)/shard_map/ppermute | solution.py:14
  30.6 106.9 %collective-permute-start = (f32[1024,1,768]{2,1,0:T(1,128)S(1)}, f32[1024,1,768]{2,1,0:T(1,128)}, u32[]{:S(2)}, u32[]{:S(2)}) collective-permute-start(f32[1024,1,768]{2,1,0:T(1,128)S(1)} %copy-done), channel_id=1, source_target_pairs={{0,112},{16,0},{32,16},{48,32},{64,48},{80,64},{96,80},{112,96},{1... | collective-permute-start | bytes 9437192 | tf_op jit(solution)/shard_map/ppermute | solution.py:14
  39.3 68.9 %collective-permute-start.5 = (f32[48,768]{1,0:T(8,128)}, f32[48,768]{1,0:T(8,128)}, u32[]{:S(2)}, u32[]{:S(2)}) collective-permute-start(f32[48,768]{1,0:T(8,128)} %constant_dynamic-slice_fusion.3), channel_id=1, source_target_pairs={{0,8},{1,9},{2,10},{3,11},{4,12},{5,13},{6,14},{7,15},{8,0},{9,1},... | collective-permute-start | bytes 442376 | tf_op jit(solution)/shard_map/ppermute | solution.py:72
  109.2 6.5 %collective-permute-start.6 = (f32[48,768]{1,0:T(8,128)S(1)}, f32[48,768]{1,0:T(8,128)S(1)}, u32[]{:S(2)}, u32[]{:S(2)}) collective-permute-start(f32[48,768]{1,0:T(8,128)S(1)} %get-tuple-element.14), channel_id=1, source_target_pairs={{0,8},{1,9},{2,10},{3,11},{4,12},{5,13},{6,14},{7,15},{8,0},{9,1},... | collective-permute-start | bytes 442376 | tf_op jit(solution)/shard_map/ppermute | solution.py:80
  115.7 5.9 %collective-permute-start.7 = (f32[96,768]{1,0:T(8,128)S(1)}, f32[96,768]{1,0:T(8,128)S(1)}, u32[]{:S(2)}, u32[]{:S(2)}) collective-permute-start(f32[96,768]{1,0:T(8,128)S(1)} %constant_dynamic-update-slice_fusion.22), channel_id=1, source_target_pairs={{0,6},{1,3},{2,4},{3,1},{4,2},{5,7},{6,0},{7,5},{8,14},{9,11},{10,... | collective-permute-start | bytes 884744 | tf_op jit(solution)/shard_map/ppermute | solution.py:80
  121.7 10.0 %collective-permute-start.8 = (f32[192,768]{1,0:T(8,128)S(1)}, f32[192,768]{1,0:T(8,128)S(1)}, u32[]{:S(2)}, u32[]{:S(2)}) collective-permute-start(f32[192,768]{1,0:T(8,128)S(1)} %constant_dynamic-update-slice_fusion.20), channel_id=1, source_target_pairs={{0,2},{1,7},{2,0},{3,5},{4,6},{5,3},{6,4},{7,1},{8,10},{9,15},{10,... | collective-permute-start | bytes 1769480 | tf_op jit(solution)/shard_map/ppermute | solution.py:80
  131.7 8.1 %collective-permute-start.9 = (f32[384,768]{1,0:T(8,128)S(1)}, f32[384,768]{1,0:T(8,128)S(1)}, u32[]{:S(2)}, u32[]{:S(2)}) collective-permute-start(f32[384,768]{1,0:T(8,128)S(1)} %constant_dynamic-update-slice_fusion.18), channel_id=1, source_target_pairs={{0,1},{1,0},{2,3},{3,2},{4,5},{5,4},{6,7},{7,6},{8,9},{9,8},{10,11... | collective-permute-start | bytes 3538952 | tf_op jit(solution)/shard_map/ppermute | solution.py:80
  148.8 2.9 %collective-permute-start.10 = (f32[384,768]{1,0:T(8,128)S(1)}, f32[384,768]{1,0:T(8,128)S(1)}, u32[]{:S(2)}, u32[]{:S(2)}) collective-permute-start(f32[384,768]{1,0:T(8,128)S(1)} %dynamic-slice_bitcast_fusion), channel_id=1, source_target_pairs={{0,1},{1,0},{2,3},{3,2},{4,5},{5,4},{6,7},{7,6},{8,9},{9,8},{10,11... | collective-permute-start | bytes 3538952 | tf_op jit(solution)/shard_map/ppermute | solution.py:72
  151.9 10.0 %collective-permute-start.11 = (f32[192,768]{1,0:T(8,128)S(1)}, f32[192,768]{1,0:T(8,128)S(1)}, u32[]{:S(2)}, u32[]{:S(2)}) collective-permute-start(f32[192,768]{1,0:T(8,128)S(1)} %constant_dynamic-slice_fusion.2), channel_id=1, source_target_pairs={{0,2},{1,7},{2,0},{3,5},{4,6},{5,3},{6,4},{7,1},{8,10},{9,15},{10,... | collective-permute-start | bytes 1769480 | tf_op jit(solution)/shard_map/ppermute | solution.py:72
  162.1 5.9 %collective-permute-start.12 = (f32[96,768]{1,0:T(8,128)S(1)}, f32[96,768]{1,0:T(8,128)S(1)}, u32[]{:S(2)}, u32[]{:S(2)}) collective-permute-start(f32[96,768]{1,0:T(8,128)S(1)} %constant_dynamic-slice_fusion.1), channel_id=1, source_target_pairs={{0,6},{1,3},{2,4},{3,1},{4,2},{5,7},{6,0},{7,5},{8,14},{9,11},{10,... | collective-permute-start | bytes 884744 | tf_op jit(solution)/shard_map/ppermute | solution.py:72
  168.1 5.6 %collective-permute-start.13 = (f32[48,768]{1,0:T(8,128)S(1)}, f32[48,768]{1,0:T(8,128)S(1)}, u32[]{:S(2)}, u32[]{:S(2)}) collective-permute-start(f32[48,768]{1,0:T(8,128)S(1)} %constant_dynamic-slice_fusion), channel_id=1, source_target_pairs={{0,8},{1,9},{2,10},{3,11},{4,12},{5,13},{6,14},{7,15},{8,0},{9,1},... | collective-permute-start | bytes 442376 | tf_op jit(solution)/shard_map/ppermute | solution.py:72
  173.8 5.6 %collective-permute-start.14 = (f32[48,768]{1,0:T(8,128)S(1)}, f32[48,768]{1,0:T(8,128)S(1)}, u32[]{:S(2)}, u32[]{:S(2)}) collective-permute-start(f32[48,768]{1,0:T(8,128)S(1)} %get-tuple-element.12), channel_id=1, source_target_pairs={{0,8},{1,9},{2,10},{3,11},{4,12},{5,13},{6,14},{7,15},{8,0},{9,1},... | collective-permute-start | bytes 442376 | tf_op jit(solution)/shard_map/ppermute | solution.py:80
  173.9 6.3 %collective-permute-start.18 = (f32[48,768]{1,0:T(8,128)S(1)}, f32[48,768]{1,0:T(8,128)S(1)}, u32[]{:S(2)}, u32[]{:S(2)}) collective-permute-start(f32[48,768]{1,0:T(8,128)S(1)} %get-tuple-element.12), channel_id=1, source_target_pairs={{0,16},{16,32},{32,48},{48,64},{64,80},{80,96},{96,112},{112,0},{1... | collective-permute-start | bytes 442376 | tf_op jit(solution)/shard_map/ppermute | solution.py:14
  179.4 5.7 %collective-permute-start.15 = (f32[96,768]{1,0:T(8,128)S(1)}, f32[96,768]{1,0:T(8,128)S(1)}, u32[]{:S(2)}, u32[]{:S(2)}) collective-permute-start(f32[96,768]{1,0:T(8,128)S(1)} %constant_dynamic-update-slice_fusion.14), channel_id=1, source_target_pairs={{0,6},{1,3},{2,4},{3,1},{4,2},{5,7},{6,0},{7,5},{8,14},{9,11},{10,... | collective-permute-start | bytes 884744 | tf_op jit(solution)/shard_map/ppermute | solution.py:80
  180.2 7.7 %collective-permute-start.19 = (f32[48,768]{1,0:T(8,128)S(1)}, f32[48,768]{1,0:T(8,128)S(1)}, u32[]{:S(2)}, u32[]{:S(2)}) collective-permute-start(f32[48,768]{1,0:T(8,128)S(1)} %collective-permute-done.18), channel_id=1, source_target_pairs={{0,8},{1,9},{2,10},{3,11},{4,12},{5,13},{6,14},{7,15},{8,0},{9,1},... | collective-permute-start | bytes 442376 | tf_op jit(solution)/shard_map/ppermute | solution.py:80
  185.1 12.7 %collective-permute-start.16 = (f32[192,768]{1,0:T(8,128)S(1)}, f32[192,768]{1,0:T(8,128)S(1)}, u32[]{:S(2)}, u32[]{:S(2)}) collective-permute-start(f32[192,768]{1,0:T(8,128)S(1)} %constant_dynamic-update-slice_fusion.12), channel_id=1, source_target_pairs={{0,2},{1,7},{2,0},{3,5},{4,6},{5,3},{6,4},{7,1},{8,10},{9,15},{10,... | collective-permute-start | bytes 1769480 | tf_op jit(solution)/shard_map/ppermute | solution.py:80
  187.9 5.9 %collective-permute-start.20 = (f32[96,768]{1,0:T(8,128)S(1)}, f32[96,768]{1,0:T(8,128)S(1)}, u32[]{:S(2)}, u32[]{:S(2)}) collective-permute-start(f32[96,768]{1,0:T(8,128)S(1)} %constant_dynamic-update-slice_fusion.6), channel_id=1, source_target_pairs={{0,6},{1,3},{2,4},{3,1},{4,2},{5,7},{6,0},{7,5},{8,14},{9,11},{10,... | collective-permute-start | bytes 884744 | tf_op jit(solution)/shard_map/ppermute | solution.py:80
  193.9 14.6 %collective-permute-start.21 = (f32[192,768]{1,0:T(8,128)S(1)}, f32[192,768]{1,0:T(8,128)S(1)}, u32[]{:S(2)}, u32[]{:S(2)}) collective-permute-start(f32[192,768]{1,0:T(8,128)S(1)} %constant_dynamic-update-slice_fusion.4), channel_id=1, source_target_pairs={{0,2},{1,7},{2,0},{3,5},{4,6},{5,3},{6,4},{7,1},{8,10},{9,15},{10,... | collective-permute-start | bytes 1769480 | tf_op jit(solution)/shard_map/ppermute | solution.py:80
  197.8 20.7 %collective-permute-start.17 = (f32[384,768]{1,0:T(8,128)S(1)}, f32[384,768]{1,0:T(8,128)S(1)}, u32[]{:S(2)}, u32[]{:S(2)}) collective-permute-start(f32[384,768]{1,0:T(8,128)S(1)} %constant_dynamic-update-slice_fusion.10), channel_id=1, source_target_pairs={{0,1},{1,0},{2,3},{3,2},{4,5},{5,4},{6,7},{7,6},{8,9},{9,8},{10,11... | collective-permute-start | bytes 3538952 | tf_op jit(solution)/shard_map/ppermute | solution.py:80
  208.5 14.2 %collective-permute-start.22 = (f32[384,768]{1,0:T(8,128)S(1)}, f32[384,768]{1,0:T(8,128)S(1)}, u32[]{:S(2)}, u32[]{:S(2)}) collective-permute-start(f32[384,768]{1,0:T(8,128)S(1)} %constant_dynamic-update-slice_fusion.2), channel_id=1, source_target_pairs={{0,1},{1,0},{2,3},{3,2},{4,5},{5,4},{6,7},{7,6},{8,9},{9,8},{10,11... | collective-permute-start | bytes 3538952 | tf_op jit(solution)/shard_map/ppermute | solution.py:80
where the time goes:
time: 233 us
  waiting for transfers between devices  127 us (55%)
  starting transfers between devices  50.9 us (22%)
  matrix products  24.5 us (11%)
  local copies, waits for them, and re-layouts  17.3 us (7%)
  between operations  6.64 us (3%)
  other arithmetic  6.47 us (3%)
    ppermute x8, waiting for transfers between devices, reduce_scatter_rows(): value = keep + lax.ppermute(send, 'aux', pairs)  93.3 us
    ppermute x12, starting transfers between devices, all_gather_rows(): got = lax.ppermute(value, 'aux', pairs)  35.9 us
    ppermute x12, waiting for transfers between devices, all_gather_rows(): got = lax.ppermute(value, 'aux', pairs)  33.4 us
    ppermute x8, starting transfers between devices, reduce_scatter_rows(): value = keep + lax.ppermute(send, 'aux', pairs)  10.7 us
    dot_general x1, matrix products, body(): lax.dot_general(own, own, contract_p, precision=PREC, preferred_element_t...  7.27 us
    unnamed x14, local copies, waits for them, and re-layouts  5.49 us
    reshape x1, local copies, waits for them, and re-layouts, body(): return (1.3 * total).reshape(aux_dev, occ_dev, virt)  5.31 us
    dot_general x1, matrix products, body(): lax.dot_general(own, above, contract_p, precision=PREC, preferred_element...  4.78 us
  transfers between devices with their start and end apart: 23, of which 15 were waited for; matrix products, arithmetic and copies ran while one was open for 7% of the time, Pallas kernels for 0%

commit v1 on v0

--- a/solution.py
+++ b/solution.py
@@ -95,8 +95,8 @@
     rows = width // aux_count
 
     own = factors.reshape(aux_dev, width)
-    below = passed_along(factors, "occ", 1).reshape(aux_dev, width)
-    above = passed_along(factors, "occ", -1).reshape(aux_dev, width)
+    below = passed_along(own, "occ", 1)
+    above = passed_along(own, "occ", -1)
 
     own_vals = pair_values(eps_occ, eps_vir, group, occ_dev)
     up_vals = pair_values(eps_occ, eps_vir, (group + 1) % groups, occ_dev)
@@ -108,10 +108,10 @@
                            preferred_element_type=jnp.float32)
     diag_share = reduce_scatter_rows(diag, stages, bits)
     diag_amp = diag_share / (my_vals[:, None] + own_vals[None, :])
+    above, below, diag_amp = lax.optimization_barrier((above, below, diag_amp))
     diag_full = all_gather_rows(diag_amp, stages, bits)
     t_own = lax.dot_general(own, diag_full, contract_b, precision=PREC,
                             preferred_element_type=jnp.float32)
-    above, below, t_own = lax.optimization_barrier((above, below, t_own))
 
     up = lax.dot_general(own, above, contract_p, precision=PREC,
                          preferred_element_type=jnp.float32)

time: 233 us -> 194 us (0.83)
  waiting for transfers between devices: 127 us -> 99 us
  starting transfers between devices: 50.9 us -> 30.8 us
  matrix products: 24.5 us -> 31.5 us
    ppermute x8, waiting for transfers between devices: 93.3 us -> 68.2 us  [reduce_scatter_rows(): value = keep + lax.ppermute(send, 'aux', pairs)]
    ppermute x12, starting transfers between devices: 35.9 us -> 15.5 us  [all_gather_rows(): got = lax.ppermute(value, 'aux', pairs)]
    dynamic_slice x8, local copies, waits for them, and re-layouts: 1.84 us -> 6.24 us  [reduce_scatter_rows(): send = lax.dynamic_slice_in_dim(value, (1 - bit) * half, half, 0)]
    unnamed x14 -> x9, local copies, waits for them, and re-layouts: 5.49 us -> 1.88 us
    ppermute x12, waiting for transfers between devices: 33.4 us -> 30.8 us  [all_gather_rows(): got = lax.ppermute(value, 'aux', pairs)]
  transfers between devices with their start and end apart: 23 -> 23, of which waited for: 15 -> 12; matrix products, arithmetic and copies ran while one was open for 7% -> 14% of each run, Pallas kernels for 0% -> 0%
where the time goes in v1:
time: 194 us; the launch traced here: 193 us
  waiting for transfers between devices  99 us (51%)
  matrix products  31.5 us (16%)
  starting transfers between devices  30.8 us (16%)
  local copies, waits for them, and re-layouts  18 us (9%)
  other arithmetic  7.57 us (4%)
  between operations  6.25 us (3%)
    ppermute x8, waiting for transfers between devices, reduce_scatter_rows(): value = keep + lax.ppermute(send, 'aux', pairs)  68.2 us
    ppermute x12, waiting for transfers between devices, all_gather_rows(): got = lax.ppermute(value, 'aux', pairs)  30.8 us
    ppermute x12, starting transfers between devices, all_gather_rows(): got = lax.ppermute(value, 'aux', pairs)  15.5 us
    ppermute x8, starting transfers between devices, reduce_scatter_rows(): value = keep + lax.ppermute(send, 'aux', pairs)  11 us
    dot_general x1, matrix products, body(): lax.dot_general(own, own, contract_p, precision=PREC, preferred_element_t...  8.86 us
    dot_general x1, matrix products, body(): lax.dot_general(own, above, contract_p, precision=PREC, preferred_element...  6.6 us
    dynamic_slice x8, local copies, waits for them, and re-layouts, reduce_scatter_rows(): send = lax.dynamic_slice_in_dim(value, (1 - bit) * half, half, 0)  6.24 us
    add x6, other arithmetic, reduce_scatter_rows(): value = keep + lax.ppermute(send, 'aux', pairs)  6.18 us
  transfers between devices with their start and end apart: 23, of which 12 were waited for; matrix products, arithmetic and copies ran while one was open for 14% of the time, Pallas kernels for 0%

profile of v1, /device:TPU:1, one launch (start us, length us, event | category | flops | bytes accessed | tf_op | source)
XLA Modules:
  0.0 193.2 jit_solution(16606573346754457013)
XLA Ops:
  0.0 8.9 %fusion.5 = f32[768,768]{1,0:T(8,128)} fusion(f32[1024,1,768]{2,1,0:T(1,128)} %param.5), kind=kOutput, calls=%fused_computation.50 | convolution fusion | flops 3623878656 | bytes 5505024 | tf_op jit(solution)/shard_map/dot_general | solution.py:107
  8.9 0.7 constant_dynamic-slice_fusion.7
  9.6 0.7 fusion.7
  10.9 2.4 %constant_dynamic-slice_fusion.6 = f32[384,768]{1,0:T(8,128)} fusion(f32[768,768]{1,0:T(8,128)} %fusion.5, s32[]{:T(128)S(6)} %select_n.33), kind=kLoop, calls=%fused_computation.44 | loop fusion | bytes 2359300 | tf_op jit(solution)/shard_map/dynamic_slice | solution.py:71
  13.2 1.4 collective-permute-start.2
  14.6 1.9 copy.16
  16.5 4.2 %collective-permute-start = (f32[1024,768]{1,0:T(8,128)}, f32[1024,768]{1,0:T(8,128)}, u32[]{:S(2)}, u32[]{:S(2)}) collective-permute-start(f32[1024,768]{1,0:T(8,128)} %bitcast.36), channel_id=1, source_target_pairs={{0,112},{16,0},{32,16},{48,32},{64,48},{80,64},{96,80},{112,96},{1... | collective-permute-start | bytes 9437192 | tf_op jit(solution)/shard_map/ppermute | solution.py:14
  22.0 2.8 %dynamic-slice_add_fusion = f32[384,768]{1,0:T(8,128)} fusion(f32[384,768]{1,0:T(8,128)} %collective-permute-done.2, f32[768,768]{1,0:T(8,128)} %fusion.5, s32[]{:T(128)S(6)} %select_n.32), kind=kLoop, calls=%fused_computation.7 | loop fusion | flops 294912 | bytes 3538948 | tf_op jit(solution)/shard_map/add | solution.py:72
  24.8 2.0 %constant_dynamic-slice_fusion.5 = f32[192,768]{1,0:T(8,128)} fusion(f32[384,768]{1,0:T(8,128)} %dynamic-slice_add_fusion, s32[]{:T(128)S(6)} %select_n.35), kind=kLoop, calls=%fused_computation.43 | loop fusion | bytes 1179652 | tf_op jit(solution)/shard_map/dynamic_slice | solution.py:71
  26.8 2.5 %collective-permute-start.3 = (f32[192,768]{1,0:T(8,128)}, f32[192,768]{1,0:T(8,128)}, u32[]{:S(2)}, u32[]{:S(2)}) collective-permute-start(f32[192,768]{1,0:T(8,128)} %constant_dynamic-slice_fusion.5), channel_id=1, source_target_pairs={{0,2},{1,7},{2,0},{3,5},{4,6},{5,3},{6,4},{7,1},{8,10},{9,15},{10,... | collective-permute-start | bytes 1769480 | tf_op jit(solution)/shard_map/ppermute | solution.py:72
  30.5 6.8 %collective-permute-done.3 = f32[192,768]{1,0:T(8,128)} collective-permute-done((f32[192,768]{1,0:T(8,128)}, f32[192,768]{1,0:T(8,128)}, u32[]{:S(2)}, u32[]{:S(2)}) %collective-permute-start.3) | collective-permute-done | bytes 589856 | tf_op jit(solution)/shard_map/ppermute | solution.py:72
  37.3 2.1 %dynamic-slice_add_fusion.2 = f32[192,768]{1,0:T(8,128)} fusion(f32[192,768]{1,0:T(8,128)} %collective-permute-done.3, f32[384,768]{1,0:T(8,128)} %dynamic-slice_add_fusion, s32[]{:T(128)S(6)} %select_n.34), kind=kLoop, calls=%fused_computation.9 | loop fusion | flops 147456 | bytes 1769476 | tf_op jit(solution)/shard_map/add | solution.py:72
  39.5 1.7 constant_dynamic-slice_fusion.4
  42.9 0.7 dynamic_slice.71
  44.3 0.6 fusion.6
  45.0 2.4 %collective-permute-done.4 = f32[96,768]{1,0:T(8,128)S(1)} collective-permute-done((f32[96,768]{1,0:T(8,128)}, f32[96,768]{1,0:T(8,128)S(1)}, u32[]{:S(2)}, u32[]{:S(2)}) %collective-permute-start.4) | collective-permute-done | bytes 294944 | tf_op jit(solution)/shard_map/ppermute | solution.py:72
  47.4 1.0 dynamic-slice_add_fusion.4
  48.4 3.6 %collective-permute-start.5 = (f32[48,768]{1,0:T(8,128)S(1)}, f32[48,768]{1,0:T(8,128)S(1)}, u32[]{:S(2)}, u32[]{:S(2)}) collective-permute-start(f32[48,768]{1,0:T(8,128)S(1)} %constant_dynamic-slice_fusion.3), channel_id=1, source_target_pairs={{0,8},{1,9},{2,10},{3,11},{4,12},{5,13},{6,14},{7,15},{8,0},{9,1},... | collective-permute-start | bytes 442376 | tf_op jit(solution)/shard_map/ppermute | solution.py:72
  51.9 1.2 broadcast_subtract_fusion
  53.2 44.9 %collective-permute-done.5 = f32[48,768]{1,0:T(8,128)S(1)} collective-permute-done((f32[48,768]{1,0:T(8,128)S(1)}, f32[48,768]{1,0:T(8,128)S(1)}, u32[]{:S(2)}, u32[]{:S(2)}) %collective-permute-start.5) | collective-permute-done | bytes 147488 | tf_op jit(solution)/shard_map/ppermute | solution.py:72
  98.3 6.6 %fusion.3 = f32[768,768]{0,1:T(8,128)S(1)} fusion(f32[1024,768]{1,0:T(8,128)} %collective-permute-done, f32[1024,1,768]{2,1,0:T(1,128)S(1)} %copy-done), kind=kOutput, calls=%fused_computation.48 | convolution fusion | flops 3623878656 | bytes 8650752 | tf_op jit(solution)/shard_map/dot_general | solution.py:116
  105.0 0.6 collective-permute-start.10
  105.5 2.5 %collective-permute-done.10 = f32[384,768]{1,0:T(8,128)S(1)} collective-permute-done((f32[384,768]{1,0:T(8,128)S(1)}, f32[384,768]{1,0:T(8,128)S(1)}, u32[]{:S(2)}, u32[]{:S(2)}) %collective-permute-start.10) | collective-permute-done | bytes 1179680 | tf_op jit(solution)/shard_map/ppermute | solution.py:72
  108.0 0.1 bitcast_add_fusion.1
  108.2 2.6 %collective-permute-start.11 = (f32[192,768]{1,0:T(8,128)S(1)}, f32[192,768]{1,0:T(8,128)S(1)}, u32[]{:S(2)}, u32[]{:S(2)}) collective-permute-start(f32[192,768]{1,0:T(8,128)S(1)} %constant_dynamic-slice_fusion.2), channel_id=1, source_target_pairs={{0,2},{1,7},{2,0},{3,5},{4,6},{5,3},{6,4},{7,1},{8,10},{9,15},{10,... | collective-permute-start | bytes 1769480 | tf_op jit(solution)/shard_map/ppermute | solution.py:72
  110.8 7.5 %collective-permute-done.11 = f32[192,768]{1,0:T(8,128)S(1)} collective-permute-done((f32[192,768]{1,0:T(8,128)S(1)}, f32[192,768]{1,0:T(8,128)S(1)}, u32[]{:S(2)}, u32[]{:S(2)}) %collective-permute-start.11) | collective-permute-done | bytes 589856 | tf_op jit(solution)/shard_map/ppermute | solution.py:72
  118.3 0.4 collective-permute-start.12
  118.8 1.3 collective-permute-start.7
  120.1 4.2 %collective-permute-done.12 = f32[96,768]{1,0:T(8,128)S(1)} collective-permute-done((f32[96,768]{1,0:T(8,128)S(1)}, f32[96,768]{1,0:T(8,128)S(1)}, u32[]{:S(2)}, u32[]{:S(2)}) %collective-permute-start.12) | collective-permute-done | bytes 294944 | tf_op jit(solution)/shard_map/ppermute | solution.py:72
  124.5 3.0 %collective-permute-done.7 = f32[96,768]{1,0:T(8,128)S(1)} collective-permute-done((f32[96,768]{1,0:T(8,128)S(1)}, f32[96,768]{1,0:T(8,128)S(1)}, u32[]{:S(2)}, u32[]{:S(2)}) %collective-permute-start.7) | collective-permute-done | bytes 294944 | tf_op jit(solution)/shard_map/ppermute | solution.py:80
  127.5 2.6 %collective-permute-start.8 = (f32[192,768]{1,0:T(8,128)S(1)}, f32[192,768]{1,0:T(8,128)S(1)}, u32[]{:S(2)}, u32[]{:S(2)}) collective-permute-start(f32[192,768]{1,0:T(8,128)S(1)} %constant_dynamic-update-slice_fusion.20), channel_id=1, source_target_pairs={{0,2},{1,7},{2,0},{3,5},{4,6},{5,3},{6,4},{7,1},{8,10},{9,15},{10,... | collective-permute-start | bytes 1769480 | tf_op jit(solution)/shard_map/ppermute | solution.py:80
  130.5 5.3 %collective-permute-done.14 = f32[48,768]{1,0:T(8,128)S(1)} collective-permute-done((f32[48,768]{1,0:T(8,128)S(1)}, f32[48,768]{1,0:T(8,128)S(1)}, u32[]{:S(2)}, u32[]{:S(2)}) %collective-permute-start.14) | collective-permute-done | bytes 147488 | tf_op jit(solution)/shard_map/ppermute | solution.py:80
  135.8 0.3 collective-permute-start.15
  136.0 1.5 collective-permute-done.8
  137.6 7.0 %collective-permute-start.9 = (f32[384,768]{1,0:T(8,128)S(1)}, f32[384,768]{1,0:T(8,128)S(1)}, u32[]{:S(2)}, u32[]{:S(2)}) collective-permute-start(f32[384,768]{1,0:T(8,128)S(1)} %constant_dynamic-update-slice_fusion.18), channel_id=1, source_target_pairs={{0,1},{1,0},{2,3},{3,2},{4,5},{5,4},{6,7},{7,6},{8,9},{9,8},{10,11... | collective-permute-start | bytes 3538952 | tf_op jit(solution)/shard_map/ppermute | solution.py:80
  144.8 0.4 collective-permute-start.16
  145.2 6.4 %collective-permute-done.19 = f32[48,768]{1,0:T(8,128)S(1)} collective-permute-done((f32[48,768]{1,0:T(8,128)S(1)}, f32[48,768]{1,0:T(8,128)S(1)}, u32[]{:S(2)}, u32[]{:S(2)}) %collective-permute-start.19) | collective-permute-done | bytes 147488 | tf_op jit(solution)/shard_map/ppermute | solution.py:80
  151.8 8.9 %collective-permute-done.20 = f32[96,768]{1,0:T(8,128)S(1)} collective-permute-done((f32[96,768]{1,0:T(8,128)S(1)}, f32[96,768]{1,0:T(8,128)S(1)}, u32[]{:S(2)}, u32[]{:S(2)}) %collective-permute-start.20) | collective-permute-done | bytes 294944 | tf_op jit(solution)/shard_map/ppermute | solution.py:80
  161.0 3.4 %collective-permute-start.17 = (f32[384,768]{1,0:T(8,128)S(1)}, f32[384,768]{1,0:T(8,128)S(1)}, u32[]{:S(2)}, u32[]{:S(2)}) collective-permute-start(f32[384,768]{1,0:T(8,128)S(1)} %constant_dynamic-update-slice_fusion.10), channel_id=1, source_target_pairs={{0,1},{1,0},{2,3},{3,2},{4,5},{5,4},{6,7},{7,6},{8,9},{9,8},{10,11... | collective-permute-start | bytes 3538952 | tf_op jit(solution)/shard_map/ppermute | solution.py:80
  164.4 0.2 broadcast.20.clone.1
  164.9 5.8 %collective-permute-done.21 = f32[192,768]{1,0:T(8,128)S(1)} collective-permute-done((f32[192,768]{1,0:T(8,128)S(1)}, f32[192,768]{1,0:T(8,128)S(1)}, u32[]{:S(2)}, u32[]{:S(2)}) %collective-permute-start.21) | collective-permute-done | bytes 589856 | tf_op jit(solution)/shard_map/ppermute | solution.py:80
  170.8 0.3 collective-permute-start.22
  171.1 4.0 %fusion.4 = f32[768,1024]{1,0:T(8,128)S(1)} fusion(f32[768,768]{1,0:T(8,128)S(1)} %constant_dynamic-update-slice_fusion.16, f32[1024,1,768]{2,1,0:T(1,128)S(1)} %copy-done), kind=kOutput, calls=%fused_computation.49 | convolution fusion | flops 3623878656 | bytes 8650752 | tf_op jit(solution)/shard_map/dot_general | solution.py:113
  175.1 0.2 broadcast.20.clone
  175.3 0.2 broadcast.20.clone.2
  175.7 6.0 %fusion.8 = f32[1024,768]{0,1:T(8,128)S(1)} fusion(f32[1024,768]{1,0:T(8,128)} %collective-permute-done, f32[768,768]{1,0:T(8,128)S(1)} %constant_dynamic-update-slice_fusion.8), kind=kOutput, calls=%fused_computation.53 | convolution fusion | flops 3623878656 | bytes 8650752 | tf_op jit(solution)/shard_map/dot_general | solution.py:123
  181.8 6.1 %fusion.2 = f32[1024,1,768]{0,2,1:T(8,128)S(1)} fusion(f32[1024,768]{0,1:T(8,128)S(1)} %fusion.8, f32[768,1024]{1,0:T(8,128)S(1)} %fusion.4, f32[1024,768]{1,0:T(8,128)} %collective-permute-done.1, f32[768,768]{1,0:T(8,128)S(1)} %constant_dynamic-update-slice_fusion), kind=kOutput, calls=%fused_computation.4 | convolution fusion | flops 3626237952 | bytes 14942208 | tf_op jit(solution)/shard_map/dot_general | solution.py:125
  187.9 5.3 %copy.8 = f32[1024,1,768]{2,1,0:T(1,128)} copy(f32[1024,1,768]{0,2,1:T(8,128)S(1)} %fusion.2) | data formatting | bytes 6291456 | tf_op jit(solution)/shard_map/reshape | solution.py:128
  (70 shorter events, 2.6 us)
Async XLA Ops:
  0.0 14.6 %copy-start = (f32[1024,1,768]{2,1,0:T(1,128)S(1)}, f32[1024,1,768]{2,1,0:T(1,128)}, u32[]{:S(2)}) copy-start(f32[1024,1,768]{2,1,0:T(1,128)} %param.5) | copy-start | bytes 9437188
  13.2 8.8 %collective-permute-start.2 = (f32[384,768]{1,0:T(8,128)}, f32[384,768]{1,0:T(8,128)}, u32[]{:S(2)}, u32[]{:S(2)}) collective-permute-start(f32[384,768]{1,0:T(8,128)} %constant_dynamic-slice_fusion.6), channel_id=1, source_target_pairs={{0,1},{1,0},{2,3},{3,2},{4,5},{5,4},{6,7},{7,6},{8,9},{9,8},{10,11... | collective-permute-start | bytes 3538952 | tf_op jit(solution)/shard_map/ppermute | solution.py:72
  16.5 81.8 %collective-permute-start = (f32[1024,768]{1,0:T(8,128)}, f32[1024,768]{1,0:T(8,128)}, u32[]{:S(2)}, u32[]{:S(2)}) collective-permute-start(f32[1024,768]{1,0:T(8,128)} %bitcast.36), channel_id=1, source_target_pairs={{0,112},{16,0},{32,16},{48,32},{64,48},{80,64},{96,80},{112,96},{1... | collective-permute-start | bytes 9437192 | tf_op jit(solution)/shard_map/ppermute | solution.py:14
  20.7 77.6 %collective-permute-start.1 = (f32[1024,768]{1,0:T(8,128)}, f32[1024,768]{1,0:T(8,128)}, u32[]{:S(2)}, u32[]{:S(2)}) collective-permute-start(f32[1024,768]{1,0:T(8,128)} %bitcast.36), channel_id=1, source_target_pairs={{0,16},{16,32},{32,48},{48,64},{64,80},{80,96},{96,112},{112,0},{1... | collective-permute-start | bytes 9437192 | tf_op jit(solution)/shard_map/ppermute | solution.py:14
  24.8 18.1 %copy-start.3 = (s32[16]{0:T(128)S(1)}, s32[16]{0:T(128)}, u32[]{:S(2)}) copy-start(s32[16]{0:T(128)} %constant.68.clone) | copy-start | bytes 196
  24.8 19.5 %copy-start.2 = (f32[8]{0:T(128)S(1)}, f32[8]{0:T(128)}, u32[]{:S(2)}) copy-start(f32[8]{0:T(128)} %param.6) | copy-start | bytes 100
  24.8 27.1 %copy-start.1 = (f32[768]{0:T(1024)S(1)}, f32[768]{0:T(1024)}, u32[]{:S(2)}) copy-start(f32[768]{0:T(1024)} %param.7) | copy-start | bytes 9220
  26.8 10.6 %collective-permute-start.3 = (f32[192,768]{1,0:T(8,128)}, f32[192,768]{1,0:T(8,128)}, u32[]{:S(2)}, u32[]{:S(2)}) collective-permute-start(f32[192,768]{1,0:T(8,128)} %constant_dynamic-slice_fusion.5), channel_id=1, source_target_pairs={{0,2},{1,7},{2,0},{3,5},{4,6},{5,3},{6,4},{7,1},{8,10},{9,15},{10,... | collective-permute-start | bytes 1769480 | tf_op jit(solution)/shard_map/ppermute | solution.py:72
  41.2 6.2 %collective-permute-start.4 = (f32[96,768]{1,0:T(8,128)}, f32[96,768]{1,0:T(8,128)S(1)}, u32[]{:S(2)}, u32[]{:S(2)}) collective-permute-start(f32[96,768]{1,0:T(8,128)} %constant_dynamic-slice_fusion.4), channel_id=1, source_target_pairs={{0,6},{1,3},{2,4},{3,1},{4,2},{5,7},{6,0},{7,5},{8,14},{9,11},{10,... | collective-permute-start | bytes 884744 | tf_op jit(solution)/shard_map/ppermute | solution.py:72
  48.4 49.8 %collective-permute-start.5 = (f32[48,768]{1,0:T(8,128)S(1)}, f32[48,768]{1,0:T(8,128)S(1)}, u32[]{:S(2)}, u32[]{:S(2)}) collective-permute-start(f32[48,768]{1,0:T(8,128)S(1)} %constant_dynamic-slice_fusion.3), channel_id=1, source_target_pairs={{0,8},{1,9},{2,10},{3,11},{4,12},{5,13},{6,14},{7,15},{8,0},{9,1},... | collective-permute-start | bytes 442376 | tf_op jit(solution)/shard_map/ppermute | solution.py:72
  105.0 3.0 %collective-permute-start.10 = (f32[384,768]{1,0:T(8,128)S(1)}, f32[384,768]{1,0:T(8,128)S(1)}, u32[]{:S(2)}, u32[]{:S(2)}) collective-permute-start(f32[384,768]{1,0:T(8,128)S(1)} %dynamic-slice_bitcast_fusion), channel_id=1, source_target_pairs={{0,1},{1,0},{2,3},{3,2},{4,5},{5,4},{6,7},{7,6},{8,9},{9,8},{10,11... | collective-permute-start | bytes 3538952 | tf_op jit(solution)/shard_map/ppermute | solution.py:72
  108.2 10.0 %collective-permute-start.11 = (f32[192,768]{1,0:T(8,128)S(1)}, f32[192,768]{1,0:T(8,128)S(1)}, u32[]{:S(2)}, u32[]{:S(2)}) collective-permute-start(f32[192,768]{1,0:T(8,128)S(1)} %constant_dynamic-slice_fusion.2), channel_id=1, source_target_pairs={{0,2},{1,7},{2,0},{3,5},{4,6},{5,3},{6,4},{7,1},{8,10},{9,15},{10,... | collective-permute-start | bytes 1769480 | tf_op jit(solution)/shard_map/ppermute | solution.py:72
  110.8 8.0 %collective-permute-start.6 = (f32[48,768]{1,0:T(8,128)S(1)}, f32[48,768]{1,0:T(8,128)S(1)}, u32[]{:S(2)}, u32[]{:S(2)}) collective-permute-start(f32[48,768]{1,0:T(8,128)S(1)} %add_divide_fusion.1), channel_id=1, source_target_pairs={{0,8},{1,9},{2,10},{3,11},{4,12},{5,13},{6,14},{7,15},{8,0},{9,1},... | collective-permute-start | bytes 442376 | tf_op jit(solution)/shard_map/ppermute | solution.py:80
  118.3 5.9 %collective-permute-start.12 = (f32[96,768]{1,0:T(8,128)S(1)}, f32[96,768]{1,0:T(8,128)S(1)}, u32[]{:S(2)}, u32[]{:S(2)}) collective-permute-start(f32[96,768]{1,0:T(8,128)S(1)} %constant_dynamic-slice_fusion.1), channel_id=1, source_target_pairs={{0,6},{1,3},{2,4},{3,1},{4,2},{5,7},{6,0},{7,5},{8,14},{9,11},{10,... | collective-permute-start | bytes 884744 | tf_op jit(solution)/shard_map/ppermute | solution.py:72
  118.8 8.6 %collective-permute-start.7 = (f32[96,768]{1,0:T(8,128)S(1)}, f32[96,768]{1,0:T(8,128)S(1)}, u32[]{:S(2)}, u32[]{:S(2)}) collective-permute-start(f32[96,768]{1,0:T(8,128)S(1)} %constant_dynamic-update-slice_fusion.22), channel_id=1, source_target_pairs={{0,6},{1,3},{2,4},{3,1},{4,2},{5,7},{6,0},{7,5},{8,14},{9,11},{10,... | collective-permute-start | bytes 884744 | tf_op jit(solution)/shard_map/ppermute | solution.py:80
  124.4 5.7 %collective-permute-start.13 = (f32[48,768]{1,0:T(8,128)S(1)}, f32[48,768]{1,0:T(8,128)S(1)}, u32[]{:S(2)}, u32[]{:S(2)}) collective-permute-start(f32[48,768]{1,0:T(8,128)S(1)} %constant_dynamic-slice_fusion), channel_id=1, source_target_pairs={{0,8},{1,9},{2,10},{3,11},{4,12},{5,13},{6,14},{7,15},{8,0},{9,1},... | collective-permute-start | bytes 442376 | tf_op jit(solution)/shard_map/ppermute | solution.py:72
  127.5 10.0 %collective-permute-start.8 = (f32[192,768]{1,0:T(8,128)S(1)}, f32[192,768]{1,0:T(8,128)S(1)}, u32[]{:S(2)}, u32[]{:S(2)}) collective-permute-start(f32[192,768]{1,0:T(8,128)S(1)} %constant_dynamic-update-slice_fusion.20), channel_id=1, source_target_pairs={{0,2},{1,7},{2,0},{3,5},{4,6},{5,3},{6,4},{7,1},{8,10},{9,15},{10,... | collective-permute-start | bytes 1769480 | tf_op jit(solution)/shard_map/ppermute | solution.py:80
  130.2 5.6 %collective-permute-start.14 = (f32[48,768]{1,0:T(8,128)S(1)}, f32[48,768]{1,0:T(8,128)S(1)}, u32[]{:S(2)}, u32[]{:S(2)}) collective-permute-start(f32[48,768]{1,0:T(8,128)S(1)} %get-tuple-element.12), channel_id=1, source_target_pairs={{0,8},{1,9},{2,10},{3,11},{4,12},{5,13},{6,14},{7,15},{8,0},{9,1},... | collective-permute-start | bytes 442376 | tf_op jit(solution)/shard_map/ppermute | solution.py:80
  130.4 14.2 %collective-permute-start.18 = (f32[48,768]{1,0:T(8,128)S(1)}, f32[48,768]{1,0:T(8,128)S(1)}, u32[]{:S(2)}, u32[]{:S(2)}) collective-permute-start(f32[48,768]{1,0:T(8,128)S(1)} %get-tuple-element.12), channel_id=1, source_target_pairs={{0,16},{16,32},{32,48},{48,64},{64,80},{80,96},{96,112},{112,0},{1... | collective-permute-start | bytes 442376 | tf_op jit(solution)/shard_map/ppermute | solution.py:14
  135.8 9.0 %collective-permute-start.15 = (f32[96,768]{1,0:T(8,128)S(1)}, f32[96,768]{1,0:T(8,128)S(1)}, u32[]{:S(2)}, u32[]{:S(2)}) collective-permute-start(f32[96,768]{1,0:T(8,128)S(1)} %constant_dynamic-update-slice_fusion.14), channel_id=1, source_target_pairs={{0,6},{1,3},{2,4},{3,1},{4,2},{5,7},{6,0},{7,5},{8,14},{9,11},{10,... | collective-permute-start | bytes 884744 | tf_op jit(solution)/shard_map/ppermute | solution.py:80
  137.6 27.1 %collective-permute-start.9 = (f32[384,768]{1,0:T(8,128)S(1)}, f32[384,768]{1,0:T(8,128)S(1)}, u32[]{:S(2)}, u32[]{:S(2)}) collective-permute-start(f32[384,768]{1,0:T(8,128)S(1)} %constant_dynamic-update-slice_fusion.18), channel_id=1, source_target_pairs={{0,1},{1,0},{2,3},{3,2},{4,5},{5,4},{6,7},{7,6},{8,9},{9,8},{10,11... | collective-permute-start | bytes 3538952 | tf_op jit(solution)/shard_map/ppermute | solution.py:80
  144.7 7.0 %collective-permute-start.19 = (f32[48,768]{1,0:T(8,128)S(1)}, f32[48,768]{1,0:T(8,128)S(1)}, u32[]{:S(2)}, u32[]{:S(2)}) collective-permute-start(f32[48,768]{1,0:T(8,128)S(1)} %collective-permute-done.18), channel_id=1, source_target_pairs={{0,8},{1,9},{2,10},{3,11},{4,12},{5,13},{6,14},{7,15},{8,0},{9,1},... | collective-permute-start | bytes 442376 | tf_op jit(solution)/shard_map/ppermute | solution.py:80
  144.8 16.1 %collective-permute-start.16 = (f32[192,768]{1,0:T(8,128)S(1)}, f32[192,768]{1,0:T(8,128)S(1)}, u32[]{:S(2)}, u32[]{:S(2)}) collective-permute-start(f32[192,768]{1,0:T(8,128)S(1)} %constant_dynamic-update-slice_fusion.12), channel_id=1, source_target_pairs={{0,2},{1,7},{2,0},{3,5},{4,6},{5,3},{6,4},{7,1},{8,10},{9,15},{10,... | collective-permute-start | bytes 1769480 | tf_op jit(solution)/shard_map/ppermute | solution.py:80
  151.6 9.0 %collective-permute-start.20 = (f32[96,768]{1,0:T(8,128)S(1)}, f32[96,768]{1,0:T(8,128)S(1)}, u32[]{:S(2)}, u32[]{:S(2)}) collective-permute-start(f32[96,768]{1,0:T(8,128)S(1)} %constant_dynamic-update-slice_fusion.6), channel_id=1, source_target_pairs={{0,6},{1,3},{2,4},{3,1},{4,2},{5,7},{6,0},{7,5},{8,14},{9,11},{10,... | collective-permute-start | bytes 884744 | tf_op jit(solution)/shard_map/ppermute | solution.py:80
  160.7 10.0 %collective-permute-start.21 = (f32[192,768]{1,0:T(8,128)S(1)}, f32[192,768]{1,0:T(8,128)S(1)}, u32[]{:S(2)}, u32[]{:S(2)}) collective-permute-start(f32[192,768]{1,0:T(8,128)S(1)} %constant_dynamic-update-slice_fusion.4), channel_id=1, source_target_pairs={{0,2},{1,7},{2,0},{3,5},{4,6},{5,3},{6,4},{7,1},{8,10},{9,15},{10,... | collective-permute-start | bytes 1769480 | tf_op jit(solution)/shard_map/ppermute | solution.py:80
  161.0 14.6 %collective-permute-start.17 = (f32[384,768]{1,0:T(8,128)S(1)}, f32[384,768]{1,0:T(8,128)S(1)}, u32[]{:S(2)}, u32[]{:S(2)}) collective-permute-start(f32[384,768]{1,0:T(8,128)S(1)} %constant_dynamic-update-slice_fusion.10), channel_id=1, source_target_pairs={{0,1},{1,0},{2,3},{3,2},{4,5},{5,4},{6,7},{7,6},{8,9},{9,8},{10,11... | collective-permute-start | bytes 3538952 | tf_op jit(solution)/shard_map/ppermute | solution.py:80
  170.8 10.9 %collective-permute-start.22 = (f32[384,768]{1,0:T(8,128)S(1)}, f32[384,768]{1,0:T(8,128)S(1)}, u32[]{:S(2)}, u32[]{:S(2)}) collective-permute-start(f32[384,768]{1,0:T(8,128)S(1)} %constant_dynamic-update-slice_fusion.2), channel_id=1, source_target_pairs={{0,1},{1,0},{2,3},{3,2},{4,5},{5,4},{6,7},{7,6},{8,9},{9,8},{10,11... | collective-permute-start | bytes 3538952 | tf_op jit(solution)/shard_map/ppermute | solution.py:80

commit v2 on v0

--- a/solution.py
+++ b/solution.py
@@ -63,25 +63,16 @@
     return [bits[s] for s in range(len(stages))], jnp.asarray(np.array(share, np.int32))[idx]
 
 
-def reduce_scatter_rows(value, stages, bits):
-    for stage, bit in zip(stages, bits):
-        half = value.shape[0] // 2
-        pairs = [(i, j) for i, (j, _) in enumerate(stage)]
-        keep = lax.dynamic_slice_in_dim(value, bit * half, half, 0)
-        send = lax.dynamic_slice_in_dim(value, (1 - bit) * half, half, 0)
-        value = keep + lax.ppermute(send, "aux", pairs)
-    return value
+def reduce_scatter_a2a(value, count):
+    chunks = value.reshape((count, value.shape[0] // count) + value.shape[1:])
+    got = lax.all_to_all(chunks, "aux", 0, 0, tiled=False)
+    return got.sum(axis=0)
 
 
-def all_gather_rows(value, stages, bits):
-    for stage, bit in reversed(list(zip(stages, bits))):
-        rows = value.shape[0]
-        pairs = [(i, j) for i, (j, _) in enumerate(stage)]
-        got = lax.ppermute(value, "aux", pairs)
-        out = jnp.zeros((2 * rows,) + value.shape[1:], value.dtype)
-        out = lax.dynamic_update_slice_in_dim(out, value, bit * rows, 0)
-        value = lax.dynamic_update_slice_in_dim(out, got, (1 - bit) * rows, 0)
-    return value
+def all_gather_a2a(value, count):
+    tiles = jnp.broadcast_to(value[None], (count,) + value.shape)
+    got = lax.all_to_all(tiles, "aux", 0, 0, tiled=False)
+    return got.reshape((count * value.shape[0],) + value.shape[1:])
 
 
 def body(factors, eps_occ, eps_vir):
@@ -91,7 +82,8 @@
     groups = lax.axis_size("occ")
     aux_count = lax.axis_size("aux")
     stages, share = aux_stages(aux_count)
-    bits, my_share = keep_bits(stages, share)
+    _, my_share = keep_bits(stages, share)
+    my_share = lax.axis_index("aux")
     rows = width // aux_count
 
     own = factors.reshape(aux_dev, width)
@@ -106,20 +98,20 @@
     contract_b = (((1,), (1,)), ((), ()))
     diag = lax.dot_general(own, own, contract_p, precision=PREC,
                            preferred_element_type=jnp.float32)
-    diag_share = reduce_scatter_rows(diag, stages, bits)
+    diag_share = reduce_scatter_a2a(diag, aux_count)
     diag_amp = diag_share / (my_vals[:, None] + own_vals[None, :])
-    diag_full = all_gather_rows(diag_amp, stages, bits)
+    above, below, diag_amp = lax.optimization_barrier((above, below, diag_amp))
+    diag_full = all_gather_a2a(diag_amp, aux_count)
     t_own = lax.dot_general(own, diag_full, contract_b, precision=PREC,
                             preferred_element_type=jnp.float32)
-    above, below, t_own = lax.optimization_barrier((above, below, t_own))
 
     up = lax.dot_general(own, above, contract_p, precision=PREC,
                          preferred_element_type=jnp.float32)
-    up_share = reduce_scatter_rows(up, stages, bits)
+    up_share = reduce_scatter_a2a(up, aux_count)
     up_amp = up_share / (my_vals[:, None] + up_vals[None, :])
     prev_amp = passed_along(up_amp, "occ", 1)
-    up_full = all_gather_rows(up_amp, stages, bits)
-    prev_full = all_gather_rows(prev_amp, stages, bits)
+    up_full = all_gather_a2a(up_amp, aux_count)
+    prev_full = all_gather_a2a(prev_amp, aux_count)
     t_up = lax.dot_general(above, up_full, contract_b, precision=PREC,
                            preferred_element_type=jnp.float32)
     t_prev = lax.dot_general(below, prev_full, (((1,), (0,)), ((), ())),

time: 233 us -> 287 us (1.23)
  blocking collectives: 0 us -> 35.8 us
  waiting for transfers between devices: 127 us -> 154 us
  starting transfers between devices: 50.9 us -> 29.8 us
  matrix products: 24.5 us -> 34.4 us
  local copies, waits for them, and re-layouts: 17.3 us -> 26.8 us
  between operations: 6.64 us -> 0.09 us
    all_to_all x0 -> x4, waiting for transfers between devices: none -> 144 us  [the longest x1 72.7 us: reduce_scatter_a2a(): got = lax.all_to_all(chunks, 'aux', 0, 0, tiled=False)]
    ppermute x20 -> x0, waiting for transfers between devices: 127 us -> none  [the longest x8 93.3 us: reduce_scatter_rows(): value = keep + lax.ppermute(send, 'aux', pairs)]
    ppermute x20 -> x0, starting transfers between devices: 46.6 us -> none  [the longest x12 35.9 us: all_gather_rows(): got = lax.ppermute(value, 'aux', pairs)]
    all_to_all x0 -> x1, blocking collectives: none -> 35.8 us  [reduce_scatter_a2a(): got = lax.all_to_all(chunks, 'aux', 0, 0, tiled=False)]
    all_to_all x0 -> x4, starting transfers between devices: none -> 24.9 us  [the longest x3 16.4 us: all_gather_a2a(): got = lax.all_to_all(tiles, 'aux', 0, 0, tiled=False)]
    ppermute x3, waiting for transfers between devices: 0.07 us -> 10.5 us  [passed_along(): return lax.ppermute(value, axis, pairs)]
    unnamed x14 -> x13, local copies, waits for them, and re-layouts: 5.49 us -> 12.6 us
    broadcast_in_dim x0 -> x3, local copies, waits for them, and re-layouts: none -> 5.03 us  [all_gather_a2a(): tiles = jnp.broadcast_to(value[None], (count,) + value.shape)]
  transfers between devices with their start and end apart: 23 -> 7, of which waited for: 15 -> 5; matrix products, arithmetic and copies ran while one was open for 7% -> 13% of each run, Pallas kernels for 0% -> 0%
where the time goes in v2:
time: 287 us; the launch traced here: 286 us
  waiting for transfers between devices  154 us (54%)
  blocking collectives  35.8 us (12%)
  matrix products  34.4 us (12%)
  starting transfers between devices  29.8 us (10%)
  local copies, waits for them, and re-layouts  26.8 us (9%)
  other arithmetic  4.96 us (2%)
    all_to_all x1, waiting for transfers between devices, reduce_scatter_a2a(): got = lax.all_to_all(chunks, 'aux', 0, 0, tiled=False)  72.7 us
    all_to_all x3, waiting for transfers between devices, all_gather_a2a(): got = lax.all_to_all(tiles, 'aux', 0, 0, tiled=False)  70.9 us
    all_to_all x1, blocking collectives, reduce_scatter_a2a(): got = lax.all_to_all(chunks, 'aux', 0, 0, tiled=False)  35.8 us
    all_to_all x3, starting transfers between devices, all_gather_a2a(): got = lax.all_to_all(tiles, 'aux', 0, 0, tiled=False)  16.4 us
    unnamed x13, local copies, waits for them, and re-layouts  12.6 us
    ppermute x3, waiting for transfers between devices, passed_along(): return lax.ppermute(value, axis, pairs)  10.5 us
    all_to_all x1, starting transfers between devices, reduce_scatter_a2a(): got = lax.all_to_all(chunks, 'aux', 0, 0, tiled=False)  8.48 us
    reshape x1, local copies, waits for them, and re-layouts, body(): return (1.3 * total).reshape(aux_dev, occ_dev, virt)  8.45 us
  transfers between devices with their start and end apart: 7, of which 5 were waited for; matrix products, arithmetic and copies ran while one was open for 13% of the time, Pallas kernels for 0%

profile of v2, /device:TPU:1, one launch (start us, length us, event | category | flops | bytes accessed | tf_op | source)
XLA Modules:
  0.0 285.9 jit_solution(6400180318648852275)
XLA Ops:
  0.0 2.1 collective-permute-start.1
  2.1 2.8 collective-permute-start
  4.9 6.8 %copy.8 = f32[1024,1,768]{0,2,1:T(8,128)S(1)} copy(f32[1024,1,768]{2,1,0:T(1,128)} %param.3) | data formatting | bytes 6291456 | tf_op args[0]
  11.7 7.3 %fusion.3 = f32[16,48,768]{2,1,0:T(8,128)} fusion(f32[16,48,1024]{2,1,0:T(8,128)S(1)} %bitcast.44, f32[1024,1,768]{2,1,0:T(1,128)} %param.3), kind=kOutput, calls=%fused_computation.6 | convolution fusion | flops 3623878656 | bytes 8650752 | tf_op jit(solution)/shard_map/dot_general | solution.py:99
  19.0 0.0 copy-start.4
  19.0 0.0 copy-start.3
  19.0 8.5 %all-to-all-start = ((f32[16,48,768]{2,1,0:T(8,128)}), f32[16,48,768]{2,1,0:T(8,128)}, u32[]{:S(2)}, u32[]{:S(2)}) async-start(f32[16,48,768]{2,1,0:T(8,128)} %fusion.3), calls=%async_computation | async-start | bytes 4718592 | tf_op jit(solution)/shard_map/all_to_all | solution.py:68
  27.5 0.0 copy-done.4
  27.5 0.6 fusion.10
  28.1 0.0 copy-done.3
  28.1 1.2 broadcast_subtract_fusion
  29.3 0.1 add.54
  29.4 72.7 %all-to-all-done = f32[16,48,768]{2,1,0:T(8,128)} async-done(((f32[16,48,768]{2,1,0:T(8,128)}), f32[16,48,768]{2,1,0:T(8,128)}, u32[]{:S(2)}, u32[]{:S(2)}) %all-to-all-start) | async-done | bytes 2359328 | tf_op jit(solution)/shard_map/all_to_all | solution.py:68
  102.1 1.8 reduce_sum.18
  103.9 0.1 add_divide_fusion.1
  104.0 0.0 collective-permute-done.1
  104.0 3.7 %copy.25 = f32[1024,1,768]{2,0,1:T(8,128)} copy(f32[1024,1,768]{2,1,0:T(1,128)} %collective-permute-done.1) | data formatting | bytes 6291456
  107.7 0.0 collective-permute-done
  107.7 2.1 copy.26
  109.8 0.0 copy-start
  109.8 4.3 %fusion.6 = f32[768,768]{0,1:T(8,128)S(1)} fusion(f32[1024,768]{1,0:T(8,128)S(1)} %bitcast.45, f32[1024,1,768]{0,2,1:T(8,128)S(1)} %copy.8), kind=kOutput, calls=%fused_computation.9 | convolution fusion | flops 3623878656 | bytes 8650752 | tf_op jit(solution)/shard_map/dot_general | solution.py:108
  114.1 0.0 copy-done
  114.1 35.8 %all_to_all.25 = f32[16,48,768]{2,1,0:T(8,128)} all-to-all(f32[16,48,768]{2,1,0:T(8,128)S(1)} %bitcast.48), channel_id=1, replica_groups=mesh['occ'=8,'aux'=16] {'aux'}, dimensions={0} | all-to-all | bytes 4718592 | tf_op jit(solution)/shard_map/all_to_all | solution.py:68
  149.9 1.7 broadcast_in_dim.6
  151.6 4.9 %all-to-all-start.1 = ((f32[16,48,768]{2,1,0:T(8,128)}), f32[16,48,768]{2,1,0:T(8,128)}, u32[]{:S(2)}, u32[]{:S(2)}) async-start(f32[16,48,768]{2,1,0:T(8,128)} %broadcast_in_dim.6), calls=%async_computation.1 | async-start | bytes 4718592 | tf_op jit(solution)/shard_map/all_to_all | solution.py:74
  156.5 1.8 reduce_sum.19
  158.3 0.1 add_divide_fusion
  158.4 29.6 %all-to-all-done.1 = f32[16,48,768]{2,1,0:T(8,128)} async-done(((f32[16,48,768]{2,1,0:T(8,128)}), f32[16,48,768]{2,1,0:T(8,128)}, u32[]{:S(2)}, u32[]{:S(2)}) %all-to-all-start.1) | async-done | bytes 2359328 | tf_op jit(solution)/shard_map/all_to_all | solution.py:74
  188.1 1.7 broadcast_in_dim.7
  189.8 6.0 %all-to-all-start.3 = ((f32[16,48,768]{2,1,0:T(8,128)}), f32[16,48,768]{2,1,0:T(8,128)}, u32[]{:S(2)}, u32[]{:S(2)}) async-start(f32[16,48,768]{2,1,0:T(8,128)} %broadcast_in_dim.7), calls=%async_computation.3 | async-start | bytes 4718592 | tf_op jit(solution)/shard_map/all_to_all | solution.py:74
  195.8 0.0 collective-permute-start.2
  195.8 10.5 %collective-permute-done.2 = f32[48,768]{1,0:T(8,128)S(1)} collective-permute-done((f32[48,768]{1,0:T(8,128)S(1)}, f32[48,768]{1,0:T(8,128)S(1)}, u32[]{:S(2)}, u32[]{:S(2)}) %collective-permute-start.2) | collective-permute-done | bytes 147488 | tf_op jit(solution)/shard_map/ppermute | solution.py:14
  206.3 24.6 %all-to-all-done.3 = f32[16,48,768]{2,1,0:T(8,128)} async-done(((f32[16,48,768]{2,1,0:T(8,128)}), f32[16,48,768]{2,1,0:T(8,128)}, u32[]{:S(2)}, u32[]{:S(2)}) %all-to-all-start.3) | async-done | bytes 2359328 | tf_op jit(solution)/shard_map/all_to_all | solution.py:74
  230.9 1.6 broadcast_in_dim.8
  232.5 5.5 %all-to-all-start.4 = ((f32[16,48,768]{2,1,0:T(8,128)}), f32[16,48,768]{2,1,0:T(8,128)}, u32[]{:S(2)}, u32[]{:S(2)}) async-start(f32[16,48,768]{2,1,0:T(8,128)} %broadcast_in_dim.8), calls=%async_computation.4 | async-start | bytes 4718592 | tf_op jit(solution)/shard_map/all_to_all | solution.py:74
  238.0 0.0 copy-start.1
  238.0 7.4 %fusion.8 = f32[768,1024]{1,0:T(8,128)} fusion(f32[768,768]{1,0:T(8,128)} %bitcast.6, f32[1024,1,768]{0,2,1:T(8,128)S(1)} %copy.8), kind=kOutput, calls=%fused_computation.11 | convolution fusion | flops 3623878656 | bytes 8650752 | tf_op jit(solution)/shard_map/dot_general | solution.py:105
  245.4 0.0 copy-done.1
  245.4 0.0 copy-start.2
  245.4 7.4 %fusion.11 = f32[1024,768]{0,1:T(8,128)} fusion(f32[1024,768]{1,0:T(8,128)S(1)} %bitcast.46, f32[768,768]{1,0:T(8,128)} %bitcast.11), kind=kOutput, calls=%fused_computation.18 | convolution fusion | flops 3623878656 | bytes 8650752 | tf_op jit(solution)/shard_map/dot_general | solution.py:115
  252.8 16.7 %all-to-all-done.4 = f32[16,48,768]{2,1,0:T(8,128)} async-done(((f32[16,48,768]{2,1,0:T(8,128)}), f32[16,48,768]{2,1,0:T(8,128)}, u32[]{:S(2)}, u32[]{:S(2)}) %all-to-all-start.4) | async-done | bytes 2359328 | tf_op jit(solution)/shard_map/all_to_all | solution.py:74
  269.4 0.0 copy-done.2
  269.4 8.1 %fusion.2 = f32[1024,1,768]{0,2,1:T(8,128)} fusion(f32[1024,768]{0,1:T(8,128)} %fusion.11, f32[768,1024]{1,0:T(8,128)} %fusion.8, f32[1024,768]{1,0:T(8,128)S(1)} %bitcast.47, f32[768,768]{1,0:T(8,128)} %bitcast.12), kind=kOutput, calls=%fused_computation.5 | convolution fusion | flops 3626237952 | bytes 14942208 | tf_op jit(solution)/shard_map/dot_general | solution.py:117
  277.5 8.4 %copy.12 = f32[1024,1,768]{2,1,0:T(1,128)} copy(f32[1024,1,768]{0,2,1:T(8,128)} %fusion.2) | data formatting | bytes 6291456 | tf_op jit(solution)/shard_map/reshape | solution.py:120
Async XLA Ops:
  0.0 104.0 %collective-permute-start.1 = (f32[1024,1,768]{2,1,0:T(1,128)}, f32[1024,1,768]{2,1,0:T(1,128)}, u32[]{:S(2)}, u32[]{:S(2)}) collective-permute-start(f32[1024,1,768]{2,1,0:T(1,128)} %param.3), channel_id=1, source_target_pairs={{0,16},{16,32},{32,48},{48,64},{64,80},{80,96},{96,112},{112,0},{1... | collective-permute-start | bytes 9437192 | tf_op jit(solution)/shard_map/ppermute | solution.py:14
  2.1 105.6 %collective-permute-start = (f32[1024,1,768]{2,1,0:T(1,128)}, f32[1024,1,768]{2,1,0:T(1,128)}, u32[]{:S(2)}, u32[]{:S(2)}) collective-permute-start(f32[1024,1,768]{2,1,0:T(1,128)} %param.3), channel_id=1, source_target_pairs={{0,112},{16,0},{32,16},{48,32},{64,48},{80,64},{96,80},{112,96},{1... | collective-permute-start | bytes 9437192 | tf_op jit(solution)/shard_map/ppermute | solution.py:14
  19.0 8.5 %copy-start.4 = (f32[8]{0:T(128)S(1)}, f32[8]{0:T(128)}, u32[]{:S(2)}) copy-start(f32[8]{0:T(128)} %param.4) | copy-start | bytes 100
  19.0 9.1 %copy-start.3 = (f32[768]{0:T(1024)S(1)}, f32[768]{0:T(1024)}, u32[]{:S(2)}) copy-start(f32[768]{0:T(1024)} %param.5) | copy-start | bytes 9220
  19.0 83.0 %all-to-all-start = ((f32[16,48,768]{2,1,0:T(8,128)}), f32[16,48,768]{2,1,0:T(8,128)}, u32[]{:S(2)}, u32[]{:S(2)}) async-start(f32[16,48,768]{2,1,0:T(8,128)} %fusion.3), calls=%async_computation | async-start | bytes 4718592 | tf_op jit(solution)/shard_map/all_to_all | solution.py:68
  109.8 4.4 %copy-start = (f32[1024,1,768]{2,0,1:T(8,128)}, f32[1024,1,768]{2,0,1:T(8,128)S(1)}, u32[]{:S(2)}) copy-start(f32[1024,1,768]{2,0,1:T(8,128)S(1)} %copy.26) | copy-start | bytes 9437188
  151.6 36.4 %all-to-all-start.1 = ((f32[16,48,768]{2,1,0:T(8,128)}), f32[16,48,768]{2,1,0:T(8,128)}, u32[]{:S(2)}, u32[]{:S(2)}) async-start(f32[16,48,768]{2,1,0:T(8,128)} %broadcast_in_dim.6), calls=%async_computation.1 | async-start | bytes 4718592 | tf_op jit(solution)/shard_map/all_to_all | solution.py:74
  189.8 41.1 %all-to-all-start.3 = ((f32[16,48,768]{2,1,0:T(8,128)}), f32[16,48,768]{2,1,0:T(8,128)}, u32[]{:S(2)}, u32[]{:S(2)}) async-start(f32[16,48,768]{2,1,0:T(8,128)} %broadcast_in_dim.7), calls=%async_computation.3 | async-start | bytes 4718592 | tf_op jit(solution)/shard_map/all_to_all | solution.py:74
  195.8 10.5 %collective-permute-start.2 = (f32[48,768]{1,0:T(8,128)S(1)}, f32[48,768]{1,0:T(8,128)S(1)}, u32[]{:S(2)}, u32[]{:S(2)}) collective-permute-start(f32[48,768]{1,0:T(8,128)S(1)} %add_divide_fusion), channel_id=1, source_target_pairs={{0,16},{16,32},{32,48},{48,64},{64,80},{80,96},{96,112},{112,0},{1... | collective-permute-start | bytes 442376 | tf_op jit(solution)/shard_map/ppermute | solution.py:14
  232.5 36.9 %all-to-all-start.4 = ((f32[16,48,768]{2,1,0:T(8,128)}), f32[16,48,768]{2,1,0:T(8,128)}, u32[]{:S(2)}, u32[]{:S(2)}) async-start(f32[16,48,768]{2,1,0:T(8,128)} %broadcast_in_dim.8), calls=%async_computation.4 | async-start | bytes 4718592 | tf_op jit(solution)/shard_map/all_to_all | solution.py:74
  238.0 7.4 %copy-start.1 = (f32[1024,1,768]{2,0,1:T(8,128)S(1)}, f32[1024,1,768]{2,0,1:T(8,128)}, u32[]{:S(2)}) copy-start(f32[1024,1,768]{2,0,1:T(8,128)} %copy-done) | copy-start | bytes 9437188
  245.4 24.0 %copy-start.2 = (f32[1024,1,768]{2,0,1:T(8,128)S(1)}, f32[1024,1,768]{2,0,1:T(8,128)}, u32[]{:S(2)}) copy-start(f32[1024,1,768]{2,0,1:T(8,128)} %copy.25) | copy-start | bytes 9437188

commit v3 on v0

--- a/solution.py
+++ b/solution.py
@@ -63,12 +63,14 @@
     return [bits[s] for s in range(len(stages))], jnp.asarray(np.array(share, np.int32))[idx]
 
 
-def reduce_scatter_rows(value, stages, bits):
-    for stage, bit in zip(stages, bits):
+def reduce_scatter_rows(value, stages, bits, last_parts=False):
+    for n, (stage, bit) in enumerate(zip(stages, bits)):
         half = value.shape[0] // 2
         pairs = [(i, j) for i, (j, _) in enumerate(stage)]
         keep = lax.dynamic_slice_in_dim(value, bit * half, half, 0)
         send = lax.dynamic_slice_in_dim(value, (1 - bit) * half, half, 0)
+        if last_parts and n == len(stages) - 1:
+            return keep, send, pairs
         value = keep + lax.ppermute(send, "aux", pairs)
     return value
 
@@ -101,6 +103,8 @@
     own_vals = pair_values(eps_occ, eps_vir, group, occ_dev)
     up_vals = pair_values(eps_occ, eps_vir, (group + 1) % groups, occ_dev)
     my_vals = lax.dynamic_slice_in_dim(own_vals, my_share * rows, rows)
+    dn_vals = pair_values(eps_occ, eps_vir, (group + groups - 1) % groups, occ_dev)
+    my_dn_vals = lax.dynamic_slice_in_dim(dn_vals, my_share * rows, rows)
 
     contract_p = (((0,), (0,)), ((), ()))
     contract_b = (((1,), (1,)), ((), ()))
@@ -108,21 +112,24 @@
                            preferred_element_type=jnp.float32)
     diag_share = reduce_scatter_rows(diag, stages, bits)
     diag_amp = diag_share / (my_vals[:, None] + own_vals[None, :])
+    above, below, diag_amp = lax.optimization_barrier((above, below, diag_amp))
     diag_full = all_gather_rows(diag_amp, stages, bits)
     t_own = lax.dot_general(own, diag_full, contract_b, precision=PREC,
                             preferred_element_type=jnp.float32)
-    above, below, t_own = lax.optimization_barrier((above, below, t_own))
 
     up = lax.dot_general(own, above, contract_p, precision=PREC,
                          preferred_element_type=jnp.float32)
-    up_share = reduce_scatter_rows(up, stages, bits)
+    keep, send, last = reduce_scatter_rows(up, stages, bits, last_parts=True)
+    up_share = keep + lax.ppermute(send, "aux", last)
+    across = [(g * aux_count + i, ((g + 1) % groups) * aux_count + j)
+              for g in range(groups) for i, j in last]
+    prev_share = passed_along(keep, "occ", 1) + lax.ppermute(send, ("occ", "aux"), across)
     up_amp = up_share / (my_vals[:, None] + up_vals[None, :])
-    prev_amp = passed_along(up_amp, "occ", 1)
-    up_full = all_gather_rows(up_amp, stages, bits)
-    prev_full = all_gather_rows(prev_amp, stages, bits)
-    t_up = lax.dot_general(above, up_full, contract_b, precision=PREC,
+    prev_amp = prev_share / (my_dn_vals[:, None] + own_vals[None, :])
+    pair_full = all_gather_rows(jnp.stack([up_amp, prev_amp], axis=1), stages, bits)
+    t_up = lax.dot_general(above, pair_full[:, 0], contract_b, precision=PREC,
                            preferred_element_type=jnp.float32)
-    t_prev = lax.dot_general(below, prev_full, (((1,), (0,)), ((), ())),
+    t_prev = lax.dot_general(below, pair_full[:, 1], (((1,), (0,)), ((), ())),
                              precision=PREC, preferred_element_type=jnp.float32)
     total = t_own + t_up + t_prev
     return (1.3 * total).reshape(aux_dev, occ_dev, virt)

time: 233 us -> 216 us (0.927)
  waiting for transfers between devices: 127 us -> 111 us
  starting transfers between devices: 50.9 us -> 43.3 us
  local copies, waits for them, and re-layouts: 17.3 us -> 20.6 us
    ppermute x8 -> x7, waiting for transfers between devices: 93.3 us -> 68.9 us  [reduce_scatter_rows(): value = keep + lax.ppermute(send, 'aux', pairs)]
    ppermute x12 -> x8, starting transfers between devices: 35.9 us -> 28 us  [all_gather_rows(): got = lax.ppermute(value, 'aux', pairs)]
    ppermute x0 -> x2, waiting for transfers between devices: none -> 7.67 us  [the longest x1 5.4 us: body(): up_share = keep + lax.ppermute(send, 'aux', last)]
    dynamic_slice x8, local copies, waits for them, and re-layouts: 1.84 us -> 6.33 us  [reduce_scatter_rows(): send = lax.dynamic_slice_in_dim(value, (1 - bit) * half, half, 0)]
    ppermute x3, waiting for transfers between devices: 0.07 us -> 3.96 us  [passed_along(): return lax.ppermute(value, axis, pairs)]
    ppermute x12 -> x8, waiting for transfers between devices: 33.4 us -> 30.7 us  [all_gather_rows(): got = lax.ppermute(value, 'aux', pairs)]
    unnamed x14 -> x10, local copies, waits for them, and re-layouts: 5.49 us -> 4.2 us
    ppermute x8 -> x7, starting transfers between devices: 10.7 us -> 10.9 us  [reduce_scatter_rows(): value = keep + lax.ppermute(send, 'aux', pairs)]
  transfers between devices with their start and end apart: 23 -> 20, of which waited for: 15 -> 15; matrix products, arithmetic and copies ran while one was open for 7% -> 10% of each run, Pallas kernels for 0% -> 0%
where the time goes in v3:
time: 216 us; the launch traced here: 215 us
  waiting for transfers between devices  111 us (51%)
  starting transfers between devices  43.3 us (20%)
  matrix products  26 us (12%)
  local copies, waits for them, and re-layouts  20.6 us (10%)
  other arithmetic  8.53 us (4%)
  between operations  5.76 us (3%)
    ppermute x7, waiting for transfers between devices, reduce_scatter_rows(): value = keep + lax.ppermute(send, 'aux', pairs)  68.9 us
    ppermute x8, waiting for transfers between devices, all_gather_rows(): got = lax.ppermute(value, 'aux', pairs)  30.7 us
    ppermute x8, starting transfers between devices, all_gather_rows(): got = lax.ppermute(value, 'aux', pairs)  28 us
    ppermute x7, starting transfers between devices, reduce_scatter_rows(): value = keep + lax.ppermute(send, 'aux', pairs)  10.9 us
    dot_general x1, matrix products, body(): lax.dot_general(own, own, contract_p, precision=PREC, preferred_element_t...  8.79 us
    dynamic_slice x8, local copies, waits for them, and re-layouts, reduce_scatter_rows(): send = lax.dynamic_slice_in_dim(value, (1 - bit) * half, half, 0)  6.33 us
    add x6, other arithmetic, reduce_scatter_rows(): value = keep + lax.ppermute(send, 'aux', pairs)  6.27 us
    ppermute x1, waiting for transfers between devices, body(): up_share = keep + lax.ppermute(send, 'aux', last)  5.4 us
  transfers between devices with their start and end apart: 20, of which 15 were waited for; matrix products, arithmetic and copies ran while one was open for 10% of the time, Pallas kernels for 0%

profile of v3, /device:TPU:1, one launch (start us, length us, event | category | flops | bytes accessed | tf_op | source)
XLA Modules:
  0.0 215.4 jit_solution(7113761323587829531)
XLA Ops:
  0.0 8.8 %fusion.4 = f32[768,768]{1,0:T(8,128)} fusion(f32[1024,1,768]{2,1,0:T(1,128)} %param.5), kind=kOutput, calls=%fused_computation.4 | convolution fusion | flops 3623878656 | bytes 5505024 | tf_op jit(solution)/shard_map/dot_general | solution.py:111
  8.8 0.7 constant_dynamic-slice_fusion.8
  9.5 0.6 fusion.15
  10.7 2.5 %constant_dynamic-slice_fusion.7 = f32[384,768]{1,0:T(8,128)} fusion(f32[768,768]{1,0:T(8,128)} %fusion.4, s32[]{:T(128)S(6)} %select_n.39), kind=kLoop, calls=%fused_computation.53 | loop fusion | bytes 2359300 | tf_op jit(solution)/shard_map/dynamic_slice | solution.py:71
  13.2 1.4 collective-permute-start.2
  14.6 4.2 %collective-permute-start = (f32[1024,1,768]{2,1,0:T(1,128)S(1)}, f32[1024,1,768]{2,1,0:T(1,128)}, u32[]{:S(2)}, u32[]{:S(2)}) collective-permute-start(f32[1024,1,768]{2,1,0:T(1,128)S(1)} %copy-done), channel_id=1, source_target_pairs={{0,112},{16,0},{32,16},{48,32},{64,48},{80,64},{96,80},{112,96},{1... | collective-permute-start | bytes 9437192 | tf_op jit(solution)/shard_map/ppermute | solution.py:14
  20.0 2.9 %dynamic-slice_add_fusion = f32[384,768]{1,0:T(8,128)} fusion(f32[384,768]{1,0:T(8,128)} %collective-permute-done.2, f32[768,768]{1,0:T(8,128)} %fusion.4, s32[]{:T(128)S(6)} %select_n.38), kind=kLoop, calls=%fused_computation.21 | loop fusion | flops 294912 | bytes 3538948 | tf_op jit(solution)/shard_map/add | solution.py:74
  22.9 2.0 constant_dynamic-slice_fusion.6
  24.8 2.5 %collective-permute-start.3 = (f32[192,768]{1,0:T(8,128)}, f32[192,768]{1,0:T(8,128)}, u32[]{:S(2)}, u32[]{:S(2)}) collective-permute-start(f32[192,768]{1,0:T(8,128)} %constant_dynamic-slice_fusion.6), channel_id=1, source_target_pairs={{0,2},{1,7},{2,0},{3,5},{4,6},{5,3},{6,4},{7,1},{8,10},{9,15},{10,... | collective-permute-start | bytes 1769480 | tf_op jit(solution)/shard_map/ppermute | solution.py:74
  28.5 6.9 %collective-permute-done.3 = f32[192,768]{1,0:T(8,128)} collective-permute-done((f32[192,768]{1,0:T(8,128)}, f32[192,768]{1,0:T(8,128)}, u32[]{:S(2)}, u32[]{:S(2)}) %collective-permute-start.3) | collective-permute-done | bytes 589856 | tf_op jit(solution)/shard_map/ppermute | solution.py:74
  35.4 2.1 dynamic-slice_add_fusion.2
  37.5 1.7 constant_dynamic-slice_fusion.5
  41.0 0.6 dynamic_slice.75
  42.2 0.7 fusion.14
  42.9 2.5 %collective-permute-done.4 = f32[96,768]{1,0:T(8,128)S(1)} collective-permute-done((f32[96,768]{1,0:T(8,128)}, f32[96,768]{1,0:T(8,128)S(1)}, u32[]{:S(2)}, u32[]{:S(2)}) %collective-permute-start.4) | collective-permute-done | bytes 294944 | tf_op jit(solution)/shard_map/ppermute | solution.py:74
  45.4 1.0 dynamic-slice_add_fusion.4
  46.4 3.6 %collective-permute-start.5 = (f32[48,768]{1,0:T(8,128)S(1)}, f32[48,768]{1,0:T(8,128)S(1)}, u32[]{:S(2)}, u32[]{:S(2)}) collective-permute-start(f32[48,768]{1,0:T(8,128)S(1)} %constant_dynamic-slice_fusion.4), channel_id=1, source_target_pairs={{0,8},{1,9},{2,10},{3,11},{4,12},{5,13},{6,14},{7,15},{8,0},{9,1},... | collective-permute-start | bytes 442376 | tf_op jit(solution)/shard_map/ppermute | solution.py:74
  50.0 1.9 broadcast_subtract_fusion
  52.0 44.0 %collective-permute-done.5 = f32[48,768]{1,0:T(8,128)S(1)} collective-permute-done((f32[48,768]{1,0:T(8,128)S(1)}, f32[48,768]{1,0:T(8,128)S(1)}, u32[]{:S(2)}, u32[]{:S(2)}) %collective-permute-start.5) | collective-permute-done | bytes 147488 | tf_op jit(solution)/shard_map/ppermute | solution.py:74
  96.1 2.1 copy.29
  98.2 2.1 copy.28
  100.3 4.7 %fusion = f32[768,768]{0,1:T(8,128)S(1)} fusion(f32[1024,768]{1,0:T(8,128)S(1)} %bitcast.55, f32[1024,1,768]{2,1,0:T(1,128)S(1)} %copy-done), kind=kOutput, calls=%fused_computation | convolution fusion | flops 3623878656 | bytes 8650752 | tf_op jit(solution)/shard_map/dot_general | solution.py:120
  105.2 0.6 collective-permute-start.10
  105.7 2.5 %collective-permute-done.10 = f32[384,768]{1,0:T(8,128)S(1)} collective-permute-done((f32[384,768]{1,0:T(8,128)S(1)}, f32[384,768]{1,0:T(8,128)S(1)}, u32[]{:S(2)}, u32[]{:S(2)}) %collective-permute-start.10) | collective-permute-done | bytes 1179680 | tf_op jit(solution)/shard_map/ppermute | solution.py:74
  108.4 2.6 %collective-permute-start.11 = (f32[192,768]{1,0:T(8,128)S(1)}, f32[192,768]{1,0:T(8,128)S(1)}, u32[]{:S(2)}, u32[]{:S(2)}) collective-permute-start(f32[192,768]{1,0:T(8,128)S(1)} %constant_dynamic-slice_fusion.3), channel_id=1, source_target_pairs={{0,2},{1,7},{2,0},{3,5},{4,6},{5,3},{6,4},{7,1},{8,10},{9,15},{10,... | collective-permute-start | bytes 1769480 | tf_op jit(solution)/shard_map/ppermute | solution.py:74
  111.0 7.5 %collective-permute-done.11 = f32[192,768]{1,0:T(8,128)S(1)} collective-permute-done((f32[192,768]{1,0:T(8,128)S(1)}, f32[192,768]{1,0:T(8,128)S(1)}, u32[]{:S(2)}, u32[]{:S(2)}) %collective-permute-start.11) | collective-permute-done | bytes 589856 | tf_op jit(solution)/shard_map/ppermute | solution.py:74
  118.6 0.4 collective-permute-start.12
  118.9 5.6 %collective-permute-done.12 = f32[96,768]{1,0:T(8,128)S(1)} collective-permute-done((f32[96,768]{1,0:T(8,128)S(1)}, f32[96,768]{1,0:T(8,128)S(1)}, u32[]{:S(2)}, u32[]{:S(2)}) %collective-permute-start.12) | collective-permute-done | bytes 294944 | tf_op jit(solution)/shard_map/ppermute | solution.py:74
  124.8 5.4 %collective-permute-done.13 = f32[48,768]{1,0:T(8,128)S(1)} collective-permute-done((f32[48,768]{1,0:T(8,128)S(1)}, f32[48,768]{1,0:T(8,128)S(1)}, u32[]{:S(2)}, u32[]{:S(2)}) %collective-permute-start.13) | collective-permute-done | bytes 147488 | tf_op jit(solution)/shard_map/ppermute | solution.py:123
  130.4 2.3 %collective-permute-done.15 = f32[48,768]{1,0:T(8,128)S(1)} collective-permute-done((f32[48,768]{1,0:T(8,128)S(1)}, f32[48,768]{1,0:T(8,128)S(1)}, u32[]{:S(2)}, u32[]{:S(2)}) %collective-permute-start.15) | collective-permute-done | bytes 147488 | tf_op jit(solution)/shard_map/ppermute | solution.py:126
  132.7 4.0 %collective-permute-done.14 = f32[48,768]{1,0:T(8,128)S(1)} collective-permute-done((f32[48,768]{1,0:T(8,128)S(1)}, f32[48,768]{1,0:T(8,128)S(1)}, u32[]{:S(2)}, u32[]{:S(2)}) %collective-permute-start.14) | collective-permute-done | bytes 147488 | tf_op jit(solution)/shard_map/ppermute | solution.py:14
  136.8 1.1 collective-permute-start.16
  137.9 6.1 %collective-permute-done.16 = f32[48,2,768]{2,0,1:T(8,128)S(1)} collective-permute-done((f32[48,2,768]{2,0,1:T(8,128)S(1)}, f32[48,2,768]{2,0,1:T(8,128)S(1)}, u32[]{:S(2)}, u32[]{:S(2)}) %collective-permute-start.16) | collective-permute-done | bytes 294944 | tf_op jit(solution)/shard_map/ppermute | solution.py:82
  144.3 8.5 %collective-permute-done.17 = f32[96,2,768]{2,0,1:T(8,128)S(1)} collective-permute-done((f32[96,2,768]{2,0,1:T(8,128)S(1)}, f32[96,2,768]{2,0,1:T(8,128)S(1)}, u32[]{:S(2)}, u32[]{:S(2)}) %collective-permute-start.17) | collective-permute-done | bytes 589856 | tf_op jit(solution)/shard_map/ppermute | solution.py:82
  152.9 2.6 %collective-permute-start.18 = (f32[192,2,768]{2,0,1:T(8,128)S(1)}, f32[192,2,768]{2,0,1:T(8,128)S(1)}, u32[]{:S(2)}, u32[]{:S(2)}) collective-permute-start(f32[192,2,768]{2,0,1:T(8,128)S(1)} %constant_dynamic-update-slice_fusion.4), channel_id=1, source_target_pairs={{0,2},{1,7},{2,0},{3,5},{4,6},{5,3},{6,4},{7,1},{8,10},{9,15},{10,... | collective-permute-start | bytes 3538952 | tf_op jit(solution)/shard_map/ppermute | solution.py:82
  155.5 3.3 %collective-permute-start.6 = (f32[48,768]{1,0:T(8,128)S(1)}, f32[48,768]{1,0:T(8,128)S(1)}, u32[]{:S(2)}, u32[]{:S(2)}) collective-permute-start(f32[48,768]{1,0:T(8,128)S(1)} %add_divide_fusion), channel_id=1, source_target_pairs={{0,8},{1,9},{2,10},{3,11},{4,12},{5,13},{6,14},{7,15},{8,0},{9,1},... | collective-permute-start | bytes 442376 | tf_op jit(solution)/shard_map/ppermute | solution.py:82
  158.8 2.5 %collective-permute-done.6 = f32[48,768]{1,0:T(8,128)S(1)} collective-permute-done((f32[48,768]{1,0:T(8,128)S(1)}, f32[48,768]{1,0:T(8,128)S(1)}, u32[]{:S(2)}, u32[]{:S(2)}) %collective-permute-start.6) | collective-permute-done | bytes 147488 | tf_op jit(solution)/shard_map/ppermute | solution.py:82
  161.5 5.5 %collective-permute-done.7 = f32[96,768]{1,0:T(8,128)S(1)} collective-permute-done((f32[96,768]{1,0:T(8,128)S(1)}, f32[96,768]{1,0:T(8,128)S(1)}, u32[]{:S(2)}, u32[]{:S(2)}) %collective-permute-start.7) | collective-permute-done | bytes 294944 | tf_op jit(solution)/shard_map/ppermute | solution.py:82
  167.0 0.6 collective-permute-start.8
  167.8 5.9 %collective-permute-done.18 = f32[192,2,768]{2,0,1:T(8,128)S(1)} collective-permute-done((f32[192,2,768]{2,0,1:T(8,128)S(1)}, f32[192,2,768]{2,0,1:T(8,128)S(1)}, u32[]{:S(2)}, u32[]{:S(2)}) %collective-permute-start.18) | collective-permute-done | bytes 1179680 | tf_op jit(solution)/shard_map/ppermute | solution.py:82
  173.9 10.6 %collective-permute-start.19 = (f32[384,2,768]{2,0,1:T(8,128)S(1)}, f32[384,2,768]{2,0,1:T(8,128)S(1)}, u32[]{:S(2)}, u32[]{:S(2)}) collective-permute-start(f32[384,2,768]{2,0,1:T(8,128)S(1)} %constant_dynamic-update-slice_fusion.2), channel_id=1, source_target_pairs={{0,1},{1,0},{2,3},{3,2},{4,5},{5,4},{6,7},{7,6},{8,9},{9,8},{10,11... | collective-permute-start | bytes 7077896 | tf_op jit(solution)/shard_map/ppermute | solution.py:82
  184.7 9.6 %collective-permute-start.9 = (f32[384,768]{1,0:T(8,128)S(1)}, f32[384,768]{1,0:T(8,128)S(1)}, u32[]{:S(2)}, u32[]{:S(2)}) collective-permute-start(f32[384,768]{1,0:T(8,128)S(1)} %constant_dynamic-update-slice_fusion.10), channel_id=1, source_target_pairs={{0,1},{1,0},{2,3},{3,2},{4,5},{5,4},{6,7},{7,6},{8,9},{9,8},{10,11... | collective-permute-start | bytes 3538952 | tf_op jit(solution)/shard_map/ppermute | solution.py:82
  194.5 2.2 %collective-permute-done.9 = f32[384,768]{1,0:T(8,128)S(1)} collective-permute-done((f32[384,768]{1,0:T(8,128)S(1)}, f32[384,768]{1,0:T(8,128)S(1)}, u32[]{:S(2)}, u32[]{:S(2)}) %collective-permute-start.9) | collective-permute-done | bytes 1179680 | tf_op jit(solution)/shard_map/ppermute | solution.py:82
  196.8 4.0 %fusion.2 = f32[768,1024]{1,0:T(8,128)S(1)} fusion(f32[768,768]{1,0:T(8,128)S(1)} %constant_dynamic-update-slice_fusion.8, f32[1024,1,768]{2,1,0:T(1,128)S(1)} %copy-done), kind=kOutput, calls=%fused_computation.2 | convolution fusion | flops 3623878656 | bytes 8650752 | tf_op jit(solution)/shard_map/dot_general | solution.py:117
  200.8 0.3 broadcast_in_dim.37
  201.6 4.1 %fusion.13 = f32[1024,768]{0,1:T(8,128)S(1)} fusion(f32[1024,768]{1,0:T(8,128)S(1)} %bitcast.56, f32[768,2,768]{2,0,1:T(8,128)S(1)} %constant_dynamic-update-slice_fusion), kind=kOutput, calls=%fused_computation.18 | convolution fusion | flops 3623878656 | bytes 8650752 | tf_op jit(solution)/shard_map/dot_general | solution.py:130
  205.7 4.3 %fusion.8 = f32[1024,1,768]{0,2,1:T(8,128)S(1)} fusion(f32[1024,768]{0,1:T(8,128)S(1)} %fusion.13, f32[768,1024]{1,0:T(8,128)S(1)} %fusion.2, f32[1024,768]{1,0:T(8,128)S(1)} %bitcast.57, f32[768,2,768]{2,0,1:T(8,128)S(1)} %constant_dynamic-update-slice_fusion), kind=kOutput, calls=%fused_computation.11 | convolution fusion | flops 3626237952 | bytes 14942208 | tf_op jit(solution)/shard_map/dot_general | solution.py:132
  210.1 5.3 %copy.8 = f32[1024,1,768]{2,1,0:T(1,128)} copy(f32[1024,1,768]{0,2,1:T(8,128)S(1)} %fusion.8) | data formatting | bytes 6291456 | tf_op jit(solution)/shard_map/reshape | solution.py:135
  (56 shorter events, 3.1 us)
Async XLA Ops:
  0.0 14.6 %copy-start = (f32[1024,1,768]{2,1,0:T(1,128)S(1)}, f32[1024,1,768]{2,1,0:T(1,128)}, u32[]{:S(2)}) copy-start(f32[1024,1,768]{2,1,0:T(1,128)} %param.5) | copy-start | bytes 9437188
  13.2 6.8 %collective-permute-start.2 = (f32[384,768]{1,0:T(8,128)}, f32[384,768]{1,0:T(8,128)}, u32[]{:S(2)}, u32[]{:S(2)}) collective-permute-start(f32[384,768]{1,0:T(8,128)} %constant_dynamic-slice_fusion.7), channel_id=1, source_target_pairs={{0,1},{1,0},{2,3},{3,2},{4,5},{5,4},{6,7},{7,6},{8,9},{9,8},{10,11... | collective-permute-start | bytes 3538952 | tf_op jit(solution)/shard_map/ppermute | solution.py:74
  14.6 81.6 %collective-permute-start = (f32[1024,1,768]{2,1,0:T(1,128)S(1)}, f32[1024,1,768]{2,1,0:T(1,128)}, u32[]{:S(2)}, u32[]{:S(2)}) collective-permute-start(f32[1024,1,768]{2,1,0:T(1,128)S(1)} %copy-done), channel_id=1, source_target_pairs={{0,112},{16,0},{32,16},{48,32},{64,48},{80,64},{96,80},{112,96},{1... | collective-permute-start | bytes 9437192 | tf_op jit(solution)/shard_map/ppermute | solution.py:14
  18.8 79.5 %collective-permute-start.1 = (f32[1024,1,768]{2,1,0:T(1,128)S(1)}, f32[1024,1,768]{2,1,0:T(1,128)}, u32[]{:S(2)}, u32[]{:S(2)}) collective-permute-start(f32[1024,1,768]{2,1,0:T(1,128)S(1)} %copy-done), channel_id=1, source_target_pairs={{0,16},{16,32},{32,48},{48,64},{64,80},{80,96},{96,112},{112,0},{1... | collective-permute-start | bytes 9437192 | tf_op jit(solution)/shard_map/ppermute | solution.py:14
  22.9 18.1 %copy-start.3 = (s32[16]{0:T(128)S(1)}, s32[16]{0:T(128)}, u32[]{:S(2)}) copy-start(s32[16]{0:T(128)} %constant.79.clone) | copy-start | bytes 196
  22.9 19.4 %copy-start.1 = (f32[8]{0:T(128)S(1)}, f32[8]{0:T(128)}, u32[]{:S(2)}) copy-start(f32[8]{0:T(128)} %param.6) | copy-start | bytes 100
  22.9 27.1 %copy-start.2 = (f32[768]{0:T(1024)S(1)}, f32[768]{0:T(1024)}, u32[]{:S(2)}) copy-start(f32[768]{0:T(1024)} %param.7) | copy-start | bytes 9220
  24.8 10.6 %collective-permute-start.3 = (f32[192,768]{1,0:T(8,128)}, f32[192,768]{1,0:T(8,128)}, u32[]{:S(2)}, u32[]{:S(2)}) collective-permute-start(f32[192,768]{1,0:T(8,128)} %constant_dynamic-slice_fusion.6), channel_id=1, source_target_pairs={{0,2},{1,7},{2,0},{3,5},{4,6},{5,3},{6,4},{7,1},{8,10},{9,15},{10,... | collective-permute-start | bytes 1769480 | tf_op jit(solution)/shard_map/ppermute | solution.py:74
  39.2 6.2 %collective-permute-start.4 = (f32[96,768]{1,0:T(8,128)}, f32[96,768]{1,0:T(8,128)S(1)}, u32[]{:S(2)}, u32[]{:S(2)}) collective-permute-start(f32[96,768]{1,0:T(8,128)} %constant_dynamic-slice_fusion.5), channel_id=1, source_target_pairs={{0,6},{1,3},{2,4},{3,1},{4,2},{5,7},{6,0},{7,5},{8,14},{9,11},{10,... | collective-permute-start | bytes 884744 | tf_op jit(solution)/shard_map/ppermute | solution.py:74
  46.4 49.6 %collective-permute-start.5 = (f32[48,768]{1,0:T(8,128)S(1)}, f32[48,768]{1,0:T(8,128)S(1)}, u32[]{:S(2)}, u32[]{:S(2)}) collective-permute-start(f32[48,768]{1,0:T(8,128)S(1)} %constant_dynamic-slice_fusion.4), channel_id=1, source_target_pairs={{0,8},{1,9},{2,10},{3,11},{4,12},{5,13},{6,14},{7,15},{8,0},{9,1},... | collective-permute-start | bytes 442376 | tf_op jit(solution)/shard_map/ppermute | solution.py:74
  105.2 3.0 %collective-permute-start.10 = (f32[384,768]{1,0:T(8,128)S(1)}, f32[384,768]{1,0:T(8,128)S(1)}, u32[]{:S(2)}, u32[]{:S(2)}) collective-permute-start(f32[384,768]{1,0:T(8,128)S(1)} %dynamic-slice_bitcast_fusion), channel_id=1, source_target_pairs={{0,1},{1,0},{2,3},{3,2},{4,5},{5,4},{6,7},{7,6},{8,9},{9,8},{10,11... | collective-permute-start | bytes 3538952 | tf_op jit(solution)/shard_map/ppermute | solution.py:74
  108.4 10.0 %collective-permute-start.11 = (f32[192,768]{1,0:T(8,128)S(1)}, f32[192,768]{1,0:T(8,128)S(1)}, u32[]{:S(2)}, u32[]{:S(2)}) collective-permute-start(f32[192,768]{1,0:T(8,128)S(1)} %constant_dynamic-slice_fusion.3), channel_id=1, source_target_pairs={{0,2},{1,7},{2,0},{3,5},{4,6},{5,3},{6,4},{7,1},{8,10},{9,15},{10,... | collective-permute-start | bytes 1769480 | tf_op jit(solution)/shard_map/ppermute | solution.py:74
  118.6 5.9 %collective-permute-start.12 = (f32[96,768]{1,0:T(8,128)S(1)}, f32[96,768]{1,0:T(8,128)S(1)}, u32[]{:S(2)}, u32[]{:S(2)}) collective-permute-start(f32[96,768]{1,0:T(8,128)S(1)} %constant_dynamic-slice_fusion.2), channel_id=1, source_target_pairs={{0,6},{1,3},{2,4},{3,1},{4,2},{5,7},{6,0},{7,5},{8,14},{9,11},{10,... | collective-permute-start | bytes 884744 | tf_op jit(solution)/shard_map/ppermute | solution.py:74
  124.6 5.6 %collective-permute-start.13 = (f32[48,768]{1,0:T(8,128)S(1)}, f32[48,768]{1,0:T(8,128)S(1)}, u32[]{:S(2)}, u32[]{:S(2)}) collective-permute-start(f32[48,768]{1,0:T(8,128)S(1)} %constant_dynamic-slice_fusion), channel_id=1, source_target_pairs={{0,8},{1,9},{2,10},{3,11},{4,12},{5,13},{6,14},{7,15},{8,0},{9,1},... | collective-permute-start | bytes 442376 | tf_op jit(solution)/shard_map/ppermute | solution.py:123
  124.7 8.0 %collective-permute-start.15 = (f32[48,768]{1,0:T(8,128)S(1)}, f32[48,768]{1,0:T(8,128)S(1)}, u32[]{:S(2)}, u32[]{:S(2)}) collective-permute-start(f32[48,768]{1,0:T(8,128)S(1)} %constant_dynamic-slice_fusion), channel_id=1, source_target_pairs={{0,24},{1,25},{2,26},{3,27},{4,28},{5,29},{6,30},{7,31},{8,16},{9,... | collective-permute-start | bytes 442376 | tf_op jit(solution)/shard_map/ppermute | solution.py:126
  130.3 6.4 %collective-permute-start.14 = (f32[48,768]{1,0:T(8,128)S(1)}, f32[48,768]{1,0:T(8,128)S(1)}, u32[]{:S(2)}, u32[]{:S(2)}) collective-permute-start(f32[48,768]{1,0:T(8,128)S(1)} %get-tuple-element.12), channel_id=1, source_target_pairs={{0,16},{16,32},{32,48},{48,64},{64,80},{80,96},{96,112},{112,0},{1... | collective-permute-start | bytes 442376 | tf_op jit(solution)/shard_map/ppermute | solution.py:14
  136.8 7.2 %collective-permute-start.16 = (f32[48,2,768]{2,0,1:T(8,128)S(1)}, f32[48,2,768]{2,0,1:T(8,128)S(1)}, u32[]{:S(2)}, u32[]{:S(2)}) collective-permute-start(f32[48,2,768]{2,0,1:T(8,128)S(1)} %get-tuple-element.13), channel_id=1, source_target_pairs={{0,8},{1,9},{2,10},{3,11},{4,12},{5,13},{6,14},{7,15},{8,0},{9,1},... | collective-permute-start | bytes 884744 | tf_op jit(solution)/shard_map/ppermute | solution.py:82
  144.0 8.8 %collective-permute-start.17 = (f32[96,2,768]{2,0,1:T(8,128)S(1)}, f32[96,2,768]{2,0,1:T(8,128)S(1)}, u32[]{:S(2)}, u32[]{:S(2)}) collective-permute-start(f32[96,2,768]{2,0,1:T(8,128)S(1)} %constant_dynamic-update-slice_fusion.6), channel_id=1, source_target_pairs={{0,6},{1,3},{2,4},{3,1},{4,2},{5,7},{6,0},{7,5},{8,14},{9,11},{10,... | collective-permute-start | bytes 1769480 | tf_op jit(solution)/shard_map/ppermute | solution.py:82
  152.9 20.9 %collective-permute-start.18 = (f32[192,2,768]{2,0,1:T(8,128)S(1)}, f32[192,2,768]{2,0,1:T(8,128)S(1)}, u32[]{:S(2)}, u32[]{:S(2)}) collective-permute-start(f32[192,2,768]{2,0,1:T(8,128)S(1)} %constant_dynamic-update-slice_fusion.4), channel_id=1, source_target_pairs={{0,2},{1,7},{2,0},{3,5},{4,6},{5,3},{6,4},{7,1},{8,10},{9,15},{10,... | collective-permute-start | bytes 3538952 | tf_op jit(solution)/shard_map/ppermute | solution.py:82
  155.5 5.8 %collective-permute-start.6 = (f32[48,768]{1,0:T(8,128)S(1)}, f32[48,768]{1,0:T(8,128)S(1)}, u32[]{:S(2)}, u32[]{:S(2)}) collective-permute-start(f32[48,768]{1,0:T(8,128)S(1)} %add_divide_fusion), channel_id=1, source_target_pairs={{0,8},{1,9},{2,10},{3,11},{4,12},{5,13},{6,14},{7,15},{8,0},{9,1},... | collective-permute-start | bytes 442376 | tf_op jit(solution)/shard_map/ppermute | solution.py:82
  161.3 5.7 %collective-permute-start.7 = (f32[96,768]{1,0:T(8,128)S(1)}, f32[96,768]{1,0:T(8,128)S(1)}, u32[]{:S(2)}, u32[]{:S(2)}) collective-permute-start(f32[96,768]{1,0:T(8,128)S(1)} %constant_dynamic-update-slice_fusion.14), channel_id=1, source_target_pairs={{0,6},{1,3},{2,4},{3,1},{4,2},{5,7},{6,0},{7,5},{8,14},{9,11},{10,... | collective-permute-start | bytes 884744 | tf_op jit(solution)/shard_map/ppermute | solution.py:82
  167.0 17.7 %collective-permute-start.8 = (f32[192,768]{1,0:T(8,128)S(1)}, f32[192,768]{1,0:T(8,128)S(1)}, u32[]{:S(2)}, u32[]{:S(2)}) collective-permute-start(f32[192,768]{1,0:T(8,128)S(1)} %constant_dynamic-update-slice_fusion.12), channel_id=1, source_target_pairs={{0,2},{1,7},{2,0},{3,5},{4,6},{5,3},{6,4},{7,1},{8,10},{9,15},{10,... | collective-permute-start | bytes 1769480 | tf_op jit(solution)/shard_map/ppermute | solution.py:82
  173.9 27.5 %collective-permute-start.19 = (f32[384,2,768]{2,0,1:T(8,128)S(1)}, f32[384,2,768]{2,0,1:T(8,128)S(1)}, u32[]{:S(2)}, u32[]{:S(2)}) collective-permute-start(f32[384,2,768]{2,0,1:T(8,128)S(1)} %constant_dynamic-update-slice_fusion.2), channel_id=1, source_target_pairs={{0,1},{1,0},{2,3},{3,2},{4,5},{5,4},{6,7},{7,6},{8,9},{9,8},{10,11... | collective-permute-start | bytes 7077896 | tf_op jit(solution)/shard_map/ppermute | solution.py:82
  184.7 12.0 %collective-permute-start.9 = (f32[384,768]{1,0:T(8,128)S(1)}, f32[384,768]{1,0:T(8,128)S(1)}, u32[]{:S(2)}, u32[]{:S(2)}) collective-permute-start(f32[384,768]{1,0:T(8,128)S(1)} %constant_dynamic-update-slice_fusion.10), channel_id=1, source_target_pairs={{0,1},{1,0},{2,3},{3,2},{4,5},{5,4},{6,7},{7,6},{8,9},{9,8},{10,11... | collective-permute-start | bytes 3538952 | tf_op jit(solution)/shard_map/ppermute | solution.py:82

commit v4 on v3

--- a/solution.py
+++ b/solution.py
@@ -126,10 +126,11 @@
     prev_share = passed_along(keep, "occ", 1) + lax.ppermute(send, ("occ", "aux"), across)
     up_amp = up_share / (my_vals[:, None] + up_vals[None, :])
     prev_amp = prev_share / (my_dn_vals[:, None] + own_vals[None, :])
-    pair_full = all_gather_rows(jnp.stack([up_amp, prev_amp], axis=1), stages, bits)
-    t_up = lax.dot_general(above, pair_full[:, 0], contract_b, precision=PREC,
+    up_full = all_gather_rows(up_amp, stages, bits)
+    prev_full = all_gather_rows(prev_amp, stages, bits)
+    t_up = lax.dot_general(above, up_full, contract_b, precision=PREC,
                            preferred_element_type=jnp.float32)
-    t_prev = lax.dot_general(below, pair_full[:, 1], (((1,), (0,)), ((), ())),
+    t_prev = lax.dot_general(below, prev_full, (((1,), (0,)), ((), ())),
                              precision=PREC, preferred_element_type=jnp.float32)
     total = t_own + t_up + t_prev
     return (1.3 * total).reshape(aux_dev, occ_dev, virt)

time: 216 us -> 198 us (0.917)
  waiting for transfers between devices: 111 us -> 91 us
  starting transfers between devices: 43.3 us -> 45.7 us
    ppermute x7, waiting for transfers between devices: 68.9 us -> 58.7 us  [reduce_scatter_rows(): value = keep + lax.ppermute(send, 'aux', pairs)]
    ppermute x8 -> x12, waiting for transfers between devices: 30.7 us -> 23.4 us  [all_gather_rows(): got = lax.ppermute(value, 'aux', pairs)]
    ppermute x3, waiting for transfers between devices: 3.96 us -> 1.64 us  [passed_along(): return lax.ppermute(value, axis, pairs)]
    ppermute x8 -> x12, starting transfers between devices: 28 us -> 29.5 us  [all_gather_rows(): got = lax.ppermute(value, 'aux', pairs)]
  transfers between devices with their start and end apart: 20 -> 24, of which waited for: 15 -> 17; matrix products, arithmetic and copies ran while one was open for 10% -> 13% of each run, Pallas kernels for 0% -> 0%
where the time goes in v4:
time: 198 us
  waiting for transfers between devices  91 us (46%)
  starting transfers between devices  45.7 us (23%)
  matrix products  26 us (13%)
  local copies, waits for them, and re-layouts  20.5 us (10%)
  other arithmetic  8.64 us (4%)
  between operations  6.06 us (3%)
    ppermute x7, waiting for transfers between devices, reduce_scatter_rows(): value = keep + lax.ppermute(send, 'aux', pairs)  58.7 us
    ppermute x12, starting transfers between devices, all_gather_rows(): got = lax.ppermute(value, 'aux', pairs)  29.5 us
    ppermute x12, waiting for transfers between devices, all_gather_rows(): got = lax.ppermute(value, 'aux', pairs)  23.4 us
    ppermute x7, starting transfers between devices, reduce_scatter_rows(): value = keep + lax.ppermute(send, 'aux', pairs)  11.8 us
    dot_general x1, matrix products, body(): lax.dot_general(own, own, contract_p, precision=PREC, preferred_element_t...  8.79 us
    dynamic_slice x8, local copies, waits for them, and re-layouts, reduce_scatter_rows(): send = lax.dynamic_slice_in_dim(value, (1 - bit) * half, half, 0)  6.34 us
    add x6, other arithmetic, reduce_scatter_rows(): value = keep + lax.ppermute(send, 'aux', pairs)  6.27 us
    ppermute x1, waiting for transfers between devices, body(): up_share = keep + lax.ppermute(send, 'aux', last)  5.4 us
  transfers between devices with their start and end apart: 24, of which 17 were waited for; matrix products, arithmetic and copies ran while one was open for 13% of the time, Pallas kernels for 0%

profile of v4, /device:TPU:1, one launch (start us, length us, event | category | flops | bytes accessed | tf_op | source)
XLA Modules:
  0.0 197.9 jit_solution(13221110344580286159)
XLA Ops:
  0.0 8.8 %fusion.4 = f32[768,768]{1,0:T(8,128)} fusion(f32[1024,1,768]{2,1,0:T(1,128)} %param.5), kind=kOutput, calls=%fused_computation.4 | convolution fusion | flops 3623878656 | bytes 5505024 | tf_op jit(solution)/shard_map/dot_general | solution.py:111
  8.8 0.7 constant_dynamic-slice_fusion.8
  9.5 0.7 fusion.13
  10.7 2.5 %constant_dynamic-slice_fusion.7 = f32[384,768]{1,0:T(8,128)} fusion(f32[768,768]{1,0:T(8,128)} %fusion.4, s32[]{:T(128)S(6)} %select_n.39), kind=kLoop, calls=%fused_computation.56 | loop fusion | bytes 2359300 | tf_op jit(solution)/shard_map/dynamic_slice | solution.py:71
  13.2 1.4 collective-permute-start.2
  14.6 4.2 %collective-permute-start = (f32[1024,1,768]{2,1,0:T(1,128)S(1)}, f32[1024,1,768]{2,1,0:T(1,128)}, u32[]{:S(2)}, u32[]{:S(2)}) collective-permute-start(f32[1024,1,768]{2,1,0:T(1,128)S(1)} %copy-done), channel_id=1, source_target_pairs={{0,112},{16,0},{32,16},{48,32},{64,48},{80,64},{96,80},{112,96},{1... | collective-permute-start | bytes 9437192 | tf_op jit(solution)/shard_map/ppermute | solution.py:14
  19.9 2.9 %dynamic-slice_add_fusion = f32[384,768]{1,0:T(8,128)} fusion(f32[384,768]{1,0:T(8,128)} %collective-permute-done.2, f32[768,768]{1,0:T(8,128)} %fusion.4, s32[]{:T(128)S(6)} %select_n.38), kind=kLoop, calls=%fused_computation.17 | loop fusion | flops 294912 | bytes 3538948 | tf_op jit(solution)/shard_map/add | solution.py:74
  22.8 2.0 constant_dynamic-slice_fusion.6
  24.8 2.5 %collective-permute-start.3 = (f32[192,768]{1,0:T(8,128)}, f32[192,768]{1,0:T(8,128)}, u32[]{:S(2)}, u32[]{:S(2)}) collective-permute-start(f32[192,768]{1,0:T(8,128)} %constant_dynamic-slice_fusion.6), channel_id=1, source_target_pairs={{0,2},{1,7},{2,0},{3,5},{4,6},{5,3},{6,4},{7,1},{8,10},{9,15},{10,... | collective-permute-start | bytes 1769480 | tf_op jit(solution)/shard_map/ppermute | solution.py:74
  28.6 6.8 %collective-permute-done.3 = f32[192,768]{1,0:T(8,128)} collective-permute-done((f32[192,768]{1,0:T(8,128)}, f32[192,768]{1,0:T(8,128)}, u32[]{:S(2)}, u32[]{:S(2)}) %collective-permute-start.3) | collective-permute-done | bytes 589856 | tf_op jit(solution)/shard_map/ppermute | solution.py:74
  35.4 2.1 %dynamic-slice_add_fusion.2 = f32[192,768]{1,0:T(8,128)} fusion(f32[192,768]{1,0:T(8,128)} %collective-permute-done.3, f32[384,768]{1,0:T(8,128)} %dynamic-slice_add_fusion, s32[]{:T(128)S(6)} %select_n.40), kind=kLoop, calls=%fused_computation.19 | loop fusion | flops 147456 | bytes 1769476 | tf_op jit(solution)/shard_map/add | solution.py:74
  37.5 1.7 constant_dynamic-slice_fusion.5
  41.2 0.6 dynamic_slice.75
  42.4 0.7 fusion.12
  43.1 2.3 %collective-permute-done.4 = f32[96,768]{1,0:T(8,128)S(1)} collective-permute-done((f32[96,768]{1,0:T(8,128)}, f32[96,768]{1,0:T(8,128)S(1)}, u32[]{:S(2)}, u32[]{:S(2)}) %collective-permute-start.4) | collective-permute-done | bytes 294944 | tf_op jit(solution)/shard_map/ppermute | solution.py:74
  45.4 1.0 dynamic-slice_add_fusion.4
  46.4 3.6 %collective-permute-start.5 = (f32[48,768]{1,0:T(8,128)S(1)}, f32[48,768]{1,0:T(8,128)S(1)}, u32[]{:S(2)}, u32[]{:S(2)}) collective-permute-start(f32[48,768]{1,0:T(8,128)S(1)} %constant_dynamic-slice_fusion.4), channel_id=1, source_target_pairs={{0,8},{1,9},{2,10},{3,11},{4,12},{5,13},{6,14},{7,15},{8,0},{9,1},... | collective-permute-start | bytes 442376 | tf_op jit(solution)/shard_map/ppermute | solution.py:74
  50.0 2.1 %broadcast_subtract_fusion.1 = (f32[768]{0:T(1024)S(1)}, f32[768]{0:T(1024)S(1)}, f32[768]{0:T(1024)S(1)}) fusion(f32[768]{0:T(1024)S(1)} %copy-done.2, f32[]{:T(128)} %bitcast.13, f32[]{:T(128)} %bitcast.8, f32[]{:T(128)} %bitcast.14), kind=kLoop, calls=%fused_computation.59 | loop fusion | flops 2304 | bytes 12300 | tf_op jit(solution)/shard_map/sub | solution.py:19
  52.1 43.9 %collective-permute-done.5 = f32[48,768]{1,0:T(8,128)S(1)} collective-permute-done((f32[48,768]{1,0:T(8,128)S(1)}, f32[48,768]{1,0:T(8,128)S(1)}, u32[]{:S(2)}, u32[]{:S(2)}) %collective-permute-start.5) | collective-permute-done | bytes 147488 | tf_op jit(solution)/shard_map/ppermute | solution.py:74
  96.1 2.1 %copy.29 = f32[1024,1,768]{2,0,1:T(8,128)S(1)} copy(f32[1024,1,768]{2,1,0:T(1,128)} %collective-permute-done) | data formatting | bytes 6291456
  98.2 2.1 %copy.28 = f32[1024,1,768]{2,0,1:T(8,128)S(1)} copy(f32[1024,1,768]{2,1,0:T(1,128)} %collective-permute-done.1) | data formatting | bytes 6291456
  100.3 4.8 %fusion = f32[768,768]{0,1:T(8,128)S(1)} fusion(f32[1024,768]{1,0:T(8,128)S(1)} %bitcast.45, f32[1024,1,768]{2,1,0:T(1,128)S(1)} %copy-done), kind=kOutput, calls=%fused_computation | convolution fusion | flops 3623878656 | bytes 8650752 | tf_op jit(solution)/shard_map/dot_general | solution.py:120
  105.2 0.6 collective-permute-start.10
  105.8 2.5 %collective-permute-done.10 = f32[384,768]{1,0:T(8,128)S(1)} collective-permute-done((f32[384,768]{1,0:T(8,128)S(1)}, f32[384,768]{1,0:T(8,128)S(1)}, u32[]{:S(2)}, u32[]{:S(2)}) %collective-permute-start.10) | collective-permute-done | bytes 1179680 | tf_op jit(solution)/shard_map/ppermute | solution.py:74
  108.5 2.6 %collective-permute-start.11 = (f32[192,768]{1,0:T(8,128)S(1)}, f32[192,768]{1,0:T(8,128)S(1)}, u32[]{:S(2)}, u32[]{:S(2)}) collective-permute-start(f32[192,768]{1,0:T(8,128)S(1)} %constant_dynamic-slice_fusion.3), channel_id=1, source_target_pairs={{0,2},{1,7},{2,0},{3,5},{4,6},{5,3},{6,4},{7,1},{8,10},{9,15},{10,... | collective-permute-start | bytes 1769480 | tf_op jit(solution)/shard_map/ppermute | solution.py:74
  111.1 7.0 %collective-permute-done.6 = f32[48,768]{1,0:T(8,128)S(1)} collective-permute-done((f32[48,768]{1,0:T(8,128)S(1)}, f32[48,768]{1,0:T(8,128)S(1)}, u32[]{:S(2)}, u32[]{:S(2)}) %collective-permute-start.6) | collective-permute-done | bytes 147488 | tf_op jit(solution)/shard_map/ppermute | solution.py:82
  118.6 1.2 collective-permute-start.12
  119.9 4.1 %collective-permute-done.7 = f32[96,768]{1,0:T(8,128)S(1)} collective-permute-done((f32[96,768]{1,0:T(8,128)S(1)}, f32[96,768]{1,0:T(8,128)S(1)}, u32[]{:S(2)}, u32[]{:S(2)}) %collective-permute-start.7) | collective-permute-done | bytes 294944 | tf_op jit(solution)/shard_map/ppermute | solution.py:82
  124.2 3.0 %collective-permute-done.12 = f32[96,768]{1,0:T(8,128)S(1)} collective-permute-done((f32[96,768]{1,0:T(8,128)S(1)}, f32[96,768]{1,0:T(8,128)S(1)}, u32[]{:S(2)}, u32[]{:S(2)}) %collective-permute-start.12) | collective-permute-done | bytes 294944 | tf_op jit(solution)/shard_map/ppermute | solution.py:74
  127.5 5.4 %collective-permute-done.13 = f32[48,768]{1,0:T(8,128)S(1)} collective-permute-done((f32[48,768]{1,0:T(8,128)S(1)}, f32[48,768]{1,0:T(8,128)S(1)}, u32[]{:S(2)}, u32[]{:S(2)}) %collective-permute-start.13) | collective-permute-done | bytes 147488 | tf_op jit(solution)/shard_map/ppermute | solution.py:123
  133.4 1.9 collective-permute-done.8
  135.4 3.0 %collective-permute-start.9 = (f32[384,768]{1,0:T(8,128)S(1)}, f32[384,768]{1,0:T(8,128)S(1)}, u32[]{:S(2)}, u32[]{:S(2)}) collective-permute-start(f32[384,768]{1,0:T(8,128)S(1)} %constant_dynamic-update-slice_fusion.18), channel_id=1, source_target_pairs={{0,1},{1,0},{2,3},{3,2},{4,5},{5,4},{6,7},{7,6},{8,9},{9,8},{10,11... | collective-permute-start | bytes 3538952 | tf_op jit(solution)/shard_map/ppermute | solution.py:82
  138.3 0.2 collective-permute-done.14
  138.8 1.8 collective-permute-done.19
  140.6 1.6 collective-permute-done.18
  142.4 1.2 collective-permute-start.20
  143.7 0.9 collective-permute-done.15
  144.6 3.4 %collective-permute-start.16 = (f32[192,768]{1,0:T(8,128)S(1)}, f32[192,768]{1,0:T(8,128)S(1)}, u32[]{:S(2)}, u32[]{:S(2)}) collective-permute-start(f32[192,768]{1,0:T(8,128)S(1)} %constant_dynamic-update-slice_fusion.12), channel_id=1, source_target_pairs={{0,2},{1,7},{2,0},{3,5},{4,6},{5,3},{6,4},{7,1},{8,10},{9,15},{10,... | collective-permute-start | bytes 1769480 | tf_op jit(solution)/shard_map/ppermute | solution.py:82
  148.0 1.4 collective-permute-done.20
  149.6 5.8 %collective-permute-done.21 = f32[96,768]{1,0:T(8,128)S(1)} collective-permute-done((f32[96,768]{1,0:T(8,128)S(1)}, f32[96,768]{1,0:T(8,128)S(1)}, u32[]{:S(2)}, u32[]{:S(2)}) %collective-permute-start.21) | collective-permute-done | bytes 294944 | tf_op jit(solution)/shard_map/ppermute | solution.py:82
  155.4 0.9 collective-permute-start.22
  156.4 2.0 %collective-permute-done.16 = f32[192,768]{1,0:T(8,128)S(1)} collective-permute-done((f32[192,768]{1,0:T(8,128)S(1)}, f32[192,768]{1,0:T(8,128)S(1)}, u32[]{:S(2)}, u32[]{:S(2)}) %collective-permute-start.16) | collective-permute-done | bytes 589856 | tf_op jit(solution)/shard_map/ppermute | solution.py:82
  158.5 11.0 %collective-permute-start.17 = (f32[384,768]{1,0:T(8,128)S(1)}, f32[384,768]{1,0:T(8,128)S(1)}, u32[]{:S(2)}, u32[]{:S(2)}) collective-permute-start(f32[384,768]{1,0:T(8,128)S(1)} %constant_dynamic-update-slice_fusion.10), channel_id=1, source_target_pairs={{0,1},{1,0},{2,3},{3,2},{4,5},{5,4},{6,7},{7,6},{8,9},{9,8},{10,11... | collective-permute-start | bytes 3538952 | tf_op jit(solution)/shard_map/ppermute | solution.py:82
  170.1 9.4 %collective-permute-start.23 = (f32[384,768]{1,0:T(8,128)S(1)}, f32[384,768]{1,0:T(8,128)S(1)}, u32[]{:S(2)}, u32[]{:S(2)}) collective-permute-start(f32[384,768]{1,0:T(8,128)S(1)} %constant_dynamic-update-slice_fusion.2), channel_id=1, source_target_pairs={{0,1},{1,0},{2,3},{3,2},{4,5},{5,4},{6,7},{7,6},{8,9},{9,8},{10,11... | collective-permute-start | bytes 3538952 | tf_op jit(solution)/shard_map/ppermute | solution.py:82
  179.4 4.0 %fusion.2 = f32[768,1024]{1,0:T(8,128)S(1)} fusion(f32[768,768]{1,0:T(8,128)S(1)} %constant_dynamic-update-slice_fusion.16, f32[1024,1,768]{2,1,0:T(1,128)S(1)} %copy-done), kind=kOutput, calls=%fused_computation.2 | convolution fusion | flops 3623878656 | bytes 8650752 | tf_op jit(solution)/shard_map/dot_general | solution.py:117
  184.1 4.1 %fusion.14 = f32[1024,768]{0,1:T(8,128)S(1)} fusion(f32[1024,768]{1,0:T(8,128)S(1)} %bitcast.46, f32[768,768]{1,0:T(8,128)S(1)} %constant_dynamic-update-slice_fusion.8), kind=kOutput, calls=%fused_computation.63 | convolution fusion | flops 3623878656 | bytes 8650752 | tf_op jit(solution)/shard_map/dot_general | solution.py:131
  188.2 4.3 %fusion.8 = f32[1024,1,768]{0,2,1:T(8,128)S(1)} fusion(f32[1024,768]{0,1:T(8,128)S(1)} %fusion.14, f32[768,1024]{1,0:T(8,128)S(1)} %fusion.2, f32[1024,768]{1,0:T(8,128)S(1)} %bitcast.47, f32[768,768]{1,0:T(8,128)S(1)} %constant_dynamic-update-slice_fusion), kind=kOutput, calls=%fused_computation.11 | convolution fusion | flops 3626237952 | bytes 14942208 | tf_op jit(solution)/shard_map/dot_general | solution.py:133
  192.6 5.3 %copy.8 = f32[1024,1,768]{2,1,0:T(1,128)} copy(f32[1024,1,768]{0,2,1:T(8,128)S(1)} %fusion.8) | data formatting | bytes 6291456 | tf_op jit(solution)/shard_map/reshape | solution.py:136
  (74 shorter events, 3.9 us)
Async XLA Ops:
  0.0 14.6 %copy-start = (f32[1024,1,768]{2,1,0:T(1,128)S(1)}, f32[1024,1,768]{2,1,0:T(1,128)}, u32[]{:S(2)}) copy-start(f32[1024,1,768]{2,1,0:T(1,128)} %param.5) | copy-start | bytes 9437188
  13.2 6.7 %collective-permute-start.2 = (f32[384,768]{1,0:T(8,128)}, f32[384,768]{1,0:T(8,128)}, u32[]{:S(2)}, u32[]{:S(2)}) collective-permute-start(f32[384,768]{1,0:T(8,128)} %constant_dynamic-slice_fusion.7), channel_id=1, source_target_pairs={{0,1},{1,0},{2,3},{3,2},{4,5},{5,4},{6,7},{7,6},{8,9},{9,8},{10,11... | collective-permute-start | bytes 3538952 | tf_op jit(solution)/shard_map/ppermute | solution.py:74
  14.6 81.6 %collective-permute-start = (f32[1024,1,768]{2,1,0:T(1,128)S(1)}, f32[1024,1,768]{2,1,0:T(1,128)}, u32[]{:S(2)}, u32[]{:S(2)}) collective-permute-start(f32[1024,1,768]{2,1,0:T(1,128)S(1)} %copy-done), channel_id=1, source_target_pairs={{0,112},{16,0},{32,16},{48,32},{64,48},{80,64},{96,80},{112,96},{1... | collective-permute-start | bytes 9437192 | tf_op jit(solution)/shard_map/ppermute | solution.py:14
  18.8 79.5 %collective-permute-start.1 = (f32[1024,1,768]{2,1,0:T(1,128)S(1)}, f32[1024,1,768]{2,1,0:T(1,128)}, u32[]{:S(2)}, u32[]{:S(2)}) collective-permute-start(f32[1024,1,768]{2,1,0:T(1,128)S(1)} %copy-done), channel_id=1, source_target_pairs={{0,16},{16,32},{32,48},{48,64},{64,80},{80,96},{96,112},{112,0},{1... | collective-permute-start | bytes 9437192 | tf_op jit(solution)/shard_map/ppermute | solution.py:14
  22.8 18.3 %copy-start.3 = (s32[16]{0:T(128)S(1)}, s32[16]{0:T(128)}, u32[]{:S(2)}) copy-start(s32[16]{0:T(128)} %constant.75.clone) | copy-start | bytes 196
  22.8 19.6 %copy-start.1 = (f32[8]{0:T(128)S(1)}, f32[8]{0:T(128)}, u32[]{:S(2)}) copy-start(f32[8]{0:T(128)} %param.6) | copy-start | bytes 100
  22.8 27.1 %copy-start.2 = (f32[768]{0:T(1024)S(1)}, f32[768]{0:T(1024)}, u32[]{:S(2)}) copy-start(f32[768]{0:T(1024)} %param.7) | copy-start | bytes 9220
  24.8 10.6 %collective-permute-start.3 = (f32[192,768]{1,0:T(8,128)}, f32[192,768]{1,0:T(8,128)}, u32[]{:S(2)}, u32[]{:S(2)}) collective-permute-start(f32[192,768]{1,0:T(8,128)} %constant_dynamic-slice_fusion.6), channel_id=1, source_target_pairs={{0,2},{1,7},{2,0},{3,5},{4,6},{5,3},{6,4},{7,1},{8,10},{9,15},{10,... | collective-permute-start | bytes 1769480 | tf_op jit(solution)/shard_map/ppermute | solution.py:74
  39.2 6.2 %collective-permute-start.4 = (f32[96,768]{1,0:T(8,128)}, f32[96,768]{1,0:T(8,128)S(1)}, u32[]{:S(2)}, u32[]{:S(2)}) collective-permute-start(f32[96,768]{1,0:T(8,128)} %constant_dynamic-slice_fusion.5), channel_id=1, source_target_pairs={{0,6},{1,3},{2,4},{3,1},{4,2},{5,7},{6,0},{7,5},{8,14},{9,11},{10,... | collective-permute-start | bytes 884744 | tf_op jit(solution)/shard_map/ppermute | solution.py:74
  46.4 49.6 %collective-permute-start.5 = (f32[48,768]{1,0:T(8,128)S(1)}, f32[48,768]{1,0:T(8,128)S(1)}, u32[]{:S(2)}, u32[]{:S(2)}) collective-permute-start(f32[48,768]{1,0:T(8,128)S(1)} %constant_dynamic-slice_fusion.4), channel_id=1, source_target_pairs={{0,8},{1,9},{2,10},{3,11},{4,12},{5,13},{6,14},{7,15},{8,0},{9,1},... | collective-permute-start | bytes 442376 | tf_op jit(solution)/shard_map/ppermute | solution.py:74
  105.2 3.0 %collective-permute-start.10 = (f32[384,768]{1,0:T(8,128)S(1)}, f32[384,768]{1,0:T(8,128)S(1)}, u32[]{:S(2)}, u32[]{:S(2)}) collective-permute-start(f32[384,768]{1,0:T(8,128)S(1)} %dynamic-slice_bitcast_fusion), channel_id=1, source_target_pairs={{0,1},{1,0},{2,3},{3,2},{4,5},{5,4},{6,7},{7,6},{8,9},{9,8},{10,11... | collective-permute-start | bytes 3538952 | tf_op jit(solution)/shard_map/ppermute | solution.py:74
  108.5 10.0 %collective-permute-start.11 = (f32[192,768]{1,0:T(8,128)S(1)}, f32[192,768]{1,0:T(8,128)S(1)}, u32[]{:S(2)}, u32[]{:S(2)}) collective-permute-start(f32[192,768]{1,0:T(8,128)S(1)} %constant_dynamic-slice_fusion.3), channel_id=1, source_target_pairs={{0,2},{1,7},{2,0},{3,5},{4,6},{5,3},{6,4},{7,1},{8,10},{9,15},{10,... | collective-permute-start | bytes 1769480 | tf_op jit(solution)/shard_map/ppermute | solution.py:74
  111.0 7.1 %collective-permute-start.6 = (f32[48,768]{1,0:T(8,128)S(1)}, f32[48,768]{1,0:T(8,128)S(1)}, u32[]{:S(2)}, u32[]{:S(2)}) collective-permute-start(f32[48,768]{1,0:T(8,128)S(1)} %add_divide_fusion.2), channel_id=1, source_target_pairs={{0,8},{1,9},{2,10},{3,11},{4,12},{5,13},{6,14},{7,15},{8,0},{9,1},... | collective-permute-start | bytes 442376 | tf_op jit(solution)/shard_map/ppermute | solution.py:82
  118.1 5.9 %collective-permute-start.7 = (f32[96,768]{1,0:T(8,128)S(1)}, f32[96,768]{1,0:T(8,128)S(1)}, u32[]{:S(2)}, u32[]{:S(2)}) collective-permute-start(f32[96,768]{1,0:T(8,128)S(1)} %constant_dynamic-update-slice_fusion.22), channel_id=1, source_target_pairs={{0,6},{1,3},{2,4},{3,1},{4,2},{5,7},{6,0},{7,5},{8,14},{9,11},{10,... | collective-permute-start | bytes 884744 | tf_op jit(solution)/shard_map/ppermute | solution.py:82
  118.6 8.6 %collective-permute-start.12 = (f32[96,768]{1,0:T(8,128)S(1)}, f32[96,768]{1,0:T(8,128)S(1)}, u32[]{:S(2)}, u32[]{:S(2)}) collective-permute-start(f32[96,768]{1,0:T(8,128)S(1)} %constant_dynamic-slice_fusion.2), channel_id=1, source_target_pairs={{0,6},{1,3},{2,4},{3,1},{4,2},{5,7},{6,0},{7,5},{8,14},{9,11},{10,... | collective-permute-start | bytes 884744 | tf_op jit(solution)/shard_map/ppermute | solution.py:74
  124.1 11.2 %collective-permute-start.8 = (f32[192,768]{1,0:T(8,128)S(1)}, f32[192,768]{1,0:T(8,128)S(1)}, u32[]{:S(2)}, u32[]{:S(2)}) collective-permute-start(f32[192,768]{1,0:T(8,128)S(1)} %constant_dynamic-update-slice_fusion.20), channel_id=1, source_target_pairs={{0,2},{1,7},{2,0},{3,5},{4,6},{5,3},{6,4},{7,1},{8,10},{9,15},{10,... | collective-permute-start | bytes 1769480 | tf_op jit(solution)/shard_map/ppermute | solution.py:82
  127.3 5.6 %collective-permute-start.13 = (f32[48,768]{1,0:T(8,128)S(1)}, f32[48,768]{1,0:T(8,128)S(1)}, u32[]{:S(2)}, u32[]{:S(2)}) collective-permute-start(f32[48,768]{1,0:T(8,128)S(1)} %constant_dynamic-slice_fusion), channel_id=1, source_target_pairs={{0,8},{1,9},{2,10},{3,11},{4,12},{5,13},{6,14},{7,15},{8,0},{9,1},... | collective-permute-start | bytes 442376 | tf_op jit(solution)/shard_map/ppermute | solution.py:123
  133.0 5.6 %collective-permute-start.14 = (f32[48,768]{1,0:T(8,128)S(1)}, f32[48,768]{1,0:T(8,128)S(1)}, u32[]{:S(2)}, u32[]{:S(2)}) collective-permute-start(f32[48,768]{1,0:T(8,128)S(1)} %get-tuple-element.12), channel_id=1, source_target_pairs={{0,8},{1,9},{2,10},{3,11},{4,12},{5,13},{6,14},{7,15},{8,0},{9,1},... | collective-permute-start | bytes 442376 | tf_op jit(solution)/shard_map/ppermute | solution.py:82
  133.2 7.4 %collective-permute-start.19 = (f32[48,768]{1,0:T(8,128)S(1)}, f32[48,768]{1,0:T(8,128)S(1)}, u32[]{:S(2)}, u32[]{:S(2)}) collective-permute-start(f32[48,768]{1,0:T(8,128)S(1)} %constant_dynamic-slice_fusion), channel_id=1, source_target_pairs={{0,24},{1,25},{2,26},{3,27},{4,28},{5,29},{6,30},{7,31},{8,16},{9,... | collective-permute-start | bytes 442376 | tf_op jit(solution)/shard_map/ppermute | solution.py:126
  133.3 8.9 %collective-permute-start.18 = (f32[48,768]{1,0:T(8,128)S(1)}, f32[48,768]{1,0:T(8,128)S(1)}, u32[]{:S(2)}, u32[]{:S(2)}) collective-permute-start(f32[48,768]{1,0:T(8,128)S(1)} %get-tuple-element.13), channel_id=1, source_target_pairs={{0,16},{16,32},{32,48},{48,64},{64,80},{80,96},{96,112},{112,0},{1... | collective-permute-start | bytes 442376 | tf_op jit(solution)/shard_map/ppermute | solution.py:14
  135.4 34.4 %collective-permute-start.9 = (f32[384,768]{1,0:T(8,128)S(1)}, f32[384,768]{1,0:T(8,128)S(1)}, u32[]{:S(2)}, u32[]{:S(2)}) collective-permute-start(f32[384,768]{1,0:T(8,128)S(1)} %constant_dynamic-update-slice_fusion.18), channel_id=1, source_target_pairs={{0,1},{1,0},{2,3},{3,2},{4,5},{5,4},{6,7},{7,6},{8,9},{9,8},{10,11... | collective-permute-start | bytes 3538952 | tf_op jit(solution)/shard_map/ppermute | solution.py:82
  138.6 5.9 %collective-permute-start.15 = (f32[96,768]{1,0:T(8,128)S(1)}, f32[96,768]{1,0:T(8,128)S(1)}, u32[]{:S(2)}, u32[]{:S(2)}) collective-permute-start(f32[96,768]{1,0:T(8,128)S(1)} %constant_dynamic-update-slice_fusion.14), channel_id=1, source_target_pairs={{0,6},{1,3},{2,4},{3,1},{4,2},{5,7},{6,0},{7,5},{8,14},{9,11},{10,... | collective-permute-start | bytes 884744 | tf_op jit(solution)/shard_map/ppermute | solution.py:82
  142.4 7.1 %collective-permute-start.20 = (f32[48,768]{1,0:T(8,128)S(1)}, f32[48,768]{1,0:T(8,128)S(1)}, u32[]{:S(2)}, u32[]{:S(2)}) collective-permute-start(f32[48,768]{1,0:T(8,128)S(1)} %get-tuple-element.15), channel_id=1, source_target_pairs={{0,8},{1,9},{2,10},{3,11},{4,12},{5,13},{6,14},{7,15},{8,0},{9,1},... | collective-permute-start | bytes 442376 | tf_op jit(solution)/shard_map/ppermute | solution.py:82
  144.6 13.9 %collective-permute-start.16 = (f32[192,768]{1,0:T(8,128)S(1)}, f32[192,768]{1,0:T(8,128)S(1)}, u32[]{:S(2)}, u32[]{:S(2)}) collective-permute-start(f32[192,768]{1,0:T(8,128)S(1)} %constant_dynamic-update-slice_fusion.12), channel_id=1, source_target_pairs={{0,2},{1,7},{2,0},{3,5},{4,6},{5,3},{6,4},{7,1},{8,10},{9,15},{10,... | collective-permute-start | bytes 1769480 | tf_op jit(solution)/shard_map/ppermute | solution.py:82
  149.5 5.9 %collective-permute-start.21 = (f32[96,768]{1,0:T(8,128)S(1)}, f32[96,768]{1,0:T(8,128)S(1)}, u32[]{:S(2)}, u32[]{:S(2)}) collective-permute-start(f32[96,768]{1,0:T(8,128)S(1)} %constant_dynamic-update-slice_fusion.6), channel_id=1, source_target_pairs={{0,6},{1,3},{2,4},{3,1},{4,2},{5,7},{6,0},{7,5},{8,14},{9,11},{10,... | collective-permute-start | bytes 884744 | tf_op jit(solution)/shard_map/ppermute | solution.py:82
  155.4 14.6 %collective-permute-start.22 = (f32[192,768]{1,0:T(8,128)S(1)}, f32[192,768]{1,0:T(8,128)S(1)}, u32[]{:S(2)}, u32[]{:S(2)}) collective-permute-start(f32[192,768]{1,0:T(8,128)S(1)} %constant_dynamic-update-slice_fusion.4), channel_id=1, source_target_pairs={{0,2},{1,7},{2,0},{3,5},{4,6},{5,3},{6,4},{7,1},{8,10},{9,15},{10,... | collective-permute-start | bytes 1769480 | tf_op jit(solution)/shard_map/ppermute | solution.py:82
  158.5 25.5 %collective-permute-start.17 = (f32[384,768]{1,0:T(8,128)S(1)}, f32[384,768]{1,0:T(8,128)S(1)}, u32[]{:S(2)}, u32[]{:S(2)}) collective-permute-start(f32[384,768]{1,0:T(8,128)S(1)} %constant_dynamic-update-slice_fusion.10), channel_id=1, source_target_pairs={{0,1},{1,0},{2,3},{3,2},{4,5},{5,4},{6,7},{7,6},{8,9},{9,8},{10,11... | collective-permute-start | bytes 3538952 | tf_op jit(solution)/shard_map/ppermute | solution.py:82
  170.1 18.1 %collective-permute-start.23 = (f32[384,768]{1,0:T(8,128)S(1)}, f32[384,768]{1,0:T(8,128)S(1)}, u32[]{:S(2)}, u32[]{:S(2)}) collective-permute-start(f32[384,768]{1,0:T(8,128)S(1)} %constant_dynamic-update-slice_fusion.2), channel_id=1, source_target_pairs={{0,1},{1,0},{2,3},{3,2},{4,5},{5,4},{6,7},{7,6},{8,9},{9,8},{10,11... | collective-permute-start | bytes 3538952 | tf_op jit(solution)/shard_map/ppermute | solution.py:82

commit v5 on v1

--- a/solution.py
+++ b/solution.py
@@ -85,7 +85,7 @@
 
 
 def body(factors, eps_occ, eps_vir):
-    aux_dev, occ_dev, virt = factors.shape
+    _, occ_dev, virt = factors.shape
     width = occ_dev * virt
     group = lax.axis_index("occ")
     groups = lax.axis_size("occ")
@@ -94,26 +94,25 @@
     bits, my_share = keep_bits(stages, share)
     rows = width // aux_count
 
-    own = factors.reshape(aux_dev, width)
-    below = passed_along(own, "occ", 1)
-    above = passed_along(own, "occ", -1)
+    below = passed_along(factors, "occ", 1)
+    above = passed_along(factors, "occ", -1)
 
     own_vals = pair_values(eps_occ, eps_vir, group, occ_dev)
     up_vals = pair_values(eps_occ, eps_vir, (group + 1) % groups, occ_dev)
     my_vals = lax.dynamic_slice_in_dim(own_vals, my_share * rows, rows)
 
-    contract_p = (((0,), (0,)), ((), ()))
-    contract_b = (((1,), (1,)), ((), ()))
-    diag = lax.dot_general(own, own, contract_p, precision=PREC,
+    contract_p = (((0, 1), (0, 1)), ((), ()))
+    contract_b = (((2,), (1,)), ((), ()))
+    diag = lax.dot_general(factors, factors, contract_p, precision=PREC,
                            preferred_element_type=jnp.float32)
     diag_share = reduce_scatter_rows(diag, stages, bits)
     diag_amp = diag_share / (my_vals[:, None] + own_vals[None, :])
     above, below, diag_amp = lax.optimization_barrier((above, below, diag_amp))
     diag_full = all_gather_rows(diag_amp, stages, bits)
-    t_own = lax.dot_general(own, diag_full, contract_b, precision=PREC,
+    t_own = lax.dot_general(factors, diag_full, contract_b, precision=PREC,
                             preferred_element_type=jnp.float32)
 
-    up = lax.dot_general(own, above, contract_p, precision=PREC,
+    up = lax.dot_general(factors, above, contract_p, precision=PREC,
                          preferred_element_type=jnp.float32)
     up_share = reduce_scatter_rows(up, stages, bits)
     up_amp = up_share / (my_vals[:, None] + up_vals[None, :])
@@ -122,10 +121,10 @@
     prev_full = all_gather_rows(prev_amp, stages, bits)
     t_up = lax.dot_general(above, up_full, contract_b, precision=PREC,
                            preferred_element_type=jnp.float32)
-    t_prev = lax.dot_general(below, prev_full, (((1,), (0,)), ((), ())),
+    t_prev = lax.dot_general(below, prev_full, (((2,), (0,)), ((), ())),
                              precision=PREC, preferred_element_type=jnp.float32)
     total = t_own + t_up + t_prev
-    return (1.3 * total).reshape(aux_dev, occ_dev, virt)
+    return 1.3 * total
 
 
 def solution(mesh):

time: 194 us -> 192 us (0.990)
    mul x0 -> x1, local copies, waits for them, and re-layouts: none -> 5.31 us  [body(): return 1.3 * total]
    reshape x1 -> x0, local copies, waits for them, and re-layouts: 5.31 us -> none  [body(): return (1.3 * total).reshape(aux_dev, occ_dev, virt)]
  transfers between devices with their start and end apart: 23 -> 23, of which waited for: 12 -> 12; matrix products, arithmetic and copies ran while one was open for 14% -> 13% of each run, Pallas kernels for 0% -> 0%
where the time goes in v5:
time: 192 us; the launch traced here: 191 us
  waiting for transfers between devices  98.8 us (51%)
  matrix products  31.5 us (16%)
  starting transfers between devices  30.8 us (16%)
  local copies, waits for them, and re-layouts  16.2 us (8%)
  other arithmetic  7.64 us (4%)
  between operations  6.23 us (3%)
    ppermute x8, waiting for transfers between devices, reduce_scatter_rows(): value = keep + lax.ppermute(send, 'aux', pairs)  68 us
    ppermute x12, waiting for transfers between devices, all_gather_rows(): got = lax.ppermute(value, 'aux', pairs)  30.8 us
    ppermute x12, starting transfers between devices, all_gather_rows(): got = lax.ppermute(value, 'aux', pairs)  15.5 us
    ppermute x8, starting transfers between devices, reduce_scatter_rows(): value = keep + lax.ppermute(send, 'aux', pairs)  11 us
    dot_general x1, matrix products, body(): lax.dot_general(factors, factors, contract_p, precision=PREC, preferred_e...  8.79 us
    dot_general x1, matrix products, body(): lax.dot_general(factors, above, contract_p, precision=PREC, preferred_ele...  6.57 us
    dynamic_slice x8, local copies, waits for them, and re-layouts, reduce_scatter_rows(): send = lax.dynamic_slice_in_dim(value, (1 - bit) * half, half, 0)  6.33 us
    add x6, other arithmetic, reduce_scatter_rows(): value = keep + lax.ppermute(send, 'aux', pairs)  6.26 us
  transfers between devices with their start and end apart: 23, of which 12 were waited for; matrix products, arithmetic and copies ran while one was open for 13% of the time, Pallas kernels for 0%

profile of v5, /device:TPU:1, one launch (start us, length us, event | category | flops | bytes accessed | tf_op | source)
XLA Modules:
  0.0 191.2 jit_solution(9050062272120921725)
XLA Ops:
  0.0 0.7 constant_dynamic-slice_fusion.7
  0.7 0.6 fusion.20
  1.3 8.8 %fusion.10 = f32[768,768]{1,0:T(8,128)} fusion(f32[1024,1,768]{2,1,0:T(1,128)} %param.5), kind=kOutput, calls=%fused_computation.10 | convolution fusion | flops 3623878656 | bytes 5505024 | tf_op jit(solution)/shard_map/dot_general | solution.py:106
  10.8 2.5 %constant_dynamic-slice_fusion.6 = f32[384,768]{1,0:T(8,128)} fusion(f32[768,768]{1,0:T(8,128)} %fusion.10, s32[]{:T(128)S(6)} %select_n.33), kind=kLoop, calls=%fused_computation.60 | loop fusion | bytes 2359300 | tf_op jit(solution)/shard_map/dynamic_slice | solution.py:71
  13.3 1.4 collective-permute-start.2
  14.7 4.2 %collective-permute-start = (f32[1024,1,768]{2,1,0:T(1,128)S(1)}, f32[1024,1,768]{2,1,0:T(1,128)}, u32[]{:S(2)}, u32[]{:S(2)}) collective-permute-start(f32[1024,1,768]{2,1,0:T(1,128)S(1)} %copy-done), channel_id=1, source_target_pairs={{0,112},{16,0},{32,16},{48,32},{64,48},{80,64},{96,80},{112,96},{1... | collective-permute-start | bytes 9437192 | tf_op jit(solution)/shard_map/ppermute | solution.py:14
  20.2 2.9 %dynamic-slice_add_fusion = f32[384,768]{1,0:T(8,128)} fusion(f32[384,768]{1,0:T(8,128)} %collective-permute-done.2, f32[768,768]{1,0:T(8,128)} %fusion.10, s32[]{:T(128)S(6)} %select_n.32), kind=kLoop, calls=%fused_computation.23 | loop fusion | flops 294912 | bytes 3538948 | tf_op jit(solution)/shard_map/add | solution.py:72
  23.1 2.0 %constant_dynamic-slice_fusion.5 = f32[192,768]{1,0:T(8,128)} fusion(f32[384,768]{1,0:T(8,128)} %dynamic-slice_add_fusion, s32[]{:T(128)S(6)} %select_n.35), kind=kLoop, calls=%fused_computation.59 | loop fusion | bytes 1179652 | tf_op jit(solution)/shard_map/dynamic_slice | solution.py:71
  25.0 2.5 %collective-permute-start.3 = (f32[192,768]{1,0:T(8,128)}, f32[192,768]{1,0:T(8,128)}, u32[]{:S(2)}, u32[]{:S(2)}) collective-permute-start(f32[192,768]{1,0:T(8,128)} %constant_dynamic-slice_fusion.5), channel_id=1, source_target_pairs={{0,2},{1,7},{2,0},{3,5},{4,6},{5,3},{6,4},{7,1},{8,10},{9,15},{10,... | collective-permute-start | bytes 1769480 | tf_op jit(solution)/shard_map/ppermute | solution.py:72
  28.7 6.9 %collective-permute-done.3 = f32[192,768]{1,0:T(8,128)} collective-permute-done((f32[192,768]{1,0:T(8,128)}, f32[192,768]{1,0:T(8,128)}, u32[]{:S(2)}, u32[]{:S(2)}) %collective-permute-start.3) | collective-permute-done | bytes 589856 | tf_op jit(solution)/shard_map/ppermute | solution.py:72
  35.6 2.1 %dynamic-slice_add_fusion.2 = f32[192,768]{1,0:T(8,128)} fusion(f32[192,768]{1,0:T(8,128)} %collective-permute-done.3, f32[384,768]{1,0:T(8,128)} %dynamic-slice_add_fusion, s32[]{:T(128)S(6)} %select_n.34), kind=kLoop, calls=%fused_computation.25 | loop fusion | flops 147456 | bytes 1769476 | tf_op jit(solution)/shard_map/add | solution.py:72
  37.7 1.7 constant_dynamic-slice_fusion.4
  39.4 0.7 dynamic_slice.71
  42.6 0.6 fusion.21
  43.3 2.3 %collective-permute-done.4 = f32[96,768]{1,0:T(8,128)S(1)} collective-permute-done((f32[96,768]{1,0:T(8,128)}, f32[96,768]{1,0:T(8,128)S(1)}, u32[]{:S(2)}, u32[]{:S(2)}) %collective-permute-start.4) | collective-permute-done | bytes 294944 | tf_op jit(solution)/shard_map/ppermute | solution.py:72
  45.6 1.0 dynamic-slice_add_fusion.4
  46.6 3.6 %collective-permute-start.5 = (f32[48,768]{1,0:T(8,128)S(1)}, f32[48,768]{1,0:T(8,128)S(1)}, u32[]{:S(2)}, u32[]{:S(2)}) collective-permute-start(f32[48,768]{1,0:T(8,128)S(1)} %constant_dynamic-slice_fusion.3), channel_id=1, source_target_pairs={{0,8},{1,9},{2,10},{3,11},{4,12},{5,13},{6,14},{7,15},{8,0},{9,1},... | collective-permute-start | bytes 442376 | tf_op jit(solution)/shard_map/ppermute | solution.py:72
  50.2 1.2 broadcast_subtract_fusion.1
  51.5 44.6 %collective-permute-done.5 = f32[48,768]{1,0:T(8,128)S(1)} collective-permute-done((f32[48,768]{1,0:T(8,128)S(1)}, f32[48,768]{1,0:T(8,128)S(1)}, u32[]{:S(2)}, u32[]{:S(2)}) %collective-permute-start.5) | collective-permute-done | bytes 147488 | tf_op jit(solution)/shard_map/ppermute | solution.py:72
  96.2 6.6 %fusion.5 = f32[768,768]{0,1:T(8,128)S(1)} fusion(f32[1024,1,768]{2,1,0:T(1,128)} %collective-permute-done, f32[1024,1,768]{2,1,0:T(1,128)S(1)} %copy-done), kind=kOutput, calls=%fused_computation.5 | convolution fusion | flops 3623878656 | bytes 8650752 | tf_op jit(solution)/shard_map/dot_general | solution.py:115
  102.9 0.6 collective-permute-start.10
  103.5 2.5 %collective-permute-done.10 = f32[384,768]{1,0:T(8,128)S(1)} collective-permute-done((f32[384,768]{1,0:T(8,128)S(1)}, f32[384,768]{1,0:T(8,128)S(1)}, u32[]{:S(2)}, u32[]{:S(2)}) %collective-permute-start.10) | collective-permute-done | bytes 1179680 | tf_op jit(solution)/shard_map/ppermute | solution.py:72
  105.9 0.1 bitcast_add_fusion.1
  106.2 2.6 %collective-permute-start.11 = (f32[192,768]{1,0:T(8,128)S(1)}, f32[192,768]{1,0:T(8,128)S(1)}, u32[]{:S(2)}, u32[]{:S(2)}) collective-permute-start(f32[192,768]{1,0:T(8,128)S(1)} %constant_dynamic-slice_fusion.2), channel_id=1, source_target_pairs={{0,2},{1,7},{2,0},{3,5},{4,6},{5,3},{6,4},{7,1},{8,10},{9,15},{10,... | collective-permute-start | bytes 1769480 | tf_op jit(solution)/shard_map/ppermute | solution.py:72
  108.7 7.5 %collective-permute-done.11 = f32[192,768]{1,0:T(8,128)S(1)} collective-permute-done((f32[192,768]{1,0:T(8,128)S(1)}, f32[192,768]{1,0:T(8,128)S(1)}, u32[]{:S(2)}, u32[]{:S(2)}) %collective-permute-start.11) | collective-permute-done | bytes 589856 | tf_op jit(solution)/shard_map/ppermute | solution.py:72
  116.3 0.4 collective-permute-start.12
  116.8 1.3 collective-permute-start.7
  118.1 4.2 %collective-permute-done.12 = f32[96,768]{1,0:T(8,128)S(1)} collective-permute-done((f32[96,768]{1,0:T(8,128)S(1)}, f32[96,768]{1,0:T(8,128)S(1)}, u32[]{:S(2)}, u32[]{:S(2)}) %collective-permute-start.12) | collective-permute-done | bytes 294944 | tf_op jit(solution)/shard_map/ppermute | solution.py:72
  122.4 3.0 %collective-permute-done.7 = f32[96,768]{1,0:T(8,128)S(1)} collective-permute-done((f32[96,768]{1,0:T(8,128)S(1)}, f32[96,768]{1,0:T(8,128)S(1)}, u32[]{:S(2)}, u32[]{:S(2)}) %collective-permute-start.7) | collective-permute-done | bytes 294944 | tf_op jit(solution)/shard_map/ppermute | solution.py:80
  125.4 2.6 %collective-permute-start.8 = (f32[192,768]{1,0:T(8,128)S(1)}, f32[192,768]{1,0:T(8,128)S(1)}, u32[]{:S(2)}, u32[]{:S(2)}) collective-permute-start(f32[192,768]{1,0:T(8,128)S(1)} %constant_dynamic-update-slice_fusion.20), channel_id=1, source_target_pairs={{0,2},{1,7},{2,0},{3,5},{4,6},{5,3},{6,4},{7,1},{8,10},{9,15},{10,... | collective-permute-start | bytes 1769480 | tf_op jit(solution)/shard_map/ppermute | solution.py:80
  128.0 0.1 constant_dynamic-update-slice_fusion.15
  128.4 5.3 %collective-permute-done.14 = f32[48,768]{1,0:T(8,128)S(1)} collective-permute-done((f32[48,768]{1,0:T(8,128)S(1)}, f32[48,768]{1,0:T(8,128)S(1)}, u32[]{:S(2)}, u32[]{:S(2)}) %collective-permute-start.14) | collective-permute-done | bytes 147488 | tf_op jit(solution)/shard_map/ppermute | solution.py:80
  133.7 0.3 collective-permute-start.15
  134.0 1.5 collective-permute-done.8
  135.5 7.0 %collective-permute-start.9 = (f32[384,768]{1,0:T(8,128)S(1)}, f32[384,768]{1,0:T(8,128)S(1)}, u32[]{:S(2)}, u32[]{:S(2)}) collective-permute-start(f32[384,768]{1,0:T(8,128)S(1)} %constant_dynamic-update-slice_fusion.18), channel_id=1, source_target_pairs={{0,1},{1,0},{2,3},{3,2},{4,5},{5,4},{6,7},{7,6},{8,9},{9,8},{10,11... | collective-permute-start | bytes 3538952 | tf_op jit(solution)/shard_map/ppermute | solution.py:80
  142.8 0.4 collective-permute-start.16
  143.2 6.4 %collective-permute-done.19 = f32[48,768]{1,0:T(8,128)S(1)} collective-permute-done((f32[48,768]{1,0:T(8,128)S(1)}, f32[48,768]{1,0:T(8,128)S(1)}, u32[]{:S(2)}, u32[]{:S(2)}) %collective-permute-start.19) | collective-permute-done | bytes 147488 | tf_op jit(solution)/shard_map/ppermute | solution.py:80
  149.8 8.9 %collective-permute-done.20 = f32[96,768]{1,0:T(8,128)S(1)} collective-permute-done((f32[96,768]{1,0:T(8,128)S(1)}, f32[96,768]{1,0:T(8,128)S(1)}, u32[]{:S(2)}, u32[]{:S(2)}) %collective-permute-start.20) | collective-permute-done | bytes 294944 | tf_op jit(solution)/shard_map/ppermute | solution.py:80
  158.9 3.4 %collective-permute-start.17 = (f32[384,768]{1,0:T(8,128)S(1)}, f32[384,768]{1,0:T(8,128)S(1)}, u32[]{:S(2)}, u32[]{:S(2)}) collective-permute-start(f32[384,768]{1,0:T(8,128)S(1)} %constant_dynamic-update-slice_fusion.10), channel_id=1, source_target_pairs={{0,1},{1,0},{2,3},{3,2},{4,5},{5,4},{6,7},{7,6},{8,9},{9,8},{10,11... | collective-permute-start | bytes 3538952 | tf_op jit(solution)/shard_map/ppermute | solution.py:80
  162.4 0.2 broadcast.21.clone.1
  162.9 5.8 %collective-permute-done.21 = f32[192,768]{1,0:T(8,128)S(1)} collective-permute-done((f32[192,768]{1,0:T(8,128)S(1)}, f32[192,768]{1,0:T(8,128)S(1)}, u32[]{:S(2)}, u32[]{:S(2)}) %collective-permute-start.21) | collective-permute-done | bytes 589856 | tf_op jit(solution)/shard_map/ppermute | solution.py:80
  168.7 0.3 collective-permute-start.22
  169.0 4.0 %fusion.8 = f32[768,1024]{1,0:T(8,128)S(1)} fusion(f32[768,768]{1,0:T(8,128)S(1)} %constant_dynamic-update-slice_fusion.16, f32[1024,1,768]{2,1,0:T(1,128)S(1)} %copy-done), kind=kOutput, calls=%fused_computation.8 | convolution fusion | flops 3623878656 | bytes 8650752 | tf_op jit(solution)/shard_map/dot_general | solution.py:112
  173.0 0.2 broadcast.21.clone
  173.3 0.2 broadcast.21.clone.2
  173.6 5.9 %fusion.3 = f32[1024,768]{0,1:T(8,128)S(1)} fusion(f32[768,768]{1,0:T(8,128)S(1)} %constant_dynamic-update-slice_fusion.8, f32[1024,1,768]{2,1,0:T(1,128)} %collective-permute-done), kind=kOutput, calls=%fused_computation.3 | convolution fusion | flops 3623878656 | bytes 8650752 | tf_op jit(solution)/shard_map/dot_general | solution.py:122
  179.7 6.2 %fusion.14 = f32[1024,1,768]{0,2,1:T(8,128)S(1)} fusion(f32[1024,768]{0,1:T(8,128)S(1)} %fusion.3, f32[768,1024]{1,0:T(8,128)S(1)} %fusion.8, f32[768,768]{1,0:T(8,128)S(1)} %constant_dynamic-update-slice_fusion, f32[1024,1,768]{2,1,0:T(1,128)} %collective-permute-done.1), kind=kOutput, calls=%fused_computation.15 | convolution fusion | flops 3626237952 | bytes 14942208 | tf_op jit(solution)/shard_map/dot_general | solution.py:124
  185.9 5.3 %copy.8 = f32[1024,1,768]{2,1,0:T(1,128)} copy(f32[1024,1,768]{0,2,1:T(8,128)S(1)} %fusion.14) | data formatting | bytes 6291456 | tf_op jit(solution)/shard_map/mul | solution.py:127
  (69 shorter events, 2.5 us)
Async XLA Ops:
  1.3 13.3 %copy-start = (f32[1024,1,768]{2,1,0:T(1,128)S(1)}, f32[1024,1,768]{2,1,0:T(1,128)}, u32[]{:S(2)}) copy-start(f32[1024,1,768]{2,1,0:T(1,128)} %param.5) | copy-start | bytes 9437188
  13.3 6.9 %collective-permute-start.2 = (f32[384,768]{1,0:T(8,128)}, f32[384,768]{1,0:T(8,128)}, u32[]{:S(2)}, u32[]{:S(2)}) collective-permute-start(f32[384,768]{1,0:T(8,128)} %constant_dynamic-slice_fusion.6), channel_id=1, source_target_pairs={{0,1},{1,0},{2,3},{3,2},{4,5},{5,4},{6,7},{7,6},{8,9},{9,8},{10,11... | collective-permute-start | bytes 3538952 | tf_op jit(solution)/shard_map/ppermute | solution.py:72
  14.7 81.6 %collective-permute-start = (f32[1024,1,768]{2,1,0:T(1,128)S(1)}, f32[1024,1,768]{2,1,0:T(1,128)}, u32[]{:S(2)}, u32[]{:S(2)}) collective-permute-start(f32[1024,1,768]{2,1,0:T(1,128)S(1)} %copy-done), channel_id=1, source_target_pairs={{0,112},{16,0},{32,16},{48,32},{64,48},{80,64},{96,80},{112,96},{1... | collective-permute-start | bytes 9437192 | tf_op jit(solution)/shard_map/ppermute | solution.py:14
  18.9 77.4 %collective-permute-start.1 = (f32[1024,1,768]{2,1,0:T(1,128)S(1)}, f32[1024,1,768]{2,1,0:T(1,128)}, u32[]{:S(2)}, u32[]{:S(2)}) collective-permute-start(f32[1024,1,768]{2,1,0:T(1,128)S(1)} %copy-done), channel_id=1, source_target_pairs={{0,16},{16,32},{32,48},{48,64},{64,80},{80,96},{96,112},{112,0},{1... | collective-permute-start | bytes 9437192 | tf_op jit(solution)/shard_map/ppermute | solution.py:14
  23.1 16.4 %copy-start.3 = (s32[16]{0:T(128)S(1)}, s32[16]{0:T(128)}, u32[]{:S(2)}) copy-start(s32[16]{0:T(128)} %constant.68.clone) | copy-start | bytes 196
  23.1 19.6 %copy-start.2 = (f32[8]{0:T(128)S(1)}, f32[8]{0:T(128)}, u32[]{:S(2)}) copy-start(f32[8]{0:T(128)} %param.6) | copy-start | bytes 100
  23.1 27.1 %copy-start.1 = (f32[768]{0:T(1024)S(1)}, f32[768]{0:T(1024)}, u32[]{:S(2)}) copy-start(f32[768]{0:T(1024)} %param.7) | copy-start | bytes 9220
  25.0 10.6 %collective-permute-start.3 = (f32[192,768]{1,0:T(8,128)}, f32[192,768]{1,0:T(8,128)}, u32[]{:S(2)}, u32[]{:S(2)}) collective-permute-start(f32[192,768]{1,0:T(8,128)} %constant_dynamic-slice_fusion.5), channel_id=1, source_target_pairs={{0,2},{1,7},{2,0},{3,5},{4,6},{5,3},{6,4},{7,1},{8,10},{9,15},{10,... | collective-permute-start | bytes 1769480 | tf_op jit(solution)/shard_map/ppermute | solution.py:72
  39.4 6.2 %collective-permute-start.4 = (f32[96,768]{1,0:T(8,128)}, f32[96,768]{1,0:T(8,128)S(1)}, u32[]{:S(2)}, u32[]{:S(2)}) collective-permute-start(f32[96,768]{1,0:T(8,128)} %constant_dynamic-slice_fusion.4), channel_id=1, source_target_pairs={{0,6},{1,3},{2,4},{3,1},{4,2},{5,7},{6,0},{7,5},{8,14},{9,11},{10,... | collective-permute-start | bytes 884744 | tf_op jit(solution)/shard_map/ppermute | solution.py:72
  46.6 49.5 %collective-permute-start.5 = (f32[48,768]{1,0:T(8,128)S(1)}, f32[48,768]{1,0:T(8,128)S(1)}, u32[]{:S(2)}, u32[]{:S(2)}) collective-permute-start(f32[48,768]{1,0:T(8,128)S(1)} %constant_dynamic-slice_fusion.3), channel_id=1, source_target_pairs={{0,8},{1,9},{2,10},{3,11},{4,12},{5,13},{6,14},{7,15},{8,0},{9,1},... | collective-permute-start | bytes 442376 | tf_op jit(solution)/shard_map/ppermute | solution.py:72
  102.9 3.0 %collective-permute-start.10 = (f32[384,768]{1,0:T(8,128)S(1)}, f32[384,768]{1,0:T(8,128)S(1)}, u32[]{:S(2)}, u32[]{:S(2)}) collective-permute-start(f32[384,768]{1,0:T(8,128)S(1)} %dynamic-slice_bitcast_fusion), channel_id=1, source_target_pairs={{0,1},{1,0},{2,3},{3,2},{4,5},{5,4},{6,7},{7,6},{8,9},{9,8},{10,11... | collective-permute-start | bytes 3538952 | tf_op jit(solution)/shard_map/ppermute | solution.py:72
  106.2 10.0 %collective-permute-start.11 = (f32[192,768]{1,0:T(8,128)S(1)}, f32[192,768]{1,0:T(8,128)S(1)}, u32[]{:S(2)}, u32[]{:S(2)}) collective-permute-start(f32[192,768]{1,0:T(8,128)S(1)} %constant_dynamic-slice_fusion.2), channel_id=1, source_target_pairs={{0,2},{1,7},{2,0},{3,5},{4,6},{5,3},{6,4},{7,1},{8,10},{9,15},{10,... | collective-permute-start | bytes 1769480 | tf_op jit(solution)/shard_map/ppermute | solution.py:72
  108.7 8.0 %collective-permute-start.6 = (f32[48,768]{1,0:T(8,128)S(1)}, f32[48,768]{1,0:T(8,128)S(1)}, u32[]{:S(2)}, u32[]{:S(2)}) collective-permute-start(f32[48,768]{1,0:T(8,128)S(1)} %add_divide_fusion.1), channel_id=1, source_target_pairs={{0,8},{1,9},{2,10},{3,11},{4,12},{5,13},{6,14},{7,15},{8,0},{9,1},... | collective-permute-start | bytes 442376 | tf_op jit(solution)/shard_map/ppermute | solution.py:80
  116.3 5.9 %collective-permute-start.12 = (f32[96,768]{1,0:T(8,128)S(1)}, f32[96,768]{1,0:T(8,128)S(1)}, u32[]{:S(2)}, u32[]{:S(2)}) collective-permute-start(f32[96,768]{1,0:T(8,128)S(1)} %constant_dynamic-slice_fusion.1), channel_id=1, source_target_pairs={{0,6},{1,3},{2,4},{3,1},{4,2},{5,7},{6,0},{7,5},{8,14},{9,11},{10,... | collective-permute-start | bytes 884744 | tf_op jit(solution)/shard_map/ppermute | solution.py:72
  116.8 8.6 %collective-permute-start.7 = (f32[96,768]{1,0:T(8,128)S(1)}, f32[96,768]{1,0:T(8,128)S(1)}, u32[]{:S(2)}, u32[]{:S(2)}) collective-permute-start(f32[96,768]{1,0:T(8,128)S(1)} %constant_dynamic-update-slice_fusion.22), channel_id=1, source_target_pairs={{0,6},{1,3},{2,4},{3,1},{4,2},{5,7},{6,0},{7,5},{8,14},{9,11},{10,... | collective-permute-start | bytes 884744 | tf_op jit(solution)/shard_map/ppermute | solution.py:80
  122.3 5.7 %collective-permute-start.13 = (f32[48,768]{1,0:T(8,128)S(1)}, f32[48,768]{1,0:T(8,128)S(1)}, u32[]{:S(2)}, u32[]{:S(2)}) collective-permute-start(f32[48,768]{1,0:T(8,128)S(1)} %constant_dynamic-slice_fusion), channel_id=1, source_target_pairs={{0,8},{1,9},{2,10},{3,11},{4,12},{5,13},{6,14},{7,15},{8,0},{9,1},... | collective-permute-start | bytes 442376 | tf_op jit(solution)/shard_map/ppermute | solution.py:72
  125.4 10.0 %collective-permute-start.8 = (f32[192,768]{1,0:T(8,128)S(1)}, f32[192,768]{1,0:T(8,128)S(1)}, u32[]{:S(2)}, u32[]{:S(2)}) collective-permute-start(f32[192,768]{1,0:T(8,128)S(1)} %constant_dynamic-update-slice_fusion.20), channel_id=1, source_target_pairs={{0,2},{1,7},{2,0},{3,5},{4,6},{5,3},{6,4},{7,1},{8,10},{9,15},{10,... | collective-permute-start | bytes 1769480 | tf_op jit(solution)/shard_map/ppermute | solution.py:80
  128.1 5.6 %collective-permute-start.14 = (f32[48,768]{1,0:T(8,128)S(1)}, f32[48,768]{1,0:T(8,128)S(1)}, u32[]{:S(2)}, u32[]{:S(2)}) collective-permute-start(f32[48,768]{1,0:T(8,128)S(1)} %get-tuple-element.12), channel_id=1, source_target_pairs={{0,8},{1,9},{2,10},{3,11},{4,12},{5,13},{6,14},{7,15},{8,0},{9,1},... | collective-permute-start | bytes 442376 | tf_op jit(solution)/shard_map/ppermute | solution.py:80
  128.4 14.2 %collective-permute-start.18 = (f32[48,768]{1,0:T(8,128)S(1)}, f32[48,768]{1,0:T(8,128)S(1)}, u32[]{:S(2)}, u32[]{:S(2)}) collective-permute-start(f32[48,768]{1,0:T(8,128)S(1)} %get-tuple-element.12), channel_id=1, source_target_pairs={{0,16},{16,32},{32,48},{48,64},{64,80},{80,96},{96,112},{112,0},{1... | collective-permute-start | bytes 442376 | tf_op jit(solution)/shard_map/ppermute | solution.py:14
  133.7 9.0 %collective-permute-start.15 = (f32[96,768]{1,0:T(8,128)S(1)}, f32[96,768]{1,0:T(8,128)S(1)}, u32[]{:S(2)}, u32[]{:S(2)}) collective-permute-start(f32[96,768]{1,0:T(8,128)S(1)} %constant_dynamic-update-slice_fusion.14), channel_id=1, source_target_pairs={{0,6},{1,3},{2,4},{3,1},{4,2},{5,7},{6,0},{7,5},{8,14},{9,11},{10,... | collective-permute-start | bytes 884744 | tf_op jit(solution)/shard_map/ppermute | solution.py:80
  135.5 27.1 %collective-permute-start.9 = (f32[384,768]{1,0:T(8,128)S(1)}, f32[384,768]{1,0:T(8,128)S(1)}, u32[]{:S(2)}, u32[]{:S(2)}) collective-permute-start(f32[384,768]{1,0:T(8,128)S(1)} %constant_dynamic-update-slice_fusion.18), channel_id=1, source_target_pairs={{0,1},{1,0},{2,3},{3,2},{4,5},{5,4},{6,7},{7,6},{8,9},{9,8},{10,11... | collective-permute-start | bytes 3538952 | tf_op jit(solution)/shard_map/ppermute | solution.py:80
  142.6 7.0 %collective-permute-start.19 = (f32[48,768]{1,0:T(8,128)S(1)}, f32[48,768]{1,0:T(8,128)S(1)}, u32[]{:S(2)}, u32[]{:S(2)}) collective-permute-start(f32[48,768]{1,0:T(8,128)S(1)} %collective-permute-done.18), channel_id=1, source_target_pairs={{0,8},{1,9},{2,10},{3,11},{4,12},{5,13},{6,14},{7,15},{8,0},{9,1},... | collective-permute-start | bytes 442376 | tf_op jit(solution)/shard_map/ppermute | solution.py:80
  142.8 16.1 %collective-permute-start.16 = (f32[192,768]{1,0:T(8,128)S(1)}, f32[192,768]{1,0:T(8,128)S(1)}, u32[]{:S(2)}, u32[]{:S(2)}) collective-permute-start(f32[192,768]{1,0:T(8,128)S(1)} %constant_dynamic-update-slice_fusion.12), channel_id=1, source_target_pairs={{0,2},{1,7},{2,0},{3,5},{4,6},{5,3},{6,4},{7,1},{8,10},{9,15},{10,... | collective-permute-start | bytes 1769480 | tf_op jit(solution)/shard_map/ppermute | solution.py:80
  149.6 9.0 %collective-permute-start.20 = (f32[96,768]{1,0:T(8,128)S(1)}, f32[96,768]{1,0:T(8,128)S(1)}, u32[]{:S(2)}, u32[]{:S(2)}) collective-permute-start(f32[96,768]{1,0:T(8,128)S(1)} %constant_dynamic-update-slice_fusion.6), channel_id=1, source_target_pairs={{0,6},{1,3},{2,4},{3,1},{4,2},{5,7},{6,0},{7,5},{8,14},{9,11},{10,... | collective-permute-start | bytes 884744 | tf_op jit(solution)/shard_map/ppermute | solution.py:80
  158.6 10.0 %collective-permute-start.21 = (f32[192,768]{1,0:T(8,128)S(1)}, f32[192,768]{1,0:T(8,128)S(1)}, u32[]{:S(2)}, u32[]{:S(2)}) collective-permute-start(f32[192,768]{1,0:T(8,128)S(1)} %constant_dynamic-update-slice_fusion.4), channel_id=1, source_target_pairs={{0,2},{1,7},{2,0},{3,5},{4,6},{5,3},{6,4},{7,1},{8,10},{9,15},{10,... | collective-permute-start | bytes 1769480 | tf_op jit(solution)/shard_map/ppermute | solution.py:80
  158.9 14.6 %collective-permute-start.17 = (f32[384,768]{1,0:T(8,128)S(1)}, f32[384,768]{1,0:T(8,128)S(1)}, u32[]{:S(2)}, u32[]{:S(2)}) collective-permute-start(f32[384,768]{1,0:T(8,128)S(1)} %constant_dynamic-update-slice_fusion.10), channel_id=1, source_target_pairs={{0,1},{1,0},{2,3},{3,2},{4,5},{5,4},{6,7},{7,6},{8,9},{9,8},{10,11... | collective-permute-start | bytes 3538952 | tf_op jit(solution)/shard_map/ppermute | solution.py:80
  168.7 10.9 %collective-permute-start.22 = (f32[384,768]{1,0:T(8,128)S(1)}, f32[384,768]{1,0:T(8,128)S(1)}, u32[]{:S(2)}, u32[]{:S(2)}) collective-permute-start(f32[384,768]{1,0:T(8,128)S(1)} %constant_dynamic-update-slice_fusion.2), channel_id=1, source_target_pairs={{0,1},{1,0},{2,3},{3,2},{4,5},{5,4},{6,7},{7,6},{8,9},{9,8},{10,11... | collective-permute-start | bytes 3538952 | tf_op jit(solution)/shard_map/ppermute | solution.py:80

commit v6 on v0

--- a/solution.py
+++ b/solution.py
@@ -108,18 +108,25 @@
                            preferred_element_type=jnp.float32)
     diag_share = reduce_scatter_rows(diag, stages, bits)
     diag_amp = diag_share / (my_vals[:, None] + own_vals[None, :])
+    above, below, diag_amp = lax.optimization_barrier((above, below, diag_amp))
     diag_full = all_gather_rows(diag_amp, stages, bits)
     t_own = lax.dot_general(own, diag_full, contract_b, precision=PREC,
                             preferred_element_type=jnp.float32)
-    above, below, t_own = lax.optimization_barrier((above, below, t_own))
 
     up = lax.dot_general(own, above, contract_p, precision=PREC,
                          preferred_element_type=jnp.float32)
     up_share = reduce_scatter_rows(up, stages, bits)
     up_amp = up_share / (my_vals[:, None] + up_vals[None, :])
-    prev_amp = passed_along(up_amp, "occ", 1)
+    z_pairs = [(i, j) for i, (j, _) in enumerate(stages[-1])]
+    across = [(g * aux_count + i, ((g + 1) % groups) * aux_count + j)
+              for g in range(groups) for i, j in z_pairs]
+    prev_mine = passed_along(up_amp, "occ", 1)
+    prev_pair = lax.ppermute(up_amp, ("occ", "aux"), across)
+    prev_two = jnp.zeros((2 * rows,) + up_amp.shape[1:], up_amp.dtype)
+    prev_two = lax.dynamic_update_slice_in_dim(prev_two, prev_mine, bits[-1] * rows, 0)
+    prev_two = lax.dynamic_update_slice_in_dim(prev_two, prev_pair, (1 - bits[-1]) * rows, 0)
     up_full = all_gather_rows(up_amp, stages, bits)
-    prev_full = all_gather_rows(prev_amp, stages, bits)
+    prev_full = all_gather_rows(prev_two, stages[:-1], bits[:-1])
     t_up = lax.dot_general(above, up_full, contract_b, precision=PREC,
                            preferred_element_type=jnp.float32)
     t_prev = lax.dot_general(below, prev_full, (((1,), (0,)), ((), ())),

time: 233 us -> 192 us (0.82)
  waiting for transfers between devices: 127 us -> 102 us
  starting transfers between devices: 50.9 us -> 29.3 us
  local copies, waits for them, and re-layouts: 17.3 us -> 20.4 us
    ppermute x8, waiting for transfers between devices: 93.3 us -> 67.9 us  [reduce_scatter_rows(): value = keep + lax.ppermute(send, 'aux', pairs)]
    ppermute x12 -> x11, starting transfers between devices: 35.9 us -> 14 us  [all_gather_rows(): got = lax.ppermute(value, 'aux', pairs)]
    ppermute x0 -> x1, waiting for transfers between devices: none -> 8.07 us  [body(): prev_pair = lax.ppermute(up_amp, ('occ', 'aux'), across)]
    ppermute x12 -> x11, waiting for transfers between devices: 33.4 us -> 26 us  [all_gather_rows(): got = lax.ppermute(value, 'aux', pairs)]
    dynamic_slice x8, local copies, waits for them, and re-layouts: 1.84 us -> 6.33 us  [reduce_scatter_rows(): send = lax.dynamic_slice_in_dim(value, (1 - bit) * half, half, 0)]
    unnamed x14 -> x10, local copies, waits for them, and re-layouts: 5.49 us -> 4.2 us
  transfers between devices with their start and end apart: 23 -> 23, of which waited for: 15 -> 12; matrix products, arithmetic and copies ran while one was open for 7% -> 13% of each run, Pallas kernels for 0% -> 0%
where the time goes in v6:
time: 192 us
  waiting for transfers between devices  102 us (53%)
  starting transfers between devices  29.3 us (15%)
  matrix products  26 us (14%)
  local copies, waits for them, and re-layouts  20.4 us (11%)
  other arithmetic  7.63 us (4%)
  between operations  6.28 us (3%)
    ppermute x8, waiting for transfers between devices, reduce_scatter_rows(): value = keep + lax.ppermute(send, 'aux', pairs)  67.9 us
    ppermute x11, waiting for transfers between devices, all_gather_rows(): got = lax.ppermute(value, 'aux', pairs)  26 us
    ppermute x11, starting transfers between devices, all_gather_rows(): got = lax.ppermute(value, 'aux', pairs)  14 us
    ppermute x8, starting transfers between devices, reduce_scatter_rows(): value = keep + lax.ppermute(send, 'aux', pairs)  11 us
    dot_general x1, matrix products, body(): lax.dot_general(own, own, contract_p, precision=PREC, preferred_element_t...  8.79 us
    ppermute x1, waiting for transfers between devices, body(): prev_pair = lax.ppermute(up_amp, ('occ', 'aux'), across)  8.07 us
    dynamic_slice x8, local copies, waits for them, and re-layouts, reduce_scatter_rows(): send = lax.dynamic_slice_in_dim(value, (1 - bit) * half, half, 0)  6.33 us
    add x6, other arithmetic, reduce_scatter_rows(): value = keep + lax.ppermute(send, 'aux', pairs)  6.26 us
  transfers between devices with their start and end apart: 23, of which 12 were waited for; matrix products, arithmetic and copies ran while one was open for 13% of the time, Pallas kernels for 0%

profile of v6, /device:TPU:1, one launch (start us, length us, event | category | flops | bytes accessed | tf_op | source)
XLA Modules:
  0.0 191.6 jit_solution(14513424701721212641)
XLA Ops:
  0.0 8.8 %fusion.4 = f32[768,768]{1,0:T(8,128)} fusion(f32[1024,1,768]{2,1,0:T(1,128)} %param.5), kind=kOutput, calls=%fused_computation.4 | convolution fusion | flops 3623878656 | bytes 5505024 | tf_op jit(solution)/shard_map/dot_general | solution.py:107
  8.8 0.7 constant_dynamic-slice_fusion.7
  9.5 0.6 fusion.13
  10.8 2.5 %constant_dynamic-slice_fusion.6 = f32[384,768]{1,0:T(8,128)} fusion(f32[768,768]{1,0:T(8,128)} %fusion.4, s32[]{:T(128)S(6)} %select_n.33), kind=kLoop, calls=%fused_computation.54 | loop fusion | bytes 2359300 | tf_op jit(solution)/shard_map/dynamic_slice | solution.py:71
  13.3 1.4 collective-permute-start.2
  14.7 4.2 %collective-permute-start = (f32[1024,1,768]{2,1,0:T(1,128)S(1)}, f32[1024,1,768]{2,1,0:T(1,128)}, u32[]{:S(2)}, u32[]{:S(2)}) collective-permute-start(f32[1024,1,768]{2,1,0:T(1,128)S(1)} %copy-done), channel_id=1, source_target_pairs={{0,112},{16,0},{32,16},{48,32},{64,48},{80,64},{96,80},{112,96},{1... | collective-permute-start | bytes 9437192 | tf_op jit(solution)/shard_map/ppermute | solution.py:14
  20.2 2.9 %dynamic-slice_add_fusion = f32[384,768]{1,0:T(8,128)} fusion(f32[384,768]{1,0:T(8,128)} %collective-permute-done.2, f32[768,768]{1,0:T(8,128)} %fusion.4, s32[]{:T(128)S(6)} %select_n.32), kind=kLoop, calls=%fused_computation.17 | loop fusion | flops 294912 | bytes 3538948 | tf_op jit(solution)/shard_map/add | solution.py:72
  23.1 2.0 %constant_dynamic-slice_fusion.5 = f32[192,768]{1,0:T(8,128)} fusion(f32[384,768]{1,0:T(8,128)} %dynamic-slice_add_fusion, s32[]{:T(128)S(6)} %select_n.35), kind=kLoop, calls=%fused_computation.53 | loop fusion | bytes 1179652 | tf_op jit(solution)/shard_map/dynamic_slice | solution.py:71
  25.0 2.5 %collective-permute-start.3 = (f32[192,768]{1,0:T(8,128)}, f32[192,768]{1,0:T(8,128)}, u32[]{:S(2)}, u32[]{:S(2)}) collective-permute-start(f32[192,768]{1,0:T(8,128)} %constant_dynamic-slice_fusion.5), channel_id=1, source_target_pairs={{0,2},{1,7},{2,0},{3,5},{4,6},{5,3},{6,4},{7,1},{8,10},{9,15},{10,... | collective-permute-start | bytes 1769480 | tf_op jit(solution)/shard_map/ppermute | solution.py:72
  28.7 6.9 %collective-permute-done.3 = f32[192,768]{1,0:T(8,128)} collective-permute-done((f32[192,768]{1,0:T(8,128)}, f32[192,768]{1,0:T(8,128)}, u32[]{:S(2)}, u32[]{:S(2)}) %collective-permute-start.3) | collective-permute-done | bytes 589856 | tf_op jit(solution)/shard_map/ppermute | solution.py:72
  35.6 2.1 %dynamic-slice_add_fusion.2 = f32[192,768]{1,0:T(8,128)} fusion(f32[192,768]{1,0:T(8,128)} %collective-permute-done.3, f32[384,768]{1,0:T(8,128)} %dynamic-slice_add_fusion, s32[]{:T(128)S(6)} %select_n.34), kind=kLoop, calls=%fused_computation.19 | loop fusion | flops 147456 | bytes 1769476 | tf_op jit(solution)/shard_map/add | solution.py:72
  37.7 1.7 constant_dynamic-slice_fusion.4
  41.3 0.7 dynamic_slice.71
  42.7 0.6 fusion.12
  43.3 2.3 %collective-permute-done.4 = f32[96,768]{1,0:T(8,128)S(1)} collective-permute-done((f32[96,768]{1,0:T(8,128)}, f32[96,768]{1,0:T(8,128)S(1)}, u32[]{:S(2)}, u32[]{:S(2)}) %collective-permute-start.4) | collective-permute-done | bytes 294944 | tf_op jit(solution)/shard_map/ppermute | solution.py:72
  45.6 1.0 dynamic-slice_add_fusion.4
  46.6 3.6 %collective-permute-start.5 = (f32[48,768]{1,0:T(8,128)S(1)}, f32[48,768]{1,0:T(8,128)S(1)}, u32[]{:S(2)}, u32[]{:S(2)}) collective-permute-start(f32[48,768]{1,0:T(8,128)S(1)} %constant_dynamic-slice_fusion.3), channel_id=1, source_target_pairs={{0,8},{1,9},{2,10},{3,11},{4,12},{5,13},{6,14},{7,15},{8,0},{9,1},... | collective-permute-start | bytes 442376 | tf_op jit(solution)/shard_map/ppermute | solution.py:72
  50.2 1.2 broadcast_subtract_fusion
  51.5 44.6 %collective-permute-done.5 = f32[48,768]{1,0:T(8,128)S(1)} collective-permute-done((f32[48,768]{1,0:T(8,128)S(1)}, f32[48,768]{1,0:T(8,128)S(1)}, u32[]{:S(2)}, u32[]{:S(2)}) %collective-permute-start.5) | collective-permute-done | bytes 147488 | tf_op jit(solution)/shard_map/ppermute | solution.py:72
  96.2 2.1 %copy.29 = f32[1024,1,768]{2,0,1:T(8,128)S(1)} copy(f32[1024,1,768]{2,1,0:T(1,128)} %collective-permute-done) | data formatting | bytes 6291456
  98.3 2.1 %copy.28 = f32[1024,1,768]{2,0,1:T(8,128)S(1)} copy(f32[1024,1,768]{2,1,0:T(1,128)} %collective-permute-done.1) | data formatting | bytes 6291456
  100.4 4.8 %fusion = f32[768,768]{0,1:T(8,128)S(1)} fusion(f32[1024,768]{1,0:T(8,128)S(1)} %bitcast.44, f32[1024,1,768]{2,1,0:T(1,128)S(1)} %copy-done), kind=kOutput, calls=%fused_computation | convolution fusion | flops 3623878656 | bytes 8650752 | tf_op jit(solution)/shard_map/dot_general | solution.py:116
  105.3 0.6 collective-permute-start.10
  105.9 2.5 %collective-permute-done.10 = f32[384,768]{1,0:T(8,128)S(1)} collective-permute-done((f32[384,768]{1,0:T(8,128)S(1)}, f32[384,768]{1,0:T(8,128)S(1)}, u32[]{:S(2)}, u32[]{:S(2)}) %collective-permute-start.10) | collective-permute-done | bytes 1179680 | tf_op jit(solution)/shard_map/ppermute | solution.py:72
  108.5 2.6 %collective-permute-start.11 = (f32[192,768]{1,0:T(8,128)S(1)}, f32[192,768]{1,0:T(8,128)S(1)}, u32[]{:S(2)}, u32[]{:S(2)}) collective-permute-start(f32[192,768]{1,0:T(8,128)S(1)} %constant_dynamic-slice_fusion.2), channel_id=1, source_target_pairs={{0,2},{1,7},{2,0},{3,5},{4,6},{5,3},{6,4},{7,1},{8,10},{9,15},{10,... | collective-permute-start | bytes 1769480 | tf_op jit(solution)/shard_map/ppermute | solution.py:72
  111.1 7.5 %collective-permute-done.11 = f32[192,768]{1,0:T(8,128)S(1)} collective-permute-done((f32[192,768]{1,0:T(8,128)S(1)}, f32[192,768]{1,0:T(8,128)S(1)}, u32[]{:S(2)}, u32[]{:S(2)}) %collective-permute-start.11) | collective-permute-done | bytes 589856 | tf_op jit(solution)/shard_map/ppermute | solution.py:72
  118.7 0.4 collective-permute-start.12
  119.2 1.3 collective-permute-start.7
  120.5 4.2 %collective-permute-done.12 = f32[96,768]{1,0:T(8,128)S(1)} collective-permute-done((f32[96,768]{1,0:T(8,128)S(1)}, f32[96,768]{1,0:T(8,128)S(1)}, u32[]{:S(2)}, u32[]{:S(2)}) %collective-permute-start.12) | collective-permute-done | bytes 294944 | tf_op jit(solution)/shard_map/ppermute | solution.py:72
  124.8 3.0 %collective-permute-done.7 = f32[96,768]{1,0:T(8,128)S(1)} collective-permute-done((f32[96,768]{1,0:T(8,128)S(1)}, f32[96,768]{1,0:T(8,128)S(1)}, u32[]{:S(2)}, u32[]{:S(2)}) %collective-permute-start.7) | collective-permute-done | bytes 294944 | tf_op jit(solution)/shard_map/ppermute | solution.py:80
  127.8 2.6 %collective-permute-start.8 = (f32[192,768]{1,0:T(8,128)S(1)}, f32[192,768]{1,0:T(8,128)S(1)}, u32[]{:S(2)}, u32[]{:S(2)}) collective-permute-start(f32[192,768]{1,0:T(8,128)S(1)} %constant_dynamic-update-slice_fusion.20), channel_id=1, source_target_pairs={{0,2},{1,7},{2,0},{3,5},{4,6},{5,3},{6,4},{7,1},{8,10},{9,15},{10,... | collective-permute-start | bytes 1769480 | tf_op jit(solution)/shard_map/ppermute | solution.py:80
  130.8 5.3 %collective-permute-done.14 = f32[48,768]{1,0:T(8,128)S(1)} collective-permute-done((f32[48,768]{1,0:T(8,128)S(1)}, f32[48,768]{1,0:T(8,128)S(1)}, u32[]{:S(2)}, u32[]{:S(2)}) %collective-permute-start.14) | collective-permute-done | bytes 147488 | tf_op jit(solution)/shard_map/ppermute | solution.py:80
  136.1 0.3 collective-permute-start.15
  136.4 1.5 collective-permute-done.8
  137.9 7.0 %collective-permute-start.9 = (f32[384,768]{1,0:T(8,128)S(1)}, f32[384,768]{1,0:T(8,128)S(1)}, u32[]{:S(2)}, u32[]{:S(2)}) collective-permute-start(f32[384,768]{1,0:T(8,128)S(1)} %constant_dynamic-update-slice_fusion.18), channel_id=1, source_target_pairs={{0,1},{1,0},{2,3},{3,2},{4,5},{5,4},{6,7},{7,6},{8,9},{9,8},{10,11... | collective-permute-start | bytes 3538952 | tf_op jit(solution)/shard_map/ppermute | solution.py:80
  145.1 0.4 collective-permute-start.16
  145.5 8.1 %collective-permute-done.19 = f32[48,768]{1,0:T(8,128)S(1)} collective-permute-done((f32[48,768]{1,0:T(8,128)S(1)}, f32[48,768]{1,0:T(8,128)S(1)}, u32[]{:S(2)}, u32[]{:S(2)}) %collective-permute-start.19) | collective-permute-done | bytes 147488 | tf_op jit(solution)/shard_map/ppermute | solution.py:124
  153.7 8.9 %collective-permute-done.20 = f32[96,768]{1,0:T(8,128)S(1)} collective-permute-done((f32[96,768]{1,0:T(8,128)S(1)}, f32[96,768]{1,0:T(8,128)S(1)}, u32[]{:S(2)}, u32[]{:S(2)}) %collective-permute-start.20) | collective-permute-done | bytes 294944 | tf_op jit(solution)/shard_map/ppermute | solution.py:80
  163.0 1.9 %collective-permute-start.17 = (f32[384,768]{1,0:T(8,128)S(1)}, f32[384,768]{1,0:T(8,128)S(1)}, u32[]{:S(2)}, u32[]{:S(2)}) collective-permute-start(f32[384,768]{1,0:T(8,128)S(1)} %constant_dynamic-update-slice_fusion.10), channel_id=1, source_target_pairs={{0,1},{1,0},{2,3},{3,2},{4,5},{5,4},{6,7},{7,6},{8,9},{9,8},{10,11... | collective-permute-start | bytes 3538952 | tf_op jit(solution)/shard_map/ppermute | solution.py:80
  164.9 0.2 broadcast.20.clone.1
  165.4 7.3 %collective-permute-done.21 = f32[192,768]{1,0:T(8,128)S(1)} collective-permute-done((f32[192,768]{1,0:T(8,128)S(1)}, f32[192,768]{1,0:T(8,128)S(1)}, u32[]{:S(2)}, u32[]{:S(2)}) %collective-permute-start.21) | collective-permute-done | bytes 589856 | tf_op jit(solution)/shard_map/ppermute | solution.py:80
  172.8 0.3 collective-permute-start.22
  173.1 4.0 %fusion.2 = f32[768,1024]{1,0:T(8,128)S(1)} fusion(f32[768,768]{1,0:T(8,128)S(1)} %constant_dynamic-update-slice_fusion.16, f32[1024,1,768]{2,1,0:T(1,128)S(1)} %copy-done), kind=kOutput, calls=%fused_computation.2 | convolution fusion | flops 3623878656 | bytes 8650752 | tf_op jit(solution)/shard_map/dot_general | solution.py:113
  177.1 0.2 broadcast.20.clone
  177.3 0.2 broadcast.20.clone.2
  177.7 4.1 %fusion.14 = f32[1024,768]{0,1:T(8,128)S(1)} fusion(f32[1024,768]{1,0:T(8,128)S(1)} %bitcast.45, f32[768,768]{1,0:T(8,128)S(1)} %constant_dynamic-update-slice_fusion.8), kind=kOutput, calls=%fused_computation.60 | convolution fusion | flops 3623878656 | bytes 8650752 | tf_op jit(solution)/shard_map/dot_general | solution.py:130
  181.9 4.3 %fusion.8 = f32[1024,1,768]{0,2,1:T(8,128)S(1)} fusion(f32[1024,768]{0,1:T(8,128)S(1)} %fusion.14, f32[768,1024]{1,0:T(8,128)S(1)} %fusion.2, f32[1024,768]{1,0:T(8,128)S(1)} %bitcast.46, f32[768,768]{1,0:T(8,128)S(1)} %constant_dynamic-update-slice_fusion), kind=kOutput, calls=%fused_computation.11 | convolution fusion | flops 3626237952 | bytes 14942208 | tf_op jit(solution)/shard_map/dot_general | solution.py:132
  186.2 5.3 %copy.8 = f32[1024,1,768]{2,1,0:T(1,128)} copy(f32[1024,1,768]{0,2,1:T(8,128)S(1)} %fusion.8) | data formatting | bytes 6291456 | tf_op jit(solution)/shard_map/reshape | solution.py:135
  (71 shorter events, 2.6 us)
Async XLA Ops:
  0.0 14.7 %copy-start = (f32[1024,1,768]{2,1,0:T(1,128)S(1)}, f32[1024,1,768]{2,1,0:T(1,128)}, u32[]{:S(2)}) copy-start(f32[1024,1,768]{2,1,0:T(1,128)} %param.5) | copy-start | bytes 9437188
  13.3 6.9 %collective-permute-start.2 = (f32[384,768]{1,0:T(8,128)}, f32[384,768]{1,0:T(8,128)}, u32[]{:S(2)}, u32[]{:S(2)}) collective-permute-start(f32[384,768]{1,0:T(8,128)} %constant_dynamic-slice_fusion.6), channel_id=1, source_target_pairs={{0,1},{1,0},{2,3},{3,2},{4,5},{5,4},{6,7},{7,6},{8,9},{9,8},{10,11... | collective-permute-start | bytes 3538952 | tf_op jit(solution)/shard_map/ppermute | solution.py:72
  14.7 81.6 %collective-permute-start = (f32[1024,1,768]{2,1,0:T(1,128)S(1)}, f32[1024,1,768]{2,1,0:T(1,128)}, u32[]{:S(2)}, u32[]{:S(2)}) collective-permute-start(f32[1024,1,768]{2,1,0:T(1,128)S(1)} %copy-done), channel_id=1, source_target_pairs={{0,112},{16,0},{32,16},{48,32},{64,48},{80,64},{96,80},{112,96},{1... | collective-permute-start | bytes 9437192 | tf_op jit(solution)/shard_map/ppermute | solution.py:14
  18.9 79.5 %collective-permute-start.1 = (f32[1024,1,768]{2,1,0:T(1,128)S(1)}, f32[1024,1,768]{2,1,0:T(1,128)}, u32[]{:S(2)}, u32[]{:S(2)}) collective-permute-start(f32[1024,1,768]{2,1,0:T(1,128)S(1)} %copy-done), channel_id=1, source_target_pairs={{0,16},{16,32},{32,48},{48,64},{64,80},{80,96},{96,112},{112,0},{1... | collective-permute-start | bytes 9437192 | tf_op jit(solution)/shard_map/ppermute | solution.py:14
  23.1 18.2 %copy-start.3 = (s32[16]{0:T(128)S(1)}, s32[16]{0:T(128)}, u32[]{:S(2)}) copy-start(s32[16]{0:T(128)} %constant.68.clone) | copy-start | bytes 196
  23.1 19.6 %copy-start.2 = (f32[8]{0:T(128)S(1)}, f32[8]{0:T(128)}, u32[]{:S(2)}) copy-start(f32[8]{0:T(128)} %param.6) | copy-start | bytes 100
  23.1 27.1 %copy-start.1 = (f32[768]{0:T(1024)S(1)}, f32[768]{0:T(1024)}, u32[]{:S(2)}) copy-start(f32[768]{0:T(1024)} %param.7) | copy-start | bytes 9220
  25.0 10.6 %collective-permute-start.3 = (f32[192,768]{1,0:T(8,128)}, f32[192,768]{1,0:T(8,128)}, u32[]{:S(2)}, u32[]{:S(2)}) collective-permute-start(f32[192,768]{1,0:T(8,128)} %constant_dynamic-slice_fusion.5), channel_id=1, source_target_pairs={{0,2},{1,7},{2,0},{3,5},{4,6},{5,3},{6,4},{7,1},{8,10},{9,15},{10,... | collective-permute-start | bytes 1769480 | tf_op jit(solution)/shard_map/ppermute | solution.py:72
  39.4 6.2 %collective-permute-start.4 = (f32[96,768]{1,0:T(8,128)}, f32[96,768]{1,0:T(8,128)S(1)}, u32[]{:S(2)}, u32[]{:S(2)}) collective-permute-start(f32[96,768]{1,0:T(8,128)} %constant_dynamic-slice_fusion.4), channel_id=1, source_target_pairs={{0,6},{1,3},{2,4},{3,1},{4,2},{5,7},{6,0},{7,5},{8,14},{9,11},{10,... | collective-permute-start | bytes 884744 | tf_op jit(solution)/shard_map/ppermute | solution.py:72
  46.6 49.5 %collective-permute-start.5 = (f32[48,768]{1,0:T(8,128)S(1)}, f32[48,768]{1,0:T(8,128)S(1)}, u32[]{:S(2)}, u32[]{:S(2)}) collective-permute-start(f32[48,768]{1,0:T(8,128)S(1)} %constant_dynamic-slice_fusion.3), channel_id=1, source_target_pairs={{0,8},{1,9},{2,10},{3,11},{4,12},{5,13},{6,14},{7,15},{8,0},{9,1},... | collective-permute-start | bytes 442376 | tf_op jit(solution)/shard_map/ppermute | solution.py:72
  105.3 3.0 %collective-permute-start.10 = (f32[384,768]{1,0:T(8,128)S(1)}, f32[384,768]{1,0:T(8,128)S(1)}, u32[]{:S(2)}, u32[]{:S(2)}) collective-permute-start(f32[384,768]{1,0:T(8,128)S(1)} %dynamic-slice_bitcast_fusion), channel_id=1, source_target_pairs={{0,1},{1,0},{2,3},{3,2},{4,5},{5,4},{6,7},{7,6},{8,9},{9,8},{10,11... | collective-permute-start | bytes 3538952 | tf_op jit(solution)/shard_map/ppermute | solution.py:72
  108.5 10.0 %collective-permute-start.11 = (f32[192,768]{1,0:T(8,128)S(1)}, f32[192,768]{1,0:T(8,128)S(1)}, u32[]{:S(2)}, u32[]{:S(2)}) collective-permute-start(f32[192,768]{1,0:T(8,128)S(1)} %constant_dynamic-slice_fusion.2), channel_id=1, source_target_pairs={{0,2},{1,7},{2,0},{3,5},{4,6},{5,3},{6,4},{7,1},{8,10},{9,15},{10,... | collective-permute-start | bytes 1769480 | tf_op jit(solution)/shard_map/ppermute | solution.py:72
  111.1 8.0 %collective-permute-start.6 = (f32[48,768]{1,0:T(8,128)S(1)}, f32[48,768]{1,0:T(8,128)S(1)}, u32[]{:S(2)}, u32[]{:S(2)}) collective-permute-start(f32[48,768]{1,0:T(8,128)S(1)} %add_divide_fusion.1), channel_id=1, source_target_pairs={{0,8},{1,9},{2,10},{3,11},{4,12},{5,13},{6,14},{7,15},{8,0},{9,1},... | collective-permute-start | bytes 442376 | tf_op jit(solution)/shard_map/ppermute | solution.py:80
  118.7 5.9 %collective-permute-start.12 = (f32[96,768]{1,0:T(8,128)S(1)}, f32[96,768]{1,0:T(8,128)S(1)}, u32[]{:S(2)}, u32[]{:S(2)}) collective-permute-start(f32[96,768]{1,0:T(8,128)S(1)} %constant_dynamic-slice_fusion.1), channel_id=1, source_target_pairs={{0,6},{1,3},{2,4},{3,1},{4,2},{5,7},{6,0},{7,5},{8,14},{9,11},{10,... | collective-permute-start | bytes 884744 | tf_op jit(solution)/shard_map/ppermute | solution.py:72
  119.2 8.6 %collective-permute-start.7 = (f32[96,768]{1,0:T(8,128)S(1)}, f32[96,768]{1,0:T(8,128)S(1)}, u32[]{:S(2)}, u32[]{:S(2)}) collective-permute-start(f32[96,768]{1,0:T(8,128)S(1)} %constant_dynamic-update-slice_fusion.22), channel_id=1, source_target_pairs={{0,6},{1,3},{2,4},{3,1},{4,2},{5,7},{6,0},{7,5},{8,14},{9,11},{10,... | collective-permute-start | bytes 884744 | tf_op jit(solution)/shard_map/ppermute | solution.py:80
  124.7 5.7 %collective-permute-start.13 = (f32[48,768]{1,0:T(8,128)S(1)}, f32[48,768]{1,0:T(8,128)S(1)}, u32[]{:S(2)}, u32[]{:S(2)}) collective-permute-start(f32[48,768]{1,0:T(8,128)S(1)} %constant_dynamic-slice_fusion), channel_id=1, source_target_pairs={{0,8},{1,9},{2,10},{3,11},{4,12},{5,13},{6,14},{7,15},{8,0},{9,1},... | collective-permute-start | bytes 442376 | tf_op jit(solution)/shard_map/ppermute | solution.py:72
  127.8 10.0 %collective-permute-start.8 = (f32[192,768]{1,0:T(8,128)S(1)}, f32[192,768]{1,0:T(8,128)S(1)}, u32[]{:S(2)}, u32[]{:S(2)}) collective-permute-start(f32[192,768]{1,0:T(8,128)S(1)} %constant_dynamic-update-slice_fusion.20), channel_id=1, source_target_pairs={{0,2},{1,7},{2,0},{3,5},{4,6},{5,3},{6,4},{7,1},{8,10},{9,15},{10,... | collective-permute-start | bytes 1769480 | tf_op jit(solution)/shard_map/ppermute | solution.py:80
  130.5 5.6 %collective-permute-start.14 = (f32[48,768]{1,0:T(8,128)S(1)}, f32[48,768]{1,0:T(8,128)S(1)}, u32[]{:S(2)}, u32[]{:S(2)}) collective-permute-start(f32[48,768]{1,0:T(8,128)S(1)} %get-tuple-element.12), channel_id=1, source_target_pairs={{0,8},{1,9},{2,10},{3,11},{4,12},{5,13},{6,14},{7,15},{8,0},{9,1},... | collective-permute-start | bytes 442376 | tf_op jit(solution)/shard_map/ppermute | solution.py:80
  130.8 14.2 %collective-permute-start.18 = (f32[48,768]{1,0:T(8,128)S(1)}, f32[48,768]{1,0:T(8,128)S(1)}, u32[]{:S(2)}, u32[]{:S(2)}) collective-permute-start(f32[48,768]{1,0:T(8,128)S(1)} %get-tuple-element.12), channel_id=1, source_target_pairs={{0,16},{16,32},{32,48},{48,64},{64,80},{80,96},{96,112},{112,0},{1... | collective-permute-start | bytes 442376 | tf_op jit(solution)/shard_map/ppermute | solution.py:14
  136.1 8.9 %collective-permute-start.15 = (f32[96,768]{1,0:T(8,128)S(1)}, f32[96,768]{1,0:T(8,128)S(1)}, u32[]{:S(2)}, u32[]{:S(2)}) collective-permute-start(f32[96,768]{1,0:T(8,128)S(1)} %constant_dynamic-update-slice_fusion.14), channel_id=1, source_target_pairs={{0,6},{1,3},{2,4},{3,1},{4,2},{5,7},{6,0},{7,5},{8,14},{9,11},{10,... | collective-permute-start | bytes 884744 | tf_op jit(solution)/shard_map/ppermute | solution.py:80
  137.9 27.3 %collective-permute-start.9 = (f32[384,768]{1,0:T(8,128)S(1)}, f32[384,768]{1,0:T(8,128)S(1)}, u32[]{:S(2)}, u32[]{:S(2)}) collective-permute-start(f32[384,768]{1,0:T(8,128)S(1)} %constant_dynamic-update-slice_fusion.18), channel_id=1, source_target_pairs={{0,1},{1,0},{2,3},{3,2},{4,5},{5,4},{6,7},{7,6},{8,9},{9,8},{10,11... | collective-permute-start | bytes 3538952 | tf_op jit(solution)/shard_map/ppermute | solution.py:80
  144.9 8.6 %collective-permute-start.19 = (f32[48,768]{1,0:T(8,128)S(1)}, f32[48,768]{1,0:T(8,128)S(1)}, u32[]{:S(2)}, u32[]{:S(2)}) collective-permute-start(f32[48,768]{1,0:T(8,128)S(1)} %get-tuple-element.12), channel_id=1, source_target_pairs={{0,24},{1,25},{2,26},{3,27},{4,28},{5,29},{6,30},{7,31},{8,16},{9,... | collective-permute-start | bytes 442376 | tf_op jit(solution)/shard_map/ppermute | solution.py:124
  145.1 17.8 %collective-permute-start.16 = (f32[192,768]{1,0:T(8,128)S(1)}, f32[192,768]{1,0:T(8,128)S(1)}, u32[]{:S(2)}, u32[]{:S(2)}) collective-permute-start(f32[192,768]{1,0:T(8,128)S(1)} %constant_dynamic-update-slice_fusion.12), channel_id=1, source_target_pairs={{0,2},{1,7},{2,0},{3,5},{4,6},{5,3},{6,4},{7,1},{8,10},{9,15},{10,... | collective-permute-start | bytes 1769480 | tf_op jit(solution)/shard_map/ppermute | solution.py:80
  153.6 9.1 %collective-permute-start.20 = (f32[96,768]{1,0:T(8,128)S(1)}, f32[96,768]{1,0:T(8,128)S(1)}, u32[]{:S(2)}, u32[]{:S(2)}) collective-permute-start(f32[96,768]{1,0:T(8,128)S(1)} %constant_dynamic-update-slice_fusion.6), channel_id=1, source_target_pairs={{0,6},{1,3},{2,4},{3,1},{4,2},{5,7},{6,0},{7,5},{8,14},{9,11},{10,... | collective-permute-start | bytes 884744 | tf_op jit(solution)/shard_map/ppermute | solution.py:80
  162.7 10.0 %collective-permute-start.21 = (f32[192,768]{1,0:T(8,128)S(1)}, f32[192,768]{1,0:T(8,128)S(1)}, u32[]{:S(2)}, u32[]{:S(2)}) collective-permute-start(f32[192,768]{1,0:T(8,128)S(1)} %constant_dynamic-update-slice_fusion.4), channel_id=1, source_target_pairs={{0,2},{1,7},{2,0},{3,5},{4,6},{5,3},{6,4},{7,1},{8,10},{9,15},{10,... | collective-permute-start | bytes 1769480 | tf_op jit(solution)/shard_map/ppermute | solution.py:80
  163.0 14.6 %collective-permute-start.17 = (f32[384,768]{1,0:T(8,128)S(1)}, f32[384,768]{1,0:T(8,128)S(1)}, u32[]{:S(2)}, u32[]{:S(2)}) collective-permute-start(f32[384,768]{1,0:T(8,128)S(1)} %constant_dynamic-update-slice_fusion.10), channel_id=1, source_target_pairs={{0,1},{1,0},{2,3},{3,2},{4,5},{5,4},{6,7},{7,6},{8,9},{9,8},{10,11... | collective-permute-start | bytes 3538952 | tf_op jit(solution)/shard_map/ppermute | solution.py:80
  172.8 9.0 %collective-permute-start.22 = (f32[384,768]{1,0:T(8,128)S(1)}, f32[384,768]{1,0:T(8,128)S(1)}, u32[]{:S(2)}, u32[]{:S(2)}) collective-permute-start(f32[384,768]{1,0:T(8,128)S(1)} %constant_dynamic-update-slice_fusion.2), channel_id=1, source_target_pairs={{0,1},{1,0},{2,3},{3,2},{4,5},{5,4},{6,7},{7,6},{8,9},{9,8},{10,11... | collective-permute-start | bytes 3538952 | tf_op jit(solution)/shard_map/ppermute | solution.py:80

commit v7 on v0

--- a/solution.py
+++ b/solution.py
@@ -101,6 +101,8 @@
     own_vals = pair_values(eps_occ, eps_vir, group, occ_dev)
     up_vals = pair_values(eps_occ, eps_vir, (group + 1) % groups, occ_dev)
     my_vals = lax.dynamic_slice_in_dim(own_vals, my_share * rows, rows)
+    dn_vals = pair_values(eps_occ, eps_vir, (group + groups - 1) % groups, occ_dev)
+    my_dn_vals = lax.dynamic_slice_in_dim(dn_vals, my_share * rows, rows)
 
     contract_p = (((0,), (0,)), ((), ()))
     contract_b = (((1,), (1,)), ((), ()))
@@ -108,16 +110,16 @@
                            preferred_element_type=jnp.float32)
     diag_share = reduce_scatter_rows(diag, stages, bits)
     diag_amp = diag_share / (my_vals[:, None] + own_vals[None, :])
+    above, below, diag_amp = lax.optimization_barrier((above, below, diag_amp))
     diag_full = all_gather_rows(diag_amp, stages, bits)
     t_own = lax.dot_general(own, diag_full, contract_b, precision=PREC,
                             preferred_element_type=jnp.float32)
-    above, below, t_own = lax.optimization_barrier((above, below, t_own))
 
     up = lax.dot_general(own, above, contract_p, precision=PREC,
                          preferred_element_type=jnp.float32)
     up_share = reduce_scatter_rows(up, stages, bits)
     up_amp = up_share / (my_vals[:, None] + up_vals[None, :])
-    prev_amp = passed_along(up_amp, "occ", 1)
+    prev_amp = passed_along(up_share, "occ", 1) / (my_dn_vals[:, None] + own_vals[None, :])
     up_full = all_gather_rows(up_amp, stages, bits)
     prev_full = all_gather_rows(prev_amp, stages, bits)
     t_up = lax.dot_general(above, up_full, contract_b, precision=PREC,

time: 233 us -> 197 us (0.85)
  waiting for transfers between devices: 127 us -> 88.7 us
  starting transfers between devices: 50.9 us -> 46.7 us
  local copies, waits for them, and re-layouts: 17.3 us -> 20.6 us
    ppermute x8, waiting for transfers between devices: 93.3 us -> 64.1 us  [reduce_scatter_rows(): value = keep + lax.ppermute(send, 'aux', pairs)]
    ppermute x12, waiting for transfers between devices: 33.4 us -> 24 us  [all_gather_rows(): got = lax.ppermute(value, 'aux', pairs)]
    ppermute x12, starting transfers between devices: 35.9 us -> 30.5 us  [all_gather_rows(): got = lax.ppermute(value, 'aux', pairs)]
    dynamic_slice x8, local copies, waits for them, and re-layouts: 1.84 us -> 6.34 us  [reduce_scatter_rows(): send = lax.dynamic_slice_in_dim(value, (1 - bit) * half, half, 0)]
    unnamed x14 -> x10, local copies, waits for them, and re-layouts: 5.49 us -> 4.2 us
  transfers between devices with their start and end apart: 23 -> 23, of which waited for: 15 -> 15; matrix products, arithmetic and copies ran while one was open for 7% -> 13% of each run, Pallas kernels for 0% -> 0%
where the time goes in v7:
time: 197 us
  waiting for transfers between devices  88.7 us (45%)
  starting transfers between devices  46.7 us (24%)
  matrix products  26 us (13%)
  local copies, waits for them, and re-layouts  20.6 us (10%)
  other arithmetic  8.52 us (4%)
  between operations  6.15 us (3%)
    ppermute x8, waiting for transfers between devices, reduce_scatter_rows(): value = keep + lax.ppermute(send, 'aux', pairs)  64.1 us
    ppermute x12, starting transfers between devices, all_gather_rows(): got = lax.ppermute(value, 'aux', pairs)  30.5 us
    ppermute x12, waiting for transfers between devices, all_gather_rows(): got = lax.ppermute(value, 'aux', pairs)  24 us
    ppermute x8, starting transfers between devices, reduce_scatter_rows(): value = keep + lax.ppermute(send, 'aux', pairs)  11.9 us
    dot_general x1, matrix products, body(): lax.dot_general(own, own, contract_p, precision=PREC, preferred_element_t...  8.79 us
    dynamic_slice x8, local copies, waits for them, and re-layouts, reduce_scatter_rows(): send = lax.dynamic_slice_in_dim(value, (1 - bit) * half, half, 0)  6.34 us
    add x6, other arithmetic, reduce_scatter_rows(): value = keep + lax.ppermute(send, 'aux', pairs)  6.27 us
    reshape x1, local copies, waits for them, and re-layouts, body(): return (1.3 * total).reshape(aux_dev, occ_dev, virt)  5.31 us
  transfers between devices with their start and end apart: 23, of which 15 were waited for; matrix products, arithmetic and copies ran while one was open for 13% of the time, Pallas kernels for 0%

profile of v7, /device:TPU:1, one launch (start us, length us, event | category | flops | bytes accessed | tf_op | source)
XLA Modules:
  0.0 196.6 jit_solution(17927062043849100899)
XLA Ops:
  0.0 8.8 %fusion.4 = f32[768,768]{1,0:T(8,128)} fusion(f32[1024,1,768]{2,1,0:T(1,128)} %param.5), kind=kOutput, calls=%fused_computation.4 | convolution fusion | flops 3623878656 | bytes 5505024 | tf_op jit(solution)/shard_map/dot_general | solution.py:109
  8.8 0.7 constant_dynamic-slice_fusion.7
  9.5 0.7 fusion.13
  10.7 2.5 %constant_dynamic-slice_fusion.6 = f32[384,768]{1,0:T(8,128)} fusion(f32[768,768]{1,0:T(8,128)} %fusion.4, s32[]{:T(128)S(6)} %select_n.39), kind=kLoop, calls=%fused_computation.56 | loop fusion | bytes 2359300 | tf_op jit(solution)/shard_map/dynamic_slice | solution.py:71
  13.2 1.4 collective-permute-start.2
  14.6 4.2 %collective-permute-start = (f32[1024,1,768]{2,1,0:T(1,128)S(1)}, f32[1024,1,768]{2,1,0:T(1,128)}, u32[]{:S(2)}, u32[]{:S(2)}) collective-permute-start(f32[1024,1,768]{2,1,0:T(1,128)S(1)} %copy-done), channel_id=1, source_target_pairs={{0,112},{16,0},{32,16},{48,32},{64,48},{80,64},{96,80},{112,96},{1... | collective-permute-start | bytes 9437192 | tf_op jit(solution)/shard_map/ppermute | solution.py:14
  20.1 2.9 %dynamic-slice_add_fusion = f32[384,768]{1,0:T(8,128)} fusion(f32[384,768]{1,0:T(8,128)} %collective-permute-done.2, f32[768,768]{1,0:T(8,128)} %fusion.4, s32[]{:T(128)S(6)} %select_n.38), kind=kLoop, calls=%fused_computation.17 | loop fusion | flops 294912 | bytes 3538948 | tf_op jit(solution)/shard_map/add | solution.py:72
  23.0 2.0 constant_dynamic-slice_fusion.5
  24.9 2.5 %collective-permute-start.3 = (f32[192,768]{1,0:T(8,128)}, f32[192,768]{1,0:T(8,128)}, u32[]{:S(2)}, u32[]{:S(2)}) collective-permute-start(f32[192,768]{1,0:T(8,128)} %constant_dynamic-slice_fusion.5), channel_id=1, source_target_pairs={{0,2},{1,7},{2,0},{3,5},{4,6},{5,3},{6,4},{7,1},{8,10},{9,15},{10,... | collective-permute-start | bytes 1769480 | tf_op jit(solution)/shard_map/ppermute | solution.py:72
  28.7 6.8 %collective-permute-done.3 = f32[192,768]{1,0:T(8,128)} collective-permute-done((f32[192,768]{1,0:T(8,128)}, f32[192,768]{1,0:T(8,128)}, u32[]{:S(2)}, u32[]{:S(2)}) %collective-permute-start.3) | collective-permute-done | bytes 589856 | tf_op jit(solution)/shard_map/ppermute | solution.py:72
  35.5 2.1 %dynamic-slice_add_fusion.2 = f32[192,768]{1,0:T(8,128)} fusion(f32[192,768]{1,0:T(8,128)} %collective-permute-done.3, f32[384,768]{1,0:T(8,128)} %dynamic-slice_add_fusion, s32[]{:T(128)S(6)} %select_n.40), kind=kLoop, calls=%fused_computation.19 | loop fusion | flops 147456 | bytes 1769476 | tf_op jit(solution)/shard_map/add | solution.py:72
  37.6 1.7 constant_dynamic-slice_fusion.4
  41.1 0.7 dynamic_slice.75
  42.5 0.7 fusion.12
  43.2 2.3 %collective-permute-done.4 = f32[96,768]{1,0:T(8,128)S(1)} collective-permute-done((f32[96,768]{1,0:T(8,128)}, f32[96,768]{1,0:T(8,128)S(1)}, u32[]{:S(2)}, u32[]{:S(2)}) %collective-permute-start.4) | collective-permute-done | bytes 294944 | tf_op jit(solution)/shard_map/ppermute | solution.py:72
  45.5 1.0 dynamic-slice_add_fusion.4
  46.5 3.6 %collective-permute-start.5 = (f32[48,768]{1,0:T(8,128)S(1)}, f32[48,768]{1,0:T(8,128)S(1)}, u32[]{:S(2)}, u32[]{:S(2)}) collective-permute-start(f32[48,768]{1,0:T(8,128)S(1)} %constant_dynamic-slice_fusion.3), channel_id=1, source_target_pairs={{0,8},{1,9},{2,10},{3,11},{4,12},{5,13},{6,14},{7,15},{8,0},{9,1},... | collective-permute-start | bytes 442376 | tf_op jit(solution)/shard_map/ppermute | solution.py:72
  50.1 1.9 broadcast_subtract_fusion
  52.1 43.9 %collective-permute-done.5 = f32[48,768]{1,0:T(8,128)S(1)} collective-permute-done((f32[48,768]{1,0:T(8,128)S(1)}, f32[48,768]{1,0:T(8,128)S(1)}, u32[]{:S(2)}, u32[]{:S(2)}) %collective-permute-start.5) | collective-permute-done | bytes 147488 | tf_op jit(solution)/shard_map/ppermute | solution.py:72
  96.2 2.1 %copy.29 = f32[1024,1,768]{2,0,1:T(8,128)S(1)} copy(f32[1024,1,768]{2,1,0:T(1,128)} %collective-permute-done) | data formatting | bytes 6291456
  98.3 2.1 %copy.28 = f32[1024,1,768]{2,0,1:T(8,128)S(1)} copy(f32[1024,1,768]{2,1,0:T(1,128)} %collective-permute-done.1) | data formatting | bytes 6291456
  100.4 4.8 %fusion = f32[768,768]{0,1:T(8,128)S(1)} fusion(f32[1024,768]{1,0:T(8,128)S(1)} %bitcast.45, f32[1024,1,768]{2,1,0:T(1,128)S(1)} %copy-done), kind=kOutput, calls=%fused_computation | convolution fusion | flops 3623878656 | bytes 8650752 | tf_op jit(solution)/shard_map/dot_general | solution.py:118
  105.2 0.6 collective-permute-start.10
  105.8 2.5 %collective-permute-done.10 = f32[384,768]{1,0:T(8,128)S(1)} collective-permute-done((f32[384,768]{1,0:T(8,128)S(1)}, f32[384,768]{1,0:T(8,128)S(1)}, u32[]{:S(2)}, u32[]{:S(2)}) %collective-permute-start.10) | collective-permute-done | bytes 1179680 | tf_op jit(solution)/shard_map/ppermute | solution.py:72
  108.5 2.6 %collective-permute-start.11 = (f32[192,768]{1,0:T(8,128)S(1)}, f32[192,768]{1,0:T(8,128)S(1)}, u32[]{:S(2)}, u32[]{:S(2)}) collective-permute-start(f32[192,768]{1,0:T(8,128)S(1)} %constant_dynamic-slice_fusion.2), channel_id=1, source_target_pairs={{0,2},{1,7},{2,0},{3,5},{4,6},{5,3},{6,4},{7,1},{8,10},{9,15},{10,... | collective-permute-start | bytes 1769480 | tf_op jit(solution)/shard_map/ppermute | solution.py:72
  111.1 7.0 %collective-permute-done.6 = f32[48,768]{1,0:T(8,128)S(1)} collective-permute-done((f32[48,768]{1,0:T(8,128)S(1)}, f32[48,768]{1,0:T(8,128)S(1)}, u32[]{:S(2)}, u32[]{:S(2)}) %collective-permute-start.6) | collective-permute-done | bytes 147488 | tf_op jit(solution)/shard_map/ppermute | solution.py:80
  118.1 0.2 collective-permute-start.7
  118.3 0.2 collective-permute-done.11
  118.6 1.2 collective-permute-start.12
  120.0 4.1 %collective-permute-done.7 = f32[96,768]{1,0:T(8,128)S(1)} collective-permute-done((f32[96,768]{1,0:T(8,128)S(1)}, f32[96,768]{1,0:T(8,128)S(1)}, u32[]{:S(2)}, u32[]{:S(2)}) %collective-permute-start.7) | collective-permute-done | bytes 294944 | tf_op jit(solution)/shard_map/ppermute | solution.py:80
  124.2 3.0 %collective-permute-done.12 = f32[96,768]{1,0:T(8,128)S(1)} collective-permute-done((f32[96,768]{1,0:T(8,128)S(1)}, f32[96,768]{1,0:T(8,128)S(1)}, u32[]{:S(2)}, u32[]{:S(2)}) %collective-permute-start.12) | collective-permute-done | bytes 294944 | tf_op jit(solution)/shard_map/ppermute | solution.py:72
  127.5 5.4 %collective-permute-done.13 = f32[48,768]{1,0:T(8,128)S(1)} collective-permute-done((f32[48,768]{1,0:T(8,128)S(1)}, f32[48,768]{1,0:T(8,128)S(1)}, u32[]{:S(2)}, u32[]{:S(2)}) %collective-permute-start.13) | collective-permute-done | bytes 147488 | tf_op jit(solution)/shard_map/ppermute | solution.py:72
  133.3 2.0 %collective-permute-done.8 = f32[192,768]{1,0:T(8,128)S(1)} collective-permute-done((f32[192,768]{1,0:T(8,128)S(1)}, f32[192,768]{1,0:T(8,128)S(1)}, u32[]{:S(2)}, u32[]{:S(2)}) %collective-permute-start.8) | collective-permute-done | bytes 589856 | tf_op jit(solution)/shard_map/ppermute | solution.py:80
  135.4 2.9 %collective-permute-start.9 = (f32[384,768]{1,0:T(8,128)S(1)}, f32[384,768]{1,0:T(8,128)S(1)}, u32[]{:S(2)}, u32[]{:S(2)}) collective-permute-start(f32[384,768]{1,0:T(8,128)S(1)} %constant_dynamic-update-slice_fusion.18), channel_id=1, source_target_pairs={{0,1},{1,0},{2,3},{3,2},{4,5},{5,4},{6,7},{7,6},{8,9},{9,8},{10,11... | collective-permute-start | bytes 3538952 | tf_op jit(solution)/shard_map/ppermute | solution.py:80
  138.3 0.3 collective-permute-done.14
  138.8 0.6 collective-permute-done.18
  139.5 3.0 %collective-permute-start.19 = (f32[48,768]{1,0:T(8,128)S(1)}, f32[48,768]{1,0:T(8,128)S(1)}, u32[]{:S(2)}, u32[]{:S(2)}) collective-permute-start(f32[48,768]{1,0:T(8,128)S(1)} %get-tuple-element.15), channel_id=1, source_target_pairs={{0,8},{1,9},{2,10},{3,11},{4,12},{5,13},{6,14},{7,15},{8,0},{9,1},... | collective-permute-start | bytes 442376 | tf_op jit(solution)/shard_map/ppermute | solution.py:80
  142.6 1.9 collective-permute-done.15
  144.6 2.9 %collective-permute-start.16 = (f32[192,768]{1,0:T(8,128)S(1)}, f32[192,768]{1,0:T(8,128)S(1)}, u32[]{:S(2)}, u32[]{:S(2)}) collective-permute-start(f32[192,768]{1,0:T(8,128)S(1)} %constant_dynamic-update-slice_fusion.12), channel_id=1, source_target_pairs={{0,2},{1,7},{2,0},{3,5},{4,6},{5,3},{6,4},{7,1},{8,10},{9,15},{10,... | collective-permute-start | bytes 1769480 | tf_op jit(solution)/shard_map/ppermute | solution.py:80
  147.7 5.8 %collective-permute-done.20 = f32[96,768]{1,0:T(8,128)S(1)} collective-permute-done((f32[96,768]{1,0:T(8,128)S(1)}, f32[96,768]{1,0:T(8,128)S(1)}, u32[]{:S(2)}, u32[]{:S(2)}) %collective-permute-start.20) | collective-permute-done | bytes 294944 | tf_op jit(solution)/shard_map/ppermute | solution.py:80
  153.5 1.4 collective-permute-start.21
  155.0 2.9 %collective-permute-done.16 = f32[192,768]{1,0:T(8,128)S(1)} collective-permute-done((f32[192,768]{1,0:T(8,128)S(1)}, f32[192,768]{1,0:T(8,128)S(1)}, u32[]{:S(2)}, u32[]{:S(2)}) %collective-permute-start.16) | collective-permute-done | bytes 589856 | tf_op jit(solution)/shard_map/ppermute | solution.py:80
  157.9 10.3 %collective-permute-start.17 = (f32[384,768]{1,0:T(8,128)S(1)}, f32[384,768]{1,0:T(8,128)S(1)}, u32[]{:S(2)}, u32[]{:S(2)}) collective-permute-start(f32[384,768]{1,0:T(8,128)S(1)} %constant_dynamic-update-slice_fusion.10), channel_id=1, source_target_pairs={{0,1},{1,0},{2,3},{3,2},{4,5},{5,4},{6,7},{7,6},{8,9},{9,8},{10,11... | collective-permute-start | bytes 3538952 | tf_op jit(solution)/shard_map/ppermute | solution.py:80
  168.8 9.4 %collective-permute-start.22 = (f32[384,768]{1,0:T(8,128)S(1)}, f32[384,768]{1,0:T(8,128)S(1)}, u32[]{:S(2)}, u32[]{:S(2)}) collective-permute-start(f32[384,768]{1,0:T(8,128)S(1)} %constant_dynamic-update-slice_fusion.2), channel_id=1, source_target_pairs={{0,1},{1,0},{2,3},{3,2},{4,5},{5,4},{6,7},{7,6},{8,9},{9,8},{10,11... | collective-permute-start | bytes 3538952 | tf_op jit(solution)/shard_map/ppermute | solution.py:80
  178.2 4.0 %fusion.2 = f32[768,1024]{1,0:T(8,128)S(1)} fusion(f32[768,768]{1,0:T(8,128)S(1)} %constant_dynamic-update-slice_fusion.16, f32[1024,1,768]{2,1,0:T(1,128)S(1)} %copy-done), kind=kOutput, calls=%fused_computation.2 | convolution fusion | flops 3623878656 | bytes 8650752 | tf_op jit(solution)/shard_map/dot_general | solution.py:115
  182.8 4.1 %fusion.14 = f32[1024,768]{0,1:T(8,128)S(1)} fusion(f32[1024,768]{1,0:T(8,128)S(1)} %bitcast.46, f32[768,768]{1,0:T(8,128)S(1)} %constant_dynamic-update-slice_fusion.8), kind=kOutput, calls=%fused_computation.63 | convolution fusion | flops 3623878656 | bytes 8650752 | tf_op jit(solution)/shard_map/dot_general | solution.py:125
  187.0 4.3 %fusion.8 = f32[1024,1,768]{0,2,1:T(8,128)S(1)} fusion(f32[1024,768]{0,1:T(8,128)S(1)} %fusion.14, f32[768,1024]{1,0:T(8,128)S(1)} %fusion.2, f32[1024,768]{1,0:T(8,128)S(1)} %bitcast.47, f32[768,768]{1,0:T(8,128)S(1)} %constant_dynamic-update-slice_fusion), kind=kOutput, calls=%fused_computation.11 | convolution fusion | flops 3626237952 | bytes 14942208 | tf_op jit(solution)/shard_map/dot_general | solution.py:127
  191.3 5.3 %copy.8 = f32[1024,1,768]{2,1,0:T(1,128)} copy(f32[1024,1,768]{0,2,1:T(8,128)S(1)} %fusion.8) | data formatting | bytes 6291456 | tf_op jit(solution)/shard_map/reshape | solution.py:130
  (72 shorter events, 3.4 us)
Async XLA Ops:
  0.0 14.6 %copy-start = (f32[1024,1,768]{2,1,0:T(1,128)S(1)}, f32[1024,1,768]{2,1,0:T(1,128)}, u32[]{:S(2)}) copy-start(f32[1024,1,768]{2,1,0:T(1,128)} %param.5) | copy-start | bytes 9437188
  13.2 6.9 %collective-permute-start.2 = (f32[384,768]{1,0:T(8,128)}, f32[384,768]{1,0:T(8,128)}, u32[]{:S(2)}, u32[]{:S(2)}) collective-permute-start(f32[384,768]{1,0:T(8,128)} %constant_dynamic-slice_fusion.6), channel_id=1, source_target_pairs={{0,1},{1,0},{2,3},{3,2},{4,5},{5,4},{6,7},{7,6},{8,9},{9,8},{10,11... | collective-permute-start | bytes 3538952 | tf_op jit(solution)/shard_map/ppermute | solution.py:72
  14.6 81.6 %collective-permute-start = (f32[1024,1,768]{2,1,0:T(1,128)S(1)}, f32[1024,1,768]{2,1,0:T(1,128)}, u32[]{:S(2)}, u32[]{:S(2)}) collective-permute-start(f32[1024,1,768]{2,1,0:T(1,128)S(1)} %copy-done), channel_id=1, source_target_pairs={{0,112},{16,0},{32,16},{48,32},{64,48},{80,64},{96,80},{112,96},{1... | collective-permute-start | bytes 9437192 | tf_op jit(solution)/shard_map/ppermute | solution.py:14
  18.8 79.5 %collective-permute-start.1 = (f32[1024,1,768]{2,1,0:T(1,128)S(1)}, f32[1024,1,768]{2,1,0:T(1,128)}, u32[]{:S(2)}, u32[]{:S(2)}) collective-permute-start(f32[1024,1,768]{2,1,0:T(1,128)S(1)} %copy-done), channel_id=1, source_target_pairs={{0,16},{16,32},{32,48},{48,64},{64,80},{80,96},{96,112},{112,0},{1... | collective-permute-start | bytes 9437192 | tf_op jit(solution)/shard_map/ppermute | solution.py:14
  23.0 18.2 %copy-start.3 = (s32[16]{0:T(128)S(1)}, s32[16]{0:T(128)}, u32[]{:S(2)}) copy-start(s32[16]{0:T(128)} %constant.75.clone) | copy-start | bytes 196
  23.0 19.6 %copy-start.1 = (f32[8]{0:T(128)S(1)}, f32[8]{0:T(128)}, u32[]{:S(2)}) copy-start(f32[8]{0:T(128)} %param.6) | copy-start | bytes 100
  23.0 27.1 %copy-start.2 = (f32[768]{0:T(1024)S(1)}, f32[768]{0:T(1024)}, u32[]{:S(2)}) copy-start(f32[768]{0:T(1024)} %param.7) | copy-start | bytes 9220
  24.9 10.6 %collective-permute-start.3 = (f32[192,768]{1,0:T(8,128)}, f32[192,768]{1,0:T(8,128)}, u32[]{:S(2)}, u32[]{:S(2)}) collective-permute-start(f32[192,768]{1,0:T(8,128)} %constant_dynamic-slice_fusion.5), channel_id=1, source_target_pairs={{0,2},{1,7},{2,0},{3,5},{4,6},{5,3},{6,4},{7,1},{8,10},{9,15},{10,... | collective-permute-start | bytes 1769480 | tf_op jit(solution)/shard_map/ppermute | solution.py:72
  39.3 6.2 %collective-permute-start.4 = (f32[96,768]{1,0:T(8,128)}, f32[96,768]{1,0:T(8,128)S(1)}, u32[]{:S(2)}, u32[]{:S(2)}) collective-permute-start(f32[96,768]{1,0:T(8,128)} %constant_dynamic-slice_fusion.4), channel_id=1, source_target_pairs={{0,6},{1,3},{2,4},{3,1},{4,2},{5,7},{6,0},{7,5},{8,14},{9,11},{10,... | collective-permute-start | bytes 884744 | tf_op jit(solution)/shard_map/ppermute | solution.py:72
  46.5 49.5 %collective-permute-start.5 = (f32[48,768]{1,0:T(8,128)S(1)}, f32[48,768]{1,0:T(8,128)S(1)}, u32[]{:S(2)}, u32[]{:S(2)}) collective-permute-start(f32[48,768]{1,0:T(8,128)S(1)} %constant_dynamic-slice_fusion.3), channel_id=1, source_target_pairs={{0,8},{1,9},{2,10},{3,11},{4,12},{5,13},{6,14},{7,15},{8,0},{9,1},... | collective-permute-start | bytes 442376 | tf_op jit(solution)/shard_map/ppermute | solution.py:72
  105.2 3.0 %collective-permute-start.10 = (f32[384,768]{1,0:T(8,128)S(1)}, f32[384,768]{1,0:T(8,128)S(1)}, u32[]{:S(2)}, u32[]{:S(2)}) collective-permute-start(f32[384,768]{1,0:T(8,128)S(1)} %dynamic-slice_bitcast_fusion), channel_id=1, source_target_pairs={{0,1},{1,0},{2,3},{3,2},{4,5},{5,4},{6,7},{7,6},{8,9},{9,8},{10,11... | collective-permute-start | bytes 3538952 | tf_op jit(solution)/shard_map/ppermute | solution.py:72
  108.5 10.0 %collective-permute-start.11 = (f32[192,768]{1,0:T(8,128)S(1)}, f32[192,768]{1,0:T(8,128)S(1)}, u32[]{:S(2)}, u32[]{:S(2)}) collective-permute-start(f32[192,768]{1,0:T(8,128)S(1)} %constant_dynamic-slice_fusion.2), channel_id=1, source_target_pairs={{0,2},{1,7},{2,0},{3,5},{4,6},{5,3},{6,4},{7,1},{8,10},{9,15},{10,... | collective-permute-start | bytes 1769480 | tf_op jit(solution)/shard_map/ppermute | solution.py:72
  111.0 7.1 %collective-permute-start.6 = (f32[48,768]{1,0:T(8,128)S(1)}, f32[48,768]{1,0:T(8,128)S(1)}, u32[]{:S(2)}, u32[]{:S(2)}) collective-permute-start(f32[48,768]{1,0:T(8,128)S(1)} %add_divide_fusion.2), channel_id=1, source_target_pairs={{0,8},{1,9},{2,10},{3,11},{4,12},{5,13},{6,14},{7,15},{8,0},{9,1},... | collective-permute-start | bytes 442376 | tf_op jit(solution)/shard_map/ppermute | solution.py:80
  118.1 5.9 %collective-permute-start.7 = (f32[96,768]{1,0:T(8,128)S(1)}, f32[96,768]{1,0:T(8,128)S(1)}, u32[]{:S(2)}, u32[]{:S(2)}) collective-permute-start(f32[96,768]{1,0:T(8,128)S(1)} %constant_dynamic-update-slice_fusion.22), channel_id=1, source_target_pairs={{0,6},{1,3},{2,4},{3,1},{4,2},{5,7},{6,0},{7,5},{8,14},{9,11},{10,... | collective-permute-start | bytes 884744 | tf_op jit(solution)/shard_map/ppermute | solution.py:80
  118.6 8.6 %collective-permute-start.12 = (f32[96,768]{1,0:T(8,128)S(1)}, f32[96,768]{1,0:T(8,128)S(1)}, u32[]{:S(2)}, u32[]{:S(2)}) collective-permute-start(f32[96,768]{1,0:T(8,128)S(1)} %constant_dynamic-slice_fusion.1), channel_id=1, source_target_pairs={{0,6},{1,3},{2,4},{3,1},{4,2},{5,7},{6,0},{7,5},{8,14},{9,11},{10,... | collective-permute-start | bytes 884744 | tf_op jit(solution)/shard_map/ppermute | solution.py:72
  124.1 11.2 %collective-permute-start.8 = (f32[192,768]{1,0:T(8,128)S(1)}, f32[192,768]{1,0:T(8,128)S(1)}, u32[]{:S(2)}, u32[]{:S(2)}) collective-permute-start(f32[192,768]{1,0:T(8,128)S(1)} %constant_dynamic-update-slice_fusion.20), channel_id=1, source_target_pairs={{0,2},{1,7},{2,0},{3,5},{4,6},{5,3},{6,4},{7,1},{8,10},{9,15},{10,... | collective-permute-start | bytes 1769480 | tf_op jit(solution)/shard_map/ppermute | solution.py:80
  127.3 5.6 %collective-permute-start.13 = (f32[48,768]{1,0:T(8,128)S(1)}, f32[48,768]{1,0:T(8,128)S(1)}, u32[]{:S(2)}, u32[]{:S(2)}) collective-permute-start(f32[48,768]{1,0:T(8,128)S(1)} %constant_dynamic-slice_fusion), channel_id=1, source_target_pairs={{0,8},{1,9},{2,10},{3,11},{4,12},{5,13},{6,14},{7,15},{8,0},{9,1},... | collective-permute-start | bytes 442376 | tf_op jit(solution)/shard_map/ppermute | solution.py:72
  133.0 5.6 %collective-permute-start.14 = (f32[48,768]{1,0:T(8,128)S(1)}, f32[48,768]{1,0:T(8,128)S(1)}, u32[]{:S(2)}, u32[]{:S(2)}) collective-permute-start(f32[48,768]{1,0:T(8,128)S(1)} %get-tuple-element.12), channel_id=1, source_target_pairs={{0,8},{1,9},{2,10},{3,11},{4,12},{5,13},{6,14},{7,15},{8,0},{9,1},... | collective-permute-start | bytes 442376 | tf_op jit(solution)/shard_map/ppermute | solution.py:80
  133.2 6.2 %collective-permute-start.18 = (f32[48,768]{1,0:T(8,128)S(1)}, f32[48,768]{1,0:T(8,128)S(1)}, u32[]{:S(2)}, u32[]{:S(2)}) collective-permute-start(f32[48,768]{1,0:T(8,128)S(1)} %get-tuple-element.13), channel_id=1, source_target_pairs={{0,16},{16,32},{32,48},{48,64},{64,80},{80,96},{96,112},{112,0},{1... | collective-permute-start | bytes 442376 | tf_op jit(solution)/shard_map/ppermute | solution.py:14
  135.4 33.1 %collective-permute-start.9 = (f32[384,768]{1,0:T(8,128)S(1)}, f32[384,768]{1,0:T(8,128)S(1)}, u32[]{:S(2)}, u32[]{:S(2)}) collective-permute-start(f32[384,768]{1,0:T(8,128)S(1)} %constant_dynamic-update-slice_fusion.18), channel_id=1, source_target_pairs={{0,1},{1,0},{2,3},{3,2},{4,5},{5,4},{6,7},{7,6},{8,9},{9,8},{10,11... | collective-permute-start | bytes 3538952 | tf_op jit(solution)/shard_map/ppermute | solution.py:80
  138.6 5.9 %collective-permute-start.15 = (f32[96,768]{1,0:T(8,128)S(1)}, f32[96,768]{1,0:T(8,128)S(1)}, u32[]{:S(2)}, u32[]{:S(2)}) collective-permute-start(f32[96,768]{1,0:T(8,128)S(1)} %constant_dynamic-update-slice_fusion.14), channel_id=1, source_target_pairs={{0,6},{1,3},{2,4},{3,1},{4,2},{5,7},{6,0},{7,5},{8,14},{9,11},{10,... | collective-permute-start | bytes 884744 | tf_op jit(solution)/shard_map/ppermute | solution.py:80
  139.5 7.9 %collective-permute-start.19 = (f32[48,768]{1,0:T(8,128)S(1)}, f32[48,768]{1,0:T(8,128)S(1)}, u32[]{:S(2)}, u32[]{:S(2)}) collective-permute-start(f32[48,768]{1,0:T(8,128)S(1)} %get-tuple-element.15), channel_id=1, source_target_pairs={{0,8},{1,9},{2,10},{3,11},{4,12},{5,13},{6,14},{7,15},{8,0},{9,1},... | collective-permute-start | bytes 442376 | tf_op jit(solution)/shard_map/ppermute | solution.py:80
  144.6 13.3 %collective-permute-start.16 = (f32[192,768]{1,0:T(8,128)S(1)}, f32[192,768]{1,0:T(8,128)S(1)}, u32[]{:S(2)}, u32[]{:S(2)}) collective-permute-start(f32[192,768]{1,0:T(8,128)S(1)} %constant_dynamic-update-slice_fusion.12), channel_id=1, source_target_pairs={{0,2},{1,7},{2,0},{3,5},{4,6},{5,3},{6,4},{7,1},{8,10},{9,15},{10,... | collective-permute-start | bytes 1769480 | tf_op jit(solution)/shard_map/ppermute | solution.py:80
  147.5 5.9 %collective-permute-start.20 = (f32[96,768]{1,0:T(8,128)S(1)}, f32[96,768]{1,0:T(8,128)S(1)}, u32[]{:S(2)}, u32[]{:S(2)}) collective-permute-start(f32[96,768]{1,0:T(8,128)S(1)} %constant_dynamic-update-slice_fusion.6), channel_id=1, source_target_pairs={{0,6},{1,3},{2,4},{3,1},{4,2},{5,7},{6,0},{7,5},{8,14},{9,11},{10,... | collective-permute-start | bytes 884744 | tf_op jit(solution)/shard_map/ppermute | solution.py:80
  153.5 15.3 %collective-permute-start.21 = (f32[192,768]{1,0:T(8,128)S(1)}, f32[192,768]{1,0:T(8,128)S(1)}, u32[]{:S(2)}, u32[]{:S(2)}) collective-permute-start(f32[192,768]{1,0:T(8,128)S(1)} %constant_dynamic-update-slice_fusion.4), channel_id=1, source_target_pairs={{0,2},{1,7},{2,0},{3,5},{4,6},{5,3},{6,4},{7,1},{8,10},{9,15},{10,... | collective-permute-start | bytes 1769480 | tf_op jit(solution)/shard_map/ppermute | solution.py:80
  157.9 24.7 %collective-permute-start.17 = (f32[384,768]{1,0:T(8,128)S(1)}, f32[384,768]{1,0:T(8,128)S(1)}, u32[]{:S(2)}, u32[]{:S(2)}) collective-permute-start(f32[384,768]{1,0:T(8,128)S(1)} %constant_dynamic-update-slice_fusion.10), channel_id=1, source_target_pairs={{0,1},{1,0},{2,3},{3,2},{4,5},{5,4},{6,7},{7,6},{8,9},{9,8},{10,11... | collective-permute-start | bytes 3538952 | tf_op jit(solution)/shard_map/ppermute | solution.py:80
  168.8 18.1 %collective-permute-start.22 = (f32[384,768]{1,0:T(8,128)S(1)}, f32[384,768]{1,0:T(8,128)S(1)}, u32[]{:S(2)}, u32[]{:S(2)}) collective-permute-start(f32[384,768]{1,0:T(8,128)S(1)} %constant_dynamic-update-slice_fusion.2), channel_id=1, source_target_pairs={{0,1},{1,0},{2,3},{3,2},{4,5},{5,4},{6,7},{7,6},{8,9},{9,8},{10,11... | collective-permute-start | bytes 3538952 | tf_op jit(solution)/shard_map/ppermute | solution.py:80

commit v8 on v0

--- a/solution.py
+++ b/solution.py
@@ -69,7 +69,8 @@
         pairs = [(i, j) for i, (j, _) in enumerate(stage)]
         keep = lax.dynamic_slice_in_dim(value, bit * half, half, 0)
         send = lax.dynamic_slice_in_dim(value, (1 - bit) * half, half, 0)
-        value = keep + lax.ppermute(send, "aux", pairs)
+        got = lax.ppermute(send, "aux", pairs)
+        value = keep + got
     return value
 
 
@@ -108,10 +109,10 @@
                            preferred_element_type=jnp.float32)
     diag_share = reduce_scatter_rows(diag, stages, bits)
     diag_amp = diag_share / (my_vals[:, None] + own_vals[None, :])
+    above, below, diag_amp = lax.optimization_barrier((above, below, diag_amp))
     diag_full = all_gather_rows(diag_amp, stages, bits)
     t_own = lax.dot_general(own, diag_full, contract_b, precision=PREC,
                             preferred_element_type=jnp.float32)
-    above, below, t_own = lax.optimization_barrier((above, below, t_own))
 
     up = lax.dot_general(own, above, contract_p, precision=PREC,
                          preferred_element_type=jnp.float32)

time: 233 us -> 190 us (0.82)
  waiting for transfers between devices: 127 us -> 98.7 us
  starting transfers between devices: 50.9 us -> 30.8 us
  local copies, waits for them, and re-layouts: 17.3 us -> 20.4 us
    ppermute x8, waiting for transfers between devices: 93.3 us -> 67.9 us  [reduce_scatter_rows(): got = lax.ppermute(send, 'aux', pairs)]
    ppermute x12, starting transfers between devices: 35.9 us -> 15.5 us  [all_gather_rows(): got = lax.ppermute(value, 'aux', pairs)]
    dynamic_slice x8, local copies, waits for them, and re-layouts: 1.84 us -> 6.33 us  [reduce_scatter_rows(): send = lax.dynamic_slice_in_dim(value, (1 - bit) * half, half, 0)]
    ppermute x12, waiting for transfers between devices: 33.4 us -> 30.8 us  [all_gather_rows(): got = lax.ppermute(value, 'aux', pairs)]
    unnamed x14 -> x10, local copies, waits for them, and re-layouts: 5.49 us -> 4.2 us
  transfers between devices with their start and end apart: 23 -> 23, of which waited for: 15 -> 12; matrix products, arithmetic and copies ran while one was open for 7% -> 13% of each run, Pallas kernels for 0% -> 0%
where the time goes in v8:
time: 190 us
  waiting for transfers between devices  98.7 us (52%)
  starting transfers between devices  30.8 us (16%)
  matrix products  26 us (14%)
  local copies, waits for them, and re-layouts  20.4 us (11%)
  other arithmetic  7.63 us (4%)
  between operations  6.28 us (3%)
    ppermute x8, waiting for transfers between devices, reduce_scatter_rows(): got = lax.ppermute(send, 'aux', pairs)  67.9 us
    ppermute x12, waiting for transfers between devices, all_gather_rows(): got = lax.ppermute(value, 'aux', pairs)  30.8 us
    ppermute x12, starting transfers between devices, all_gather_rows(): got = lax.ppermute(value, 'aux', pairs)  15.5 us
    ppermute x8, starting transfers between devices, reduce_scatter_rows(): got = lax.ppermute(send, 'aux', pairs)  11 us
    dot_general x1, matrix products, body(): lax.dot_general(own, own, contract_p, precision=PREC, preferred_element_t...  8.79 us
    dynamic_slice x8, local copies, waits for them, and re-layouts, reduce_scatter_rows(): send = lax.dynamic_slice_in_dim(value, (1 - bit) * half, half, 0)  6.33 us
    add x6, other arithmetic, reduce_scatter_rows(): value = keep + got  6.26 us
    reshape x1, local copies, waits for them, and re-layouts, body(): return (1.3 * total).reshape(aux_dev, occ_dev, virt)  5.31 us
  transfers between devices with their start and end apart: 23, of which 12 were waited for; matrix products, arithmetic and copies ran while one was open for 13% of the time, Pallas kernels for 0%

profile of v8, /device:TPU:1, one launch (start us, length us, event | category | flops | bytes accessed | tf_op | source)
XLA Modules:
  0.0 189.9 jit_solution(15728157771687701696)
XLA Ops:
  0.0 8.8 %fusion.4 = f32[768,768]{1,0:T(8,128)} fusion(f32[1024,1,768]{2,1,0:T(1,128)} %param.5), kind=kOutput, calls=%fused_computation.4 | convolution fusion | flops 3623878656 | bytes 5505024 | tf_op jit(solution)/shard_map/dot_general | solution.py:108
  8.8 0.7 constant_dynamic-slice_fusion.7
  9.5 0.6 fusion.13
  10.8 2.5 %constant_dynamic-slice_fusion.6 = f32[384,768]{1,0:T(8,128)} fusion(f32[768,768]{1,0:T(8,128)} %fusion.4, s32[]{:T(128)S(6)} %select_n.33), kind=kLoop, calls=%fused_computation.54 | loop fusion | bytes 2359300 | tf_op jit(solution)/shard_map/dynamic_slice | solution.py:71
  13.3 1.4 collective-permute-start.2
  14.7 4.2 %collective-permute-start = (f32[1024,1,768]{2,1,0:T(1,128)S(1)}, f32[1024,1,768]{2,1,0:T(1,128)}, u32[]{:S(2)}, u32[]{:S(2)}) collective-permute-start(f32[1024,1,768]{2,1,0:T(1,128)S(1)} %copy-done), channel_id=1, source_target_pairs={{0,112},{16,0},{32,16},{48,32},{64,48},{80,64},{96,80},{112,96},{1... | collective-permute-start | bytes 9437192 | tf_op jit(solution)/shard_map/ppermute | solution.py:14
  20.2 2.9 %dynamic-slice_add_fusion = f32[384,768]{1,0:T(8,128)} fusion(f32[384,768]{1,0:T(8,128)} %collective-permute-done.2, f32[768,768]{1,0:T(8,128)} %fusion.4, s32[]{:T(128)S(6)} %select_n.32), kind=kLoop, calls=%fused_computation.17 | loop fusion | flops 294912 | bytes 3538948 | tf_op jit(solution)/shard_map/add | solution.py:73
  23.1 2.0 %constant_dynamic-slice_fusion.5 = f32[192,768]{1,0:T(8,128)} fusion(f32[384,768]{1,0:T(8,128)} %dynamic-slice_add_fusion, s32[]{:T(128)S(6)} %select_n.35), kind=kLoop, calls=%fused_computation.53 | loop fusion | bytes 1179652 | tf_op jit(solution)/shard_map/dynamic_slice | solution.py:71
  25.0 2.5 %collective-permute-start.3 = (f32[192,768]{1,0:T(8,128)}, f32[192,768]{1,0:T(8,128)}, u32[]{:S(2)}, u32[]{:S(2)}) collective-permute-start(f32[192,768]{1,0:T(8,128)} %constant_dynamic-slice_fusion.5), channel_id=1, source_target_pairs={{0,2},{1,7},{2,0},{3,5},{4,6},{5,3},{6,4},{7,1},{8,10},{9,15},{10,... | collective-permute-start | bytes 1769480 | tf_op jit(solution)/shard_map/ppermute | solution.py:72
  28.7 6.9 %collective-permute-done.3 = f32[192,768]{1,0:T(8,128)} collective-permute-done((f32[192,768]{1,0:T(8,128)}, f32[192,768]{1,0:T(8,128)}, u32[]{:S(2)}, u32[]{:S(2)}) %collective-permute-start.3) | collective-permute-done | bytes 589856 | tf_op jit(solution)/shard_map/ppermute | solution.py:72
  35.6 2.1 %dynamic-slice_add_fusion.2 = f32[192,768]{1,0:T(8,128)} fusion(f32[192,768]{1,0:T(8,128)} %collective-permute-done.3, f32[384,768]{1,0:T(8,128)} %dynamic-slice_add_fusion, s32[]{:T(128)S(6)} %select_n.34), kind=kLoop, calls=%fused_computation.19 | loop fusion | flops 147456 | bytes 1769476 | tf_op jit(solution)/shard_map/add | solution.py:73
  37.7 1.7 constant_dynamic-slice_fusion.4
  41.3 0.7 dynamic_slice.71
  42.7 0.6 fusion.12
  43.3 2.3 %collective-permute-done.4 = f32[96,768]{1,0:T(8,128)S(1)} collective-permute-done((f32[96,768]{1,0:T(8,128)}, f32[96,768]{1,0:T(8,128)S(1)}, u32[]{:S(2)}, u32[]{:S(2)}) %collective-permute-start.4) | collective-permute-done | bytes 294944 | tf_op jit(solution)/shard_map/ppermute | solution.py:72
  45.6 1.0 dynamic-slice_add_fusion.4
  46.6 3.6 %collective-permute-start.5 = (f32[48,768]{1,0:T(8,128)S(1)}, f32[48,768]{1,0:T(8,128)S(1)}, u32[]{:S(2)}, u32[]{:S(2)}) collective-permute-start(f32[48,768]{1,0:T(8,128)S(1)} %constant_dynamic-slice_fusion.3), channel_id=1, source_target_pairs={{0,8},{1,9},{2,10},{3,11},{4,12},{5,13},{6,14},{7,15},{8,0},{9,1},... | collective-permute-start | bytes 442376 | tf_op jit(solution)/shard_map/ppermute | solution.py:72
  50.2 1.2 broadcast_subtract_fusion
  51.5 44.6 %collective-permute-done.5 = f32[48,768]{1,0:T(8,128)S(1)} collective-permute-done((f32[48,768]{1,0:T(8,128)S(1)}, f32[48,768]{1,0:T(8,128)S(1)}, u32[]{:S(2)}, u32[]{:S(2)}) %collective-permute-start.5) | collective-permute-done | bytes 147488 | tf_op jit(solution)/shard_map/ppermute | solution.py:72
  96.2 2.1 %copy.29 = f32[1024,1,768]{2,0,1:T(8,128)S(1)} copy(f32[1024,1,768]{2,1,0:T(1,128)} %collective-permute-done) | data formatting | bytes 6291456
  98.3 2.1 %copy.28 = f32[1024,1,768]{2,0,1:T(8,128)S(1)} copy(f32[1024,1,768]{2,1,0:T(1,128)} %collective-permute-done.1) | data formatting | bytes 6291456
  100.4 4.8 %fusion = f32[768,768]{0,1:T(8,128)S(1)} fusion(f32[1024,768]{1,0:T(8,128)S(1)} %bitcast.44, f32[1024,1,768]{2,1,0:T(1,128)S(1)} %copy-done), kind=kOutput, calls=%fused_computation | convolution fusion | flops 3623878656 | bytes 8650752 | tf_op jit(solution)/shard_map/dot_general | solution.py:117
  105.3 0.6 collective-permute-start.10
  105.9 2.5 %collective-permute-done.10 = f32[384,768]{1,0:T(8,128)S(1)} collective-permute-done((f32[384,768]{1,0:T(8,128)S(1)}, f32[384,768]{1,0:T(8,128)S(1)}, u32[]{:S(2)}, u32[]{:S(2)}) %collective-permute-start.10) | collective-permute-done | bytes 1179680 | tf_op jit(solution)/shard_map/ppermute | solution.py:72
  108.5 2.6 %collective-permute-start.11 = (f32[192,768]{1,0:T(8,128)S(1)}, f32[192,768]{1,0:T(8,128)S(1)}, u32[]{:S(2)}, u32[]{:S(2)}) collective-permute-start(f32[192,768]{1,0:T(8,128)S(1)} %constant_dynamic-slice_fusion.2), channel_id=1, source_target_pairs={{0,2},{1,7},{2,0},{3,5},{4,6},{5,3},{6,4},{7,1},{8,10},{9,15},{10,... | collective-permute-start | bytes 1769480 | tf_op jit(solution)/shard_map/ppermute | solution.py:72
  111.1 7.5 %collective-permute-done.11 = f32[192,768]{1,0:T(8,128)S(1)} collective-permute-done((f32[192,768]{1,0:T(8,128)S(1)}, f32[192,768]{1,0:T(8,128)S(1)}, u32[]{:S(2)}, u32[]{:S(2)}) %collective-permute-start.11) | collective-permute-done | bytes 589856 | tf_op jit(solution)/shard_map/ppermute | solution.py:72
  118.7 0.4 collective-permute-start.12
  119.2 1.3 collective-permute-start.7
  120.5 4.2 %collective-permute-done.12 = f32[96,768]{1,0:T(8,128)S(1)} collective-permute-done((f32[96,768]{1,0:T(8,128)S(1)}, f32[96,768]{1,0:T(8,128)S(1)}, u32[]{:S(2)}, u32[]{:S(2)}) %collective-permute-start.12) | collective-permute-done | bytes 294944 | tf_op jit(solution)/shard_map/ppermute | solution.py:72
  124.8 3.0 %collective-permute-done.7 = f32[96,768]{1,0:T(8,128)S(1)} collective-permute-done((f32[96,768]{1,0:T(8,128)S(1)}, f32[96,768]{1,0:T(8,128)S(1)}, u32[]{:S(2)}, u32[]{:S(2)}) %collective-permute-start.7) | collective-permute-done | bytes 294944 | tf_op jit(solution)/shard_map/ppermute | solution.py:81
  127.8 2.6 %collective-permute-start.8 = (f32[192,768]{1,0:T(8,128)S(1)}, f32[192,768]{1,0:T(8,128)S(1)}, u32[]{:S(2)}, u32[]{:S(2)}) collective-permute-start(f32[192,768]{1,0:T(8,128)S(1)} %constant_dynamic-update-slice_fusion.20), channel_id=1, source_target_pairs={{0,2},{1,7},{2,0},{3,5},{4,6},{5,3},{6,4},{7,1},{8,10},{9,15},{10,... | collective-permute-start | bytes 1769480 | tf_op jit(solution)/shard_map/ppermute | solution.py:81
  130.8 5.3 %collective-permute-done.14 = f32[48,768]{1,0:T(8,128)S(1)} collective-permute-done((f32[48,768]{1,0:T(8,128)S(1)}, f32[48,768]{1,0:T(8,128)S(1)}, u32[]{:S(2)}, u32[]{:S(2)}) %collective-permute-start.14) | collective-permute-done | bytes 147488 | tf_op jit(solution)/shard_map/ppermute | solution.py:81
  136.1 0.3 collective-permute-start.15
  136.4 1.5 collective-permute-done.8
  137.9 7.0 %collective-permute-start.9 = (f32[384,768]{1,0:T(8,128)S(1)}, f32[384,768]{1,0:T(8,128)S(1)}, u32[]{:S(2)}, u32[]{:S(2)}) collective-permute-start(f32[384,768]{1,0:T(8,128)S(1)} %constant_dynamic-update-slice_fusion.18), channel_id=1, source_target_pairs={{0,1},{1,0},{2,3},{3,2},{4,5},{5,4},{6,7},{7,6},{8,9},{9,8},{10,11... | collective-permute-start | bytes 3538952 | tf_op jit(solution)/shard_map/ppermute | solution.py:81
  145.2 0.4 collective-permute-start.16
  145.6 6.4 %collective-permute-done.19 = f32[48,768]{1,0:T(8,128)S(1)} collective-permute-done((f32[48,768]{1,0:T(8,128)S(1)}, f32[48,768]{1,0:T(8,128)S(1)}, u32[]{:S(2)}, u32[]{:S(2)}) %collective-permute-start.19) | collective-permute-done | bytes 147488 | tf_op jit(solution)/shard_map/ppermute | solution.py:81
  152.2 8.9 %collective-permute-done.20 = f32[96,768]{1,0:T(8,128)S(1)} collective-permute-done((f32[96,768]{1,0:T(8,128)S(1)}, f32[96,768]{1,0:T(8,128)S(1)}, u32[]{:S(2)}, u32[]{:S(2)}) %collective-permute-start.20) | collective-permute-done | bytes 294944 | tf_op jit(solution)/shard_map/ppermute | solution.py:81
  161.3 3.4 %collective-permute-start.17 = (f32[384,768]{1,0:T(8,128)S(1)}, f32[384,768]{1,0:T(8,128)S(1)}, u32[]{:S(2)}, u32[]{:S(2)}) collective-permute-start(f32[384,768]{1,0:T(8,128)S(1)} %constant_dynamic-update-slice_fusion.10), channel_id=1, source_target_pairs={{0,1},{1,0},{2,3},{3,2},{4,5},{5,4},{6,7},{7,6},{8,9},{9,8},{10,11... | collective-permute-start | bytes 3538952 | tf_op jit(solution)/shard_map/ppermute | solution.py:81
  164.8 0.2 broadcast.20.clone.1
  165.3 5.8 %collective-permute-done.21 = f32[192,768]{1,0:T(8,128)S(1)} collective-permute-done((f32[192,768]{1,0:T(8,128)S(1)}, f32[192,768]{1,0:T(8,128)S(1)}, u32[]{:S(2)}, u32[]{:S(2)}) %collective-permute-start.21) | collective-permute-done | bytes 589856 | tf_op jit(solution)/shard_map/ppermute | solution.py:81
  171.1 0.3 collective-permute-start.22
  171.4 4.0 %fusion.2 = f32[768,1024]{1,0:T(8,128)S(1)} fusion(f32[768,768]{1,0:T(8,128)S(1)} %constant_dynamic-update-slice_fusion.16, f32[1024,1,768]{2,1,0:T(1,128)S(1)} %copy-done), kind=kOutput, calls=%fused_computation.2 | convolution fusion | flops 3623878656 | bytes 8650752 | tf_op jit(solution)/shard_map/dot_general | solution.py:114
  175.4 0.2 broadcast.20.clone
  175.7 0.2 broadcast.20.clone.2
  176.0 4.1 %fusion.14 = f32[1024,768]{0,1:T(8,128)S(1)} fusion(f32[1024,768]{1,0:T(8,128)S(1)} %bitcast.45, f32[768,768]{1,0:T(8,128)S(1)} %constant_dynamic-update-slice_fusion.8), kind=kOutput, calls=%fused_computation.60 | convolution fusion | flops 3623878656 | bytes 8650752 | tf_op jit(solution)/shard_map/dot_general | solution.py:124
  180.2 4.3 %fusion.8 = f32[1024,1,768]{0,2,1:T(8,128)S(1)} fusion(f32[1024,768]{0,1:T(8,128)S(1)} %fusion.14, f32[768,1024]{1,0:T(8,128)S(1)} %fusion.2, f32[1024,768]{1,0:T(8,128)S(1)} %bitcast.46, f32[768,768]{1,0:T(8,128)S(1)} %constant_dynamic-update-slice_fusion), kind=kOutput, calls=%fused_computation.11 | convolution fusion | flops 3626237952 | bytes 14942208 | tf_op jit(solution)/shard_map/dot_general | solution.py:126
  184.6 5.3 %copy.8 = f32[1024,1,768]{2,1,0:T(1,128)} copy(f32[1024,1,768]{0,2,1:T(8,128)S(1)} %fusion.8) | data formatting | bytes 6291456 | tf_op jit(solution)/shard_map/reshape | solution.py:129
  (71 shorter events, 2.7 us)
Async XLA Ops:
  0.0 14.7 %copy-start = (f32[1024,1,768]{2,1,0:T(1,128)S(1)}, f32[1024,1,768]{2,1,0:T(1,128)}, u32[]{:S(2)}) copy-start(f32[1024,1,768]{2,1,0:T(1,128)} %param.5) | copy-start | bytes 9437188
  13.3 6.9 %collective-permute-start.2 = (f32[384,768]{1,0:T(8,128)}, f32[384,768]{1,0:T(8,128)}, u32[]{:S(2)}, u32[]{:S(2)}) collective-permute-start(f32[384,768]{1,0:T(8,128)} %constant_dynamic-slice_fusion.6), channel_id=1, source_target_pairs={{0,1},{1,0},{2,3},{3,2},{4,5},{5,4},{6,7},{7,6},{8,9},{9,8},{10,11... | collective-permute-start | bytes 3538952 | tf_op jit(solution)/shard_map/ppermute | solution.py:72
  14.7 81.6 %collective-permute-start = (f32[1024,1,768]{2,1,0:T(1,128)S(1)}, f32[1024,1,768]{2,1,0:T(1,128)}, u32[]{:S(2)}, u32[]{:S(2)}) collective-permute-start(f32[1024,1,768]{2,1,0:T(1,128)S(1)} %copy-done), channel_id=1, source_target_pairs={{0,112},{16,0},{32,16},{48,32},{64,48},{80,64},{96,80},{112,96},{1... | collective-permute-start | bytes 9437192 | tf_op jit(solution)/shard_map/ppermute | solution.py:14
  18.9 79.5 %collective-permute-start.1 = (f32[1024,1,768]{2,1,0:T(1,128)S(1)}, f32[1024,1,768]{2,1,0:T(1,128)}, u32[]{:S(2)}, u32[]{:S(2)}) collective-permute-start(f32[1024,1,768]{2,1,0:T(1,128)S(1)} %copy-done), channel_id=1, source_target_pairs={{0,16},{16,32},{32,48},{48,64},{64,80},{80,96},{96,112},{112,0},{1... | collective-permute-start | bytes 9437192 | tf_op jit(solution)/shard_map/ppermute | solution.py:14
  23.1 18.2 %copy-start.3 = (s32[16]{0:T(128)S(1)}, s32[16]{0:T(128)}, u32[]{:S(2)}) copy-start(s32[16]{0:T(128)} %constant.68.clone) | copy-start | bytes 196
  23.1 19.6 %copy-start.2 = (f32[8]{0:T(128)S(1)}, f32[8]{0:T(128)}, u32[]{:S(2)}) copy-start(f32[8]{0:T(128)} %param.6) | copy-start | bytes 100
  23.1 27.1 %copy-start.1 = (f32[768]{0:T(1024)S(1)}, f32[768]{0:T(1024)}, u32[]{:S(2)}) copy-start(f32[768]{0:T(1024)} %param.7) | copy-start | bytes 9220
  25.0 10.6 %collective-permute-start.3 = (f32[192,768]{1,0:T(8,128)}, f32[192,768]{1,0:T(8,128)}, u32[]{:S(2)}, u32[]{:S(2)}) collective-permute-start(f32[192,768]{1,0:T(8,128)} %constant_dynamic-slice_fusion.5), channel_id=1, source_target_pairs={{0,2},{1,7},{2,0},{3,5},{4,6},{5,3},{6,4},{7,1},{8,10},{9,15},{10,... | collective-permute-start | bytes 1769480 | tf_op jit(solution)/shard_map/ppermute | solution.py:72
  39.4 6.2 %collective-permute-start.4 = (f32[96,768]{1,0:T(8,128)}, f32[96,768]{1,0:T(8,128)S(1)}, u32[]{:S(2)}, u32[]{:S(2)}) collective-permute-start(f32[96,768]{1,0:T(8,128)} %constant_dynamic-slice_fusion.4), channel_id=1, source_target_pairs={{0,6},{1,3},{2,4},{3,1},{4,2},{5,7},{6,0},{7,5},{8,14},{9,11},{10,... | collective-permute-start | bytes 884744 | tf_op jit(solution)/shard_map/ppermute | solution.py:72
  46.6 49.5 %collective-permute-start.5 = (f32[48,768]{1,0:T(8,128)S(1)}, f32[48,768]{1,0:T(8,128)S(1)}, u32[]{:S(2)}, u32[]{:S(2)}) collective-permute-start(f32[48,768]{1,0:T(8,128)S(1)} %constant_dynamic-slice_fusion.3), channel_id=1, source_target_pairs={{0,8},{1,9},{2,10},{3,11},{4,12},{5,13},{6,14},{7,15},{8,0},{9,1},... | collective-permute-start | bytes 442376 | tf_op jit(solution)/shard_map/ppermute | solution.py:72
  105.3 3.0 %collective-permute-start.10 = (f32[384,768]{1,0:T(8,128)S(1)}, f32[384,768]{1,0:T(8,128)S(1)}, u32[]{:S(2)}, u32[]{:S(2)}) collective-permute-start(f32[384,768]{1,0:T(8,128)S(1)} %dynamic-slice_bitcast_fusion), channel_id=1, source_target_pairs={{0,1},{1,0},{2,3},{3,2},{4,5},{5,4},{6,7},{7,6},{8,9},{9,8},{10,11... | collective-permute-start | bytes 3538952 | tf_op jit(solution)/shard_map/ppermute | solution.py:72
  108.5 10.0 %collective-permute-start.11 = (f32[192,768]{1,0:T(8,128)S(1)}, f32[192,768]{1,0:T(8,128)S(1)}, u32[]{:S(2)}, u32[]{:S(2)}) collective-permute-start(f32[192,768]{1,0:T(8,128)S(1)} %constant_dynamic-slice_fusion.2), channel_id=1, source_target_pairs={{0,2},{1,7},{2,0},{3,5},{4,6},{5,3},{6,4},{7,1},{8,10},{9,15},{10,... | collective-permute-start | bytes 1769480 | tf_op jit(solution)/shard_map/ppermute | solution.py:72
  111.1 8.0 %collective-permute-start.6 = (f32[48,768]{1,0:T(8,128)S(1)}, f32[48,768]{1,0:T(8,128)S(1)}, u32[]{:S(2)}, u32[]{:S(2)}) collective-permute-start(f32[48,768]{1,0:T(8,128)S(1)} %add_divide_fusion.1), channel_id=1, source_target_pairs={{0,8},{1,9},{2,10},{3,11},{4,12},{5,13},{6,14},{7,15},{8,0},{9,1},... | collective-permute-start | bytes 442376 | tf_op jit(solution)/shard_map/ppermute | solution.py:81
  118.7 5.9 %collective-permute-start.12 = (f32[96,768]{1,0:T(8,128)S(1)}, f32[96,768]{1,0:T(8,128)S(1)}, u32[]{:S(2)}, u32[]{:S(2)}) collective-permute-start(f32[96,768]{1,0:T(8,128)S(1)} %constant_dynamic-slice_fusion.1), channel_id=1, source_target_pairs={{0,6},{1,3},{2,4},{3,1},{4,2},{5,7},{6,0},{7,5},{8,14},{9,11},{10,... | collective-permute-start | bytes 884744 | tf_op jit(solution)/shard_map/ppermute | solution.py:72
  119.2 8.6 %collective-permute-start.7 = (f32[96,768]{1,0:T(8,128)S(1)}, f32[96,768]{1,0:T(8,128)S(1)}, u32[]{:S(2)}, u32[]{:S(2)}) collective-permute-start(f32[96,768]{1,0:T(8,128)S(1)} %constant_dynamic-update-slice_fusion.22), channel_id=1, source_target_pairs={{0,6},{1,3},{2,4},{3,1},{4,2},{5,7},{6,0},{7,5},{8,14},{9,11},{10,... | collective-permute-start | bytes 884744 | tf_op jit(solution)/shard_map/ppermute | solution.py:81
  124.7 5.7 %collective-permute-start.13 = (f32[48,768]{1,0:T(8,128)S(1)}, f32[48,768]{1,0:T(8,128)S(1)}, u32[]{:S(2)}, u32[]{:S(2)}) collective-permute-start(f32[48,768]{1,0:T(8,128)S(1)} %constant_dynamic-slice_fusion), channel_id=1, source_target_pairs={{0,8},{1,9},{2,10},{3,11},{4,12},{5,13},{6,14},{7,15},{8,0},{9,1},... | collective-permute-start | bytes 442376 | tf_op jit(solution)/shard_map/ppermute | solution.py:72
  127.8 10.0 %collective-permute-start.8 = (f32[192,768]{1,0:T(8,128)S(1)}, f32[192,768]{1,0:T(8,128)S(1)}, u32[]{:S(2)}, u32[]{:S(2)}) collective-permute-start(f32[192,768]{1,0:T(8,128)S(1)} %constant_dynamic-update-slice_fusion.20), channel_id=1, source_target_pairs={{0,2},{1,7},{2,0},{3,5},{4,6},{5,3},{6,4},{7,1},{8,10},{9,15},{10,... | collective-permute-start | bytes 1769480 | tf_op jit(solution)/shard_map/ppermute | solution.py:81
  130.5 5.6 %collective-permute-start.14 = (f32[48,768]{1,0:T(8,128)S(1)}, f32[48,768]{1,0:T(8,128)S(1)}, u32[]{:S(2)}, u32[]{:S(2)}) collective-permute-start(f32[48,768]{1,0:T(8,128)S(1)} %get-tuple-element.12), channel_id=1, source_target_pairs={{0,8},{1,9},{2,10},{3,11},{4,12},{5,13},{6,14},{7,15},{8,0},{9,1},... | collective-permute-start | bytes 442376 | tf_op jit(solution)/shard_map/ppermute | solution.py:81
  130.8 14.2 %collective-permute-start.18 = (f32[48,768]{1,0:T(8,128)S(1)}, f32[48,768]{1,0:T(8,128)S(1)}, u32[]{:S(2)}, u32[]{:S(2)}) collective-permute-start(f32[48,768]{1,0:T(8,128)S(1)} %get-tuple-element.12), channel_id=1, source_target_pairs={{0,16},{16,32},{32,48},{48,64},{64,80},{80,96},{96,112},{112,0},{1... | collective-permute-start | bytes 442376 | tf_op jit(solution)/shard_map/ppermute | solution.py:14
  136.1 9.0 %collective-permute-start.15 = (f32[96,768]{1,0:T(8,128)S(1)}, f32[96,768]{1,0:T(8,128)S(1)}, u32[]{:S(2)}, u32[]{:S(2)}) collective-permute-start(f32[96,768]{1,0:T(8,128)S(1)} %constant_dynamic-update-slice_fusion.14), channel_id=1, source_target_pairs={{0,6},{1,3},{2,4},{3,1},{4,2},{5,7},{6,0},{7,5},{8,14},{9,11},{10,... | collective-permute-start | bytes 884744 | tf_op jit(solution)/shard_map/ppermute | solution.py:81
  137.9 27.1 %collective-permute-start.9 = (f32[384,768]{1,0:T(8,128)S(1)}, f32[384,768]{1,0:T(8,128)S(1)}, u32[]{:S(2)}, u32[]{:S(2)}) collective-permute-start(f32[384,768]{1,0:T(8,128)S(1)} %constant_dynamic-update-slice_fusion.18), channel_id=1, source_target_pairs={{0,1},{1,0},{2,3},{3,2},{4,5},{5,4},{6,7},{7,6},{8,9},{9,8},{10,11... | collective-permute-start | bytes 3538952 | tf_op jit(solution)/shard_map/ppermute | solution.py:81
  145.0 7.0 %collective-permute-start.19 = (f32[48,768]{1,0:T(8,128)S(1)}, f32[48,768]{1,0:T(8,128)S(1)}, u32[]{:S(2)}, u32[]{:S(2)}) collective-permute-start(f32[48,768]{1,0:T(8,128)S(1)} %collective-permute-done.18), channel_id=1, source_target_pairs={{0,8},{1,9},{2,10},{3,11},{4,12},{5,13},{6,14},{7,15},{8,0},{9,1},... | collective-permute-start | bytes 442376 | tf_op jit(solution)/shard_map/ppermute | solution.py:81
  145.2 16.1 %collective-permute-start.16 = (f32[192,768]{1,0:T(8,128)S(1)}, f32[192,768]{1,0:T(8,128)S(1)}, u32[]{:S(2)}, u32[]{:S(2)}) collective-permute-start(f32[192,768]{1,0:T(8,128)S(1)} %constant_dynamic-update-slice_fusion.12), channel_id=1, source_target_pairs={{0,2},{1,7},{2,0},{3,5},{4,6},{5,3},{6,4},{7,1},{8,10},{9,15},{10,... | collective-permute-start | bytes 1769480 | tf_op jit(solution)/shard_map/ppermute | solution.py:81
  152.0 9.0 %collective-permute-start.20 = (f32[96,768]{1,0:T(8,128)S(1)}, f32[96,768]{1,0:T(8,128)S(1)}, u32[]{:S(2)}, u32[]{:S(2)}) collective-permute-start(f32[96,768]{1,0:T(8,128)S(1)} %constant_dynamic-update-slice_fusion.6), channel_id=1, source_target_pairs={{0,6},{1,3},{2,4},{3,1},{4,2},{5,7},{6,0},{7,5},{8,14},{9,11},{10,... | collective-permute-start | bytes 884744 | tf_op jit(solution)/shard_map/ppermute | solution.py:81
  161.0 10.0 %collective-permute-start.21 = (f32[192,768]{1,0:T(8,128)S(1)}, f32[192,768]{1,0:T(8,128)S(1)}, u32[]{:S(2)}, u32[]{:S(2)}) collective-permute-start(f32[192,768]{1,0:T(8,128)S(1)} %constant_dynamic-update-slice_fusion.4), channel_id=1, source_target_pairs={{0,2},{1,7},{2,0},{3,5},{4,6},{5,3},{6,4},{7,1},{8,10},{9,15},{10,... | collective-permute-start | bytes 1769480 | tf_op jit(solution)/shard_map/ppermute | solution.py:81
  161.3 14.6 %collective-permute-start.17 = (f32[384,768]{1,0:T(8,128)S(1)}, f32[384,768]{1,0:T(8,128)S(1)}, u32[]{:S(2)}, u32[]{:S(2)}) collective-permute-start(f32[384,768]{1,0:T(8,128)S(1)} %constant_dynamic-update-slice_fusion.10), channel_id=1, source_target_pairs={{0,1},{1,0},{2,3},{3,2},{4,5},{5,4},{6,7},{7,6},{8,9},{9,8},{10,11... | collective-permute-start | bytes 3538952 | tf_op jit(solution)/shard_map/ppermute | solution.py:81
  171.1 9.0 %collective-permute-start.22 = (f32[384,768]{1,0:T(8,128)S(1)}, f32[384,768]{1,0:T(8,128)S(1)}, u32[]{:S(2)}, u32[]{:S(2)}) collective-permute-start(f32[384,768]{1,0:T(8,128)S(1)} %constant_dynamic-update-slice_fusion.2), channel_id=1, source_target_pairs={{0,1},{1,0},{2,3},{3,2},{4,5},{5,4},{6,7},{7,6},{8,9},{9,8},{10,11... | collective-permute-start | bytes 3538952 | tf_op jit(solution)/shard_map/ppermute | solution.py:81
